TPU v7x, 256 devices: a whole 4x4x8 slice. The times are simulated.
256 devices in a mesh: section: 4 (over x_hi, core), seq: 64 (over y, x_lo, z).
Axes of the slice: x: 4 (x_hi: 2, x_lo: 2; x = x_hi * 2 + x_lo), y: 4, z: 8, core: 2. Of those that a mesh axis runs over, the one named last changes fastest.
Arguments:
- activations: bfloat16 [4, 16384, 1024], P('section', 'seq'), may hold values from -54 to 54
- cotangent: bfloat16 [4, 16384, 1024], P('section', 'seq'), may hold values from -6 to 6
- input_weights: bfloat16 [4, 1024, 3072], P('section'), may hold values from -3 to 3
- output_weights: bfloat16 [4, 1024, 1024], P('section'), may hold values from -0.1875 to 0.1875
- key_blocks: int32 [128, 4], P('seq'), may hold values from 0 to 127, as said below
- block_counts: int32 [128], P('seq'), may hold values from 1 to 4, as said below
Outputs:
- forward_out: bfloat16 [4, 16384, 1024], P('section', 'seq')
- backward_out: bfloat16 [4, 16384, 1024], P('section', 'seq')
Inputs may be any that keep to these rules, and one draw needn't show every extreme that they name: `key_blocks`: row b: slot 0 is b; slots 1 to block_counts[b] - 1 hold distinct blocks other than b, at most 2 blocks from b; later slots repeat b. `block_counts`: some block has 4 live slots and some has 1.
All inputs are finite; a program needn't handle non-finite values.
Results may differ from a plain program's by a relative error of at most 0.0036.
Values may be sent and summed in bfloat16 or wider, within the bound.
No kernel may reach another device: no remote copies, remote signals or barrier semaphores. Data moves between devices by JAX's collectives and lax.ppermute only.
A program may use at most 128 MiB of HBM per device.

v0:
```python
import jax
import jax.numpy as jnp
from jax import lax
from jax.sharding import PartitionSpec as P

HEAD_DIM = 128
BLOCK = 128
REACH = 2


EPSILON = 1e-05


def shifted(value, axis, steps):
    count = lax.axis_size(axis)
    pairs = [(source, (source + steps) % count) for source in range(count)]
    return lax.ppermute(value, axis, pairs)


def with_halo(cells, sides, width):
    for axis, dim in sides:
        count = lax.axis_size(axis)
        ends = count - 1
        head = lax.slice_in_dim(cells, 0, width, axis=dim)
        tail = lax.slice_in_dim(cells, cells.shape[dim] - width, cells.shape[dim], axis=dim)
        cells = jnp.concatenate(
            [
                lax.ppermute(tail, axis, [(i, (i + 1) % count) for i in range(ends)]),
                cells,
                lax.ppermute(head, axis, [((i + 1) % count, i) for i in range(ends)]),
            ],
            axis=dim,
        )
    return cells


def block_scores(queries, key_rows):
    scaling = queries.shape[-1] ** (-0.5)
    return (
        jnp.einsum("hbqd,hbskd->hbqsk", queries, key_rows, preferred_element_type=jnp.float32)
        * scaling
    )


def live_mask(counts, slot_count):
    return jnp.arange(slot_count)[None, :] < counts[:, None]


def heads_first(rows, block_count, head_count):
    return rows.reshape(block_count, BLOCK, head_count, HEAD_DIM).transpose(2, 0, 1, 3)


def pairs_heads_first(rows, block_count, head_count):
    return rows.reshape(block_count, BLOCK, 2, head_count, HEAD_DIM).transpose(2, 3, 0, 1, 4)


def heads_to_rows(blocks):
    head_count, block_count, row_block, head_size = blocks.shape
    return blocks.transpose(1, 2, 0, 3).reshape(block_count * row_block, head_count * head_size)


def pairs_to_rows(blocks):
    pair_count, head_count, block_count, row_block, head_size = blocks.shape
    return blocks.transpose(2, 3, 0, 1, 4).reshape(
        block_count * row_block, pair_count * head_count * head_size
    )


def per_device(activations, cotangent, input_weights, output_weights, key_blocks, block_counts):
    arrived = shifted(activations[0], "section", 1)
    upstream = shifted(cotangent[0], "section", -1)
    weights_in = input_weights[0]
    weights_out = output_weights[0]
    feature_width = weights_out.shape[0]
    head_count = feature_width // HEAD_DIM
    row_count = arrived.shape[0]
    nblock = row_count // BLOCK
    slot_count = key_blocks.shape[1]
    scaling = HEAD_DIM ** (-0.5)
    span_blocks = nblock + 2 * REACH
    first_block = lax.axis_index("seq") * nblock
    values = arrived.astype(jnp.float32)
    factor = lax.rsqrt(jnp.mean(values * values, axis=-1, keepdims=True) + EPSILON)
    normed = values * factor
    projected = jnp.dot(
        normed.astype(jnp.bfloat16), weights_in, preferred_element_type=jnp.float32
    ).astype(jnp.bfloat16)
    queries = heads_first(projected[:, :feature_width], nblock, head_count)
    key_value = projected[:, feature_width:]
    margin = REACH * BLOCK
    widened = with_halo(key_value, (("seq", 0),), margin)
    window_pairs = pairs_heads_first(widened, span_blocks, head_count)
    window_index = key_blocks - first_block + REACH
    key_rows = window_pairs[0][:, window_index]
    value_rows = window_pairs[1][:, window_index]
    live_slots = live_mask(block_counts, slot_count)[None, :, None, :, None]
    scores = jnp.where(live_slots, block_scores(queries, key_rows), -1e30)
    row_max = jnp.max(scores, axis=(3, 4), keepdims=True)
    raw_weights = jnp.where(live_slots, jnp.exp(scores - row_max), 0.0)
    row_sum = jnp.sum(raw_weights, axis=(3, 4), keepdims=True)
    weights = raw_weights / row_sum
    weights_bf = weights.astype(jnp.bfloat16)
    attended = jnp.einsum(
        "hbqsk,hbskd->hbqd", weights_bf, value_rows, preferred_element_type=jnp.float32
    )
    attended = heads_to_rows(attended.astype(jnp.bfloat16))
    result = (values + jnp.dot(attended, weights_out, preferred_element_type=jnp.float32)).astype(
        jnp.bfloat16
    )
    attended_grad = jnp.einsum(
        "rd,wd->rw", upstream, weights_out, preferred_element_type=jnp.float32
    ).astype(jnp.bfloat16)
    grad_blocks = heads_first(attended_grad, nblock, head_count)
    weight_grad = jnp.einsum(
        "hbqd,hbskd->hbqsk", grad_blocks, value_rows, preferred_element_type=jnp.float32
    )
    weight_mean = jnp.sum(weights * weight_grad, axis=(3, 4), keepdims=True)
    score_grad = (weights * (weight_grad - weight_mean) * scaling).astype(jnp.bfloat16)
    query_grad = heads_to_rows(
        jnp.einsum("hbqsk,hbskd->hbqd", score_grad, key_rows, preferred_element_type=jnp.float32)
    )
    key_grad = jnp.einsum(
        "hbqsk,hbqd->hbskd", score_grad, queries, preferred_element_type=jnp.float32
    )
    value_grad = jnp.einsum(
        "hbqsk,hbqd->hbskd", weights_bf, grad_blocks, preferred_element_type=jnp.float32
    )
    grad_terms = jnp.stack([key_grad, value_grad]).reshape(
        2, head_count, nblock * slot_count, BLOCK, HEAD_DIM
    )
    placement = (window_index.reshape(-1)[:, None] == jnp.arange(span_blocks)[None, :]).astype(
        jnp.float32
    )
    window_sums = jnp.einsum("ne,chnkd->chekd", placement, grad_terms)
    window_rows = pairs_to_rows(window_sums)
    outgoing = jnp.concatenate([window_rows[:margin], window_rows[margin + row_count :]], axis=0)
    incoming = with_halo(outgoing.astype(jnp.bfloat16), (("seq", 0),), margin).astype(
        outgoing.dtype
    )
    owned_grads = window_rows[margin : margin + row_count]
    padding = jnp.zeros((row_count - margin, 2 * feature_width), jnp.float32)
    owned_grads = owned_grads + jnp.concatenate([incoming[:margin], padding], axis=0)
    owned_grads = owned_grads + jnp.concatenate([padding, incoming[3 * margin :]], axis=0)
    all_grads = jnp.concatenate([query_grad, owned_grads], axis=-1).astype(jnp.bfloat16)
    normed_grad = jnp.einsum("rc,dc->rd", all_grads, weights_in, preferred_element_type=jnp.float32)
    correction = jnp.mean(normed_grad * normed, axis=-1, keepdims=True)
    input_grad = (
        upstream.astype(jnp.float32) + factor * (normed_grad - normed * correction)
    ).astype(jnp.bfloat16)
    return (result[None], input_grad[None])


def solution(mesh):
    in_specs = (
        P("section", "seq", None),
        P("section", "seq", None),
        P("section", None, None),
        P("section", None, None),
        P("seq", None),
        P("seq"),
    )
    out_specs = (P("section", "seq", None), P("section", "seq", None))
    return jax.shard_map(
        per_device, mesh=mesh, in_specs=in_specs, out_specs=out_specs, check_vma=False
    )
```

profile of v0, /device:TPU:24, one launch (start us, length us, event | category | flops | bytes accessed | tf_op | source)
XLA Modules:
  0.0 140.2 jit_solution(8170194338628198201)
XLA Ops:
  0.7 3.2 %collective-permute-start.3 = (bf16[256,1024]{1,0:T(8,128)(2,1)}, bf16[256,1024]{1,0:T(8,128)(2,1)S(1)}, u32[]{:S(2)}, u32[]{:S(2)}) collective-permute-start(bf16[256,1024]{1,0:T(8,128)(2,1)} %bitcast.143), channel_id=1, source_target_pairs={{0,192},{64,0},{128,64},{192,128},{1,193},{65,1},{129,65},{193,129... | collective-permute-start | bytes 1572872 | tf_op jit(solution)/shard_map/ppermute | solution.py:17
  4.0 9.4 %collective-permute-done = bf16[256,1024]{1,0:T(8,128)(2,1)S(1)} collective-permute-done((bf16[256,1024]{1,0:T(8,128)(2,1)}, bf16[256,1024]{1,0:T(8,128)(2,1)S(1)}, u32[]{:S(2)}, u32[]{:S(2)}) %collective-permute-start) | collective-permute-done | bytes 524320 | tf_op jit(solution)/shard_map/ppermute | solution.py:17
  13.6 4.7 %fusion.8 = bf16[256,3072]{1,0:T(8,128)(2,1)S(1)} fusion(bf16[1,1024,3072]{2,1,0:T(8,128)(2,1)} %param.8, bf16[256,1024]{1,0:T(8,128)(2,1)S(1)} %collective-permute-done, f32[256]{0:T(256)S(1)} %add_rsqrt_fusion), kind=kOutput, calls=%fused_computation.14 | convolution fusion | flops 1612185600 | bytes 8389632 | tf_op jit(solution)/shard_map/dot_general | solution.py:85
  19.7 9.8 %collective-permute-start.2 = (bf16[256,2048]{1,0:T(8,128)(2,1)}, bf16[256,2048]{1,0:T(8,128)(2,1)}, u32[]{:S(2)}, u32[]{:S(2)}) collective-permute-start(bf16[256,2048]{1,0:T(8,128)(2,1)} %slice.57), channel_id=1, source_target_pairs={{1,0},{2,1},{3,2},{4,3},{5,4},{6,5},{7,6},{8,7},{9,8},{10,9},{11,1... | collective-permute-start | bytes 3145736 | tf_op jit(solution)/shard_map/ppermute | solution.py:30
  29.5 1.9 %collective-permute-start.1 = (bf16[256,2048]{1,0:T(8,128)(2,1)}, bf16[256,2048]{1,0:T(8,128)(2,1)}, u32[]{:S(2)}, u32[]{:S(2)}) collective-permute-start(bf16[256,2048]{1,0:T(8,128)(2,1)} %slice.57), channel_id=1, source_target_pairs={{0,1},{1,2},{2,3},{3,4},{4,5},{5,6},{6,7},{7,8},{8,9},{9,10},{10,1... | collective-permute-start | bytes 3145736 | tf_op jit(solution)/shard_map/ppermute | solution.py:28
  34.6 16.9 %collective-permute-done.2 = bf16[256,2048]{1,0:T(8,128)(2,1)} collective-permute-done((bf16[256,2048]{1,0:T(8,128)(2,1)}, bf16[256,2048]{1,0:T(8,128)(2,1)}, u32[]{:S(2)}, u32[]{:S(2)}) %collective-permute-start.2) | collective-permute-done | bytes 1048608 | tf_op jit(solution)/shard_map/ppermute | solution.py:30
  51.5 7.1 %collective-permute-done.1 = bf16[256,2048]{1,0:T(8,128)(2,1)} collective-permute-done((bf16[256,2048]{1,0:T(8,128)(2,1)}, bf16[256,2048]{1,0:T(8,128)(2,1)}, u32[]{:S(2)}, u32[]{:S(2)}) %collective-permute-start.1) | collective-permute-done | bytes 1048608 | tf_op jit(solution)/shard_map/ppermute | solution.py:28
  58.6 2.0 %maximum_bitcast_fusion = bf16[96,8,16,128]{3,1,2,0:T(8,128)(2,1)S(1)} fusion(bf16[256,2048]{1,0:T(8,128)(2,1)} %collective-permute-done.2, bf16[256,2048]{1,0:T(8,128)(2,1)} %slice.57, bf16[256,2048]{1,0:T(8,128)(2,1)} %collective-permute-done.1), kind=kLoop, calls=%fused_computation.17 | loop fusion | flops 9437184 | bytes 6291456
  61.6 2.4 %slice_bitcast_fusion.1 = (bf16[8,6,128,128]{3,0,2,1:T(8,128)(2,1)}, bf16[8,6,128,128]{3,0,2,1:T(8,128)(2,1)}) fusion(bf16[2,8,6,128,128]{4,1,0,3,2:T(8,128)(2,1)S(1)} %bitcast.130), kind=kLoop, calls=%fused_computation.28 | loop fusion | bytes 6291456 | tf_op jit(solution)/shard_map/squeeze | solution.py:94
  64.0 3.6 %gather_fusion = bf16[8,8,128,128]{3,1,2,0:T(8,128)(2,1)} fusion(bf16[8,6,128,128]{3,0,2,1:T(8,128)(2,1)} %get-tuple-element.4, s32[1024]{0:T(1024)S(1)} %pad_clamp_fusion), kind=kCustom, calls=%fused_computation | custom fusion | bytes 4194336 | tf_op jit(solution)/shard_map/gather | solution.py:94
  67.6 3.5 %copy.17 = bf16[8,8,128,128]{3,2,0,1:T(8,128)(2,1)} copy(bf16[8,8,128,128]{3,1,2,0:T(8,128)(2,1)} %gather_fusion) | data formatting | bytes 4194304 | tf_op jit(solution)/shard_map/gather | solution.py:94
  71.1 3.6 %gather_fusion.1 = bf16[8,8,128,128]{3,1,2,0:T(8,128)(2,1)} fusion(bf16[8,6,128,128]{3,0,2,1:T(8,128)(2,1)} %get-tuple-element.5, s32[1024]{0:T(1024)S(1)} %pad_clamp_fusion), kind=kCustom, calls=%fused_computation.1 | custom fusion | bytes 4194336 | tf_op jit(solution)/shard_map/gather | solution.py:95
  74.6 2.3 %copy.18 = bf16[8,8,128,128]{3,2,0,1:T(8,128)(2,1)S(1)} copy(bf16[8,8,128,128]{3,1,2,0:T(8,128)(2,1)} %gather_fusion.1) | data formatting | bytes 4194304 | tf_op jit(solution)/shard_map/gather | solution.py:95
  80.1 1.4 copy.25
  81.5 1.6 %multiply_reduce_fusion = (f32[8,2,128]{2,1,0:T(2,128)S(1)}, f32[8,2,128,4,128]{2,4,3,1,0:T(8,128)S(1)}) fusion(f32[8,2,128]{2,1,0:T(2,128)S(1)} %fusion.16, f32[8,2,128]{2,1,0:T(2,128)S(1)} %get-tuple-element.8, f32[8,2,128,4,128]{2,4,3,1,0:T(8,128)S(1)} %get-tuple-element.9, pred[2,4]{1,0:T(4,128)(4,1)S(1)} %iota_compare_fusion.1, ...), kind=kOutput, calls=%fused_computation.11 | convolution fusion | flops 275773440 | bytes 11034632 | tf_op jit(solution)/shard_map/hbqd,hbskd->hbqsk/dot_general | solution.py:114
  83.1 1.7 %multiply_convert_fusion = bf16[8,2,128,4,128]{2,4,3,1,0:T(8,128)(2,1)S(1)} fusion(f32[8,2,128,4,128]{2,4,3,1,0:T(8,128)S(1)} %get-tuple-element.11, f32[8,2,128]{2,1,0:T(2,128)S(1)} %get-tuple-element.10, f32[8,2,128]{2,1,0:T(2,128)S(1)} %fusion.16, f32[8,2,128]{2,1,0:T(2,128)S(1)} %get-tuple-element.8, f32[8,2,128,4,128]{2,4,3,1,0:T(8,128)S(1)} %get-tuple-element.9, ...), kind=kLoop, calls=%fused_computation.10 | loop fusion | flops 9437184 | bytes 10510344 | tf_op jit(solution)/shard_map/convert_element_type | solution.py:118
  87.0 4.2 %fusion.80 = (bf16[6,128,2,8,128]{4,0,1,3,2:T(8,128)(2,1)S(1)}, f32[6,128,2,8,128]{4,0,1,3,2:T(8,128)}) fusion(s32[8]{0:T(128)S(1)} %eq.15, bf16[1,8,8,128,128]{4,2,3,1,0:T(8,128)(2,1)S(1)} %copy.25, bf16[1,8,8,128,128]{4,2,3,1,0:T(8,128)(2,1)S(1)} %copy.24), kind=kOutput, calls=%fused_computation.89 | convolution fusion | flops 28835888 | bytes 13631520 | tf_op jit(solution)/shard_map/ne,chnkd->chekd/dot_general | solution.py:134
  91.1 2.3 %fusion.79 = (bf16[2,128,2,8,128]{4,0,1,3,2:T(2,128)(2,1)S(1)}, bf16[2,128,2,8,128]{4,0,1,3,2:T(2,128)(2,1)}) fusion(bf16[6,128,2,8,128]{4,0,1,3,2:T(8,128)(2,1)S(1)} %get-tuple-element.12), kind=kLoop, calls=%fused_computation.88 | loop fusion | bytes 4194304 | tf_op jit(solution)/shard_map/slice | solution.py:136
  93.4 1.7 %copy.27 = bf16[2,128,2,8,128]{4,3,2,1,0:T(8,128)(2,1)} copy(bf16[2,128,2,8,128]{4,0,1,3,2:T(2,128)(2,1)S(1)} %get-tuple-element.2) | data formatting | bytes 2097152 | tf_op jit(solution)/shard_map/slice | solution.py:136
  95.1 1.5 %slice.47 = bf16[256,2048]{1,0:T(8,128)(2,1)S(1)} reshape(bf16[2,128,2,8,128]{4,3,2,1,0:T(8,128)(2,1)} %copy.27) | data formatting | bytes 2097152 | tf_op jit(solution)/shard_map/slice | solution.py:136
  96.6 2.9 %copy.28 = bf16[2,128,2,8,128]{4,3,2,1,0:T(8,128)(2,1)} copy(bf16[2,128,2,8,128]{4,0,1,3,2:T(2,128)(2,1)} %get-tuple-element.3) | data formatting | bytes 2097152 | tf_op jit(solution)/shard_map/slice | solution.py:136
  99.5 2.3 %slice.49 = bf16[256,2048]{1,0:T(8,128)(2,1)} reshape(bf16[2,128,2,8,128]{4,3,2,1,0:T(8,128)(2,1)} %copy.28) | data formatting | bytes 2097152 | tf_op jit(solution)/shard_map/slice | solution.py:136
  101.8 2.2 %collective-permute-start.5 = (bf16[256,2048]{1,0:T(8,128)(2,1)}, bf16[256,2048]{1,0:T(8,128)(2,1)}, u32[]{:S(2)}, u32[]{:S(2)}) collective-permute-start(bf16[256,2048]{1,0:T(8,128)(2,1)} %slice.49), channel_id=1, source_target_pairs={{1,0},{2,1},{3,2},{4,3},{5,4},{6,5},{7,6},{8,7},{9,8},{10,9},{11,1... | collective-permute-start | bytes 3145736 | tf_op jit(solution)/shard_map/ppermute | solution.py:30
  104.0 3.9 %collective-permute-start.4 = (bf16[256,2048]{1,0:T(8,128)(2,1)S(1)}, bf16[256,2048]{1,0:T(8,128)(2,1)}, u32[]{:S(2)}, u32[]{:S(2)}) collective-permute-start(bf16[256,2048]{1,0:T(8,128)(2,1)S(1)} %slice.47), channel_id=1, source_target_pairs={{0,1},{1,2},{2,3},{3,4},{4,5},{5,6},{6,7},{7,8},{8,9},{9,10},{10,1... | collective-permute-start | bytes 3145736 | tf_op jit(solution)/shard_map/ppermute | solution.py:28
  107.9 4.4 %fusion.40 = bf16[2,128,8,128]{3,1,0,2:T(8,128)(2,1)S(1)} fusion(bf16[8,2,4,128,128]{4,3,2,1,0:T(8,128)(2,1)} %bitcast.135, f32[8,2,128,4,128]{2,4,3,1,0:T(8,128)} %copy-done.1, f32[8,2,128]{2,1,0:T(2,128)S(1)} %fusion.16, f32[8,2,128]{2,1,0:T(2,128)S(1)} %get-tuple-element.8, pred[2,4]{1,0:T(4,128)(4,1)S(1)} %iota_compare_fusion.1), kind=kOutput, calls=%fused_computation.45 | convolution fusion | flops 274989056 | bytes 6832136 | tf_op jit(solution)/shard_map/hbqsk,hbskd->hbqd/dot_general | solution.py:103
  115.5 4.5 %slice.60 = f32[2,128,2,8,128]{4,0,1,3,2:T(2,128)S(1)} slice(f32[6,128,2,8,128]{4,0,1,3,2:T(8,128)} %get-tuple-element.13), slice={[2:4], [0:128], [0:2], [0:8], [0:128]} | slice | bytes 4194304 | tf_op jit(solution)/shard_map/slice | solution.py:140
  120.0 2.5 %copy.26 = f32[2,128,2,8,128]{4,3,2,1,0:T(8,128)} copy(f32[2,128,2,8,128]{4,0,1,3,2:T(2,128)S(1)} %slice.60) | data formatting | bytes 4194304 | tf_op jit(solution)/shard_map/slice | solution.py:140
  122.6 2.7 %slice.45 = f32[256,2048]{1,0:T(8,128)} reshape(f32[2,128,2,8,128]{4,3,2,1,0:T(8,128)} %copy.26) | data formatting | bytes 4194304 | tf_op jit(solution)/shard_map/slice | solution.py:140
  125.3 2.9 %fusion.44 = bf16[1,256,1024]{2,1,0:T(8,128)(2,1)} fusion(bf16[1,1024,1024]{2,1,0:T(8,128)(2,1)S(1)} %copy-done, bf16[256,1024]{1,0:T(8,128)(2,1)} %copy-done.9, bf16[32,8,8,128]{3,2,1,0:T(8,128)(2,1)} %bitcast.141), kind=kOutput, calls=%fused_computation.47 | convolution fusion | flops 537657344 | bytes 3670016 | tf_op jit(solution)/shard_map/dot_general | solution.py:107
  128.2 3.9 %collective-permute-done.4 = bf16[256,2048]{1,0:T(8,128)(2,1)} collective-permute-done((bf16[256,2048]{1,0:T(8,128)(2,1)S(1)}, bf16[256,2048]{1,0:T(8,128)(2,1)}, u32[]{:S(2)}, u32[]{:S(2)}) %collective-permute-start.4) | collective-permute-done | bytes 1048608 | tf_op jit(solution)/shard_map/ppermute | solution.py:28
  132.0 2.1 %fusion.18 = bf16[256,2048]{1,0:T(8,128)(2,1)S(1)} fusion(f32[256,2048]{1,0:T(8,128)S(1)} %copy-done.6, bf16[256,2048]{1,0:T(8,128)(2,1)} %collective-permute-done.5, bf16[256,2048]{1,0:T(8,128)(2,1)S(1)} %slice.47, bf16[256,2048]{1,0:T(8,128)(2,1)S(1)} %copy-done.7, bf16[256,2048]{1,0:T(8,128)(2,1)} %collective-permute-done.4), kind=kLoop, calls=%fused_computation.22 | loop fusion | flops 9961472 | bytes 7340032 | tf_op jit(solution)/shard_map/convert.1
  134.1 4.9 %fusion.47 = (f32[256]{0:T(256)S(1)}, f32[256,1024]{1,0:T(8,128)S(1)}) fusion(bf16[256,1024]{1,0:T(8,128)(2,1)S(1)} %copy-done.10, f32[256]{0:T(256)S(1)} %add_rsqrt_fusion, bf16[1,1024,3072]{2,1,0:T(8,128)(2,1)} %param.8, bf16[256,2048]{1,0:T(8,128)(2,1)S(1)} %fusion.18, bf16[256,1024]{1,0:T(8,128)(2,1)S(1)} %bitcast.140), kind=kOutput, calls=%fused_computation.48 | convolution fusion | flops 1614806784 | bytes 9439232 | tf_op jit(solution)/shard_map/rc,dc->rd/dot_general | solution.py:145
  (61 shorter events, 15.5 us)
Async XLA Ops:
  0.6 31.9 %copy-start = (bf16[1,1024,1024]{2,1,0:T(8,128)(2,1)S(1)}, bf16[1,1024,1024]{2,1,0:T(8,128)(2,1)}, u32[]{:S(2)}) copy-start(bf16[1,1024,1024]{2,1,0:T(8,128)(2,1)} %param.9) | copy-start | bytes 6291460
  0.6 12.7 %collective-permute-start = (bf16[256,1024]{1,0:T(8,128)(2,1)}, bf16[256,1024]{1,0:T(8,128)(2,1)S(1)}, u32[]{:S(2)}, u32[]{:S(2)}) collective-permute-start(bf16[256,1024]{1,0:T(8,128)(2,1)} %bitcast.142), channel_id=1, source_target_pairs={{0,64},{64,128},{128,192},{192,0},{1,65},{65,129},{129,193},{193,1... | collective-permute-start | bytes 1572872 | tf_op jit(solution)/shard_map/ppermute | solution.py:17
  0.7 31.0 %collective-permute-start.3 = (bf16[256,1024]{1,0:T(8,128)(2,1)}, bf16[256,1024]{1,0:T(8,128)(2,1)S(1)}, u32[]{:S(2)}, u32[]{:S(2)}) collective-permute-start(bf16[256,1024]{1,0:T(8,128)(2,1)} %bitcast.143), channel_id=1, source_target_pairs={{0,192},{64,0},{128,64},{192,128},{1,193},{65,1},{129,65},{193,129... | collective-permute-start | bytes 1572872 | tf_op jit(solution)/shard_map/ppermute | solution.py:17
  13.3 4.9 %copy-start.9 = (bf16[256,1024]{1,0:T(8,128)(2,1)}, bf16[256,1024]{1,0:T(8,128)(2,1)S(1)}, u32[]{:S(2)}) copy-start(bf16[256,1024]{1,0:T(8,128)(2,1)S(1)} %collective-permute-done) | copy-start | bytes 1572868
  13.5 17.9 %copy-start.15 = (s32[2,4]{1,0:T(2,128)S(1)}, s32[2,4]{1,0:T(2,128)}, u32[]{:S(2)}) copy-start(s32[2,4]{1,0:T(2,128)} %param.10) | copy-start | bytes 100
  13.5 18.1 %copy-start.16 = (s32[2]{0:T(128)S(1)}, s32[2]{0:T(128)}, u32[]{:S(2)}) copy-start(s32[2]{0:T(128)} %param.11) | copy-start | bytes 28
  18.3 1.5 %copy-start.11 = (bf16[256,3072]{1,0:T(8,128)(2,1)}, bf16[256,3072]{1,0:T(8,128)(2,1)S(1)}, u32[]{:S(2)}) copy-start(bf16[256,3072]{1,0:T(8,128)(2,1)S(1)} %fusion.8) | copy-start | bytes 4718596
  19.7 31.7 %collective-permute-start.2 = (bf16[256,2048]{1,0:T(8,128)(2,1)}, bf16[256,2048]{1,0:T(8,128)(2,1)}, u32[]{:S(2)}, u32[]{:S(2)}) collective-permute-start(bf16[256,2048]{1,0:T(8,128)(2,1)} %slice.57), channel_id=1, source_target_pairs={{1,0},{2,1},{3,2},{4,3},{5,4},{6,5},{7,6},{8,7},{9,8},{10,9},{11,1... | collective-permute-start | bytes 3145736 | tf_op jit(solution)/shard_map/ppermute | solution.py:30
  29.5 29.1 %collective-permute-start.1 = (bf16[256,2048]{1,0:T(8,128)(2,1)}, bf16[256,2048]{1,0:T(8,128)(2,1)}, u32[]{:S(2)}, u32[]{:S(2)}) collective-permute-start(bf16[256,2048]{1,0:T(8,128)(2,1)} %slice.57), channel_id=1, source_target_pairs={{0,1},{1,2},{2,3},{3,4},{4,5},{5,6},{6,7},{7,8},{8,9},{9,10},{10,1... | collective-permute-start | bytes 3145736 | tf_op jit(solution)/shard_map/ppermute | solution.py:28
  31.7 0.8 copy-start.13
  74.6 2.3 %copy-start.2 = (bf16[8,8,128,128]{3,2,0,1:T(8,128)(2,1)S(1)}, bf16[8,8,128,128]{3,2,0,1:T(8,128)(2,1)}, u32[]{:S(2)}) copy-start(bf16[8,8,128,128]{3,2,0,1:T(8,128)(2,1)} %copy.17) | copy-start | bytes 6291460
  76.9 4.6 %copy-start.8 = (bf16[8,8,128,128]{3,2,0,1:T(8,128)(2,1)}, bf16[8,8,128,128]{3,2,0,1:T(8,128)(2,1)S(1)}, u32[]{:S(2)}) copy-start(bf16[8,8,128,128]{3,2,0,1:T(8,128)(2,1)S(1)} %copy.18) | copy-start | bytes 6291460
  77.7 5.4 %copy-start.1 = (f32[8,2,128,4,128]{2,4,3,1,0:T(8,128)}, f32[8,2,128,4,128]{2,4,3,1,0:T(8,128)S(1)}, u32[]{:S(2)}) copy-start(f32[8,2,128,4,128]{2,4,3,1,0:T(8,128)S(1)} %get-tuple-element.9) | copy-start | bytes 12582916
  84.9 2.1 %copy-start.4 = (bf16[8,2,128,4,128]{2,4,3,1,0:T(8,128)(2,1)}, bf16[8,2,128,4,128]{2,4,3,1,0:T(8,128)(2,1)S(1)}, u32[]{:S(2)}) copy-start(bf16[8,2,128,4,128]{2,4,3,1,0:T(8,128)(2,1)S(1)} %multiply_convert_fusion) | copy-start | bytes 6291460
  101.8 11.7 %copy-start.3 = (bf16[8,8,128,128]{3,2,0,1:T(8,128)(2,1)S(1)}, bf16[8,8,128,128]{3,2,0,1:T(8,128)(2,1)}, u32[]{:S(2)}) copy-start(bf16[8,8,128,128]{3,2,0,1:T(8,128)(2,1)} %copy.17) | copy-start | bytes 6291460
  101.8 11.7 %copy-start.5 = (bf16[8,2,128,4,128]{2,4,3,1,0:T(8,128)(2,1)S(1)}, bf16[8,2,128,4,128]{2,4,3,1,0:T(8,128)(2,1)}, u32[]{:S(2)}) copy-start(bf16[8,2,128,4,128]{2,4,3,1,0:T(8,128)(2,1)} %copy-done.4) | copy-start | bytes 6291460
  101.8 26.3 %collective-permute-start.5 = (bf16[256,2048]{1,0:T(8,128)(2,1)}, bf16[256,2048]{1,0:T(8,128)(2,1)}, u32[]{:S(2)}, u32[]{:S(2)}) collective-permute-start(bf16[256,2048]{1,0:T(8,128)(2,1)} %slice.49), channel_id=1, source_target_pairs={{1,0},{2,1},{3,2},{4,3},{5,4},{6,5},{7,6},{8,7},{9,8},{10,9},{11,1... | collective-permute-start | bytes 3145736 | tf_op jit(solution)/shard_map/ppermute | solution.py:30
  104.0 28.0 %collective-permute-start.4 = (bf16[256,2048]{1,0:T(8,128)(2,1)S(1)}, bf16[256,2048]{1,0:T(8,128)(2,1)}, u32[]{:S(2)}, u32[]{:S(2)}) collective-permute-start(bf16[256,2048]{1,0:T(8,128)(2,1)S(1)} %slice.47), channel_id=1, source_target_pairs={{0,1},{1,2},{2,3},{3,4},{4,5},{5,6},{6,7},{7,8},{8,9},{9,10},{10,1... | collective-permute-start | bytes 3145736 | tf_op jit(solution)/shard_map/ppermute | solution.py:28
  125.3 6.7 %copy-start.6 = (f32[256,2048]{1,0:T(8,128)S(1)}, f32[256,2048]{1,0:T(8,128)}, u32[]{:S(2)}) copy-start(f32[256,2048]{1,0:T(8,128)} %slice.45) | copy-start | bytes 6291460
  125.3 6.7 %copy-start.7 = (bf16[256,2048]{1,0:T(8,128)(2,1)S(1)}, bf16[256,2048]{1,0:T(8,128)(2,1)}, u32[]{:S(2)}) copy-start(bf16[256,2048]{1,0:T(8,128)(2,1)} %slice.49) | copy-start | bytes 3145732
  128.1 6.0 %copy-start.10 = (bf16[256,1024]{1,0:T(8,128)(2,1)S(1)}, bf16[256,1024]{1,0:T(8,128)(2,1)}, u32[]{:S(2)}) copy-start(bf16[256,1024]{1,0:T(8,128)(2,1)} %copy-done.9) | copy-start | bytes 1572868
  128.1 6.0 %copy-start.12 = (bf16[32,8,8,128]{3,1,2,0:T(8,128)(2,1)S(1)}, bf16[32,8,8,128]{3,1,2,0:T(8,128)(2,1)}, u32[]{:S(2)}) copy-start(bf16[32,8,8,128]{3,1,2,0:T(8,128)(2,1)} %copy.66) | copy-start | bytes 1572868
  134.1 5.0 %copy-start.14 = (bf16[256,1024]{1,0:T(8,128)(2,1)S(1)}, bf16[256,1024]{1,0:T(8,128)(2,1)}, u32[]{:S(2)}) copy-start(bf16[256,1024]{1,0:T(8,128)(2,1)} %copy-done.13) | copy-start | bytes 1572868
where the time goes:
time: 141 us; the launch traced here: 140 us
  local copies, waits for them, and re-layouts  45.6 us (32%)
  waiting for transfers between devices  37.3 us (26%)
  matrix products  27 us (19%)
  starting transfers between devices  21.1 us (15%)
  other arithmetic  8.26 us (6%)
    ppermute x2, waiting for transfers between devices, with_halo(): lax.ppermute(head, axis, [((i + 1) % count, i) for i in range(ends)])  16.9 us
    ppermute x2, starting transfers between devices, with_halo(): lax.ppermute(head, axis, [((i + 1) % count, i) for i in range(ends)])  11.9 us
    ppermute x2, waiting for transfers between devices, with_halo(): lax.ppermute(tail, axis, [(i, (i + 1) % count) for i in range(ends)])  11 us
    slice x3, local copies, waits for them, and re-layouts, per_device(): owned_grads = window_rows[margin:margin + row_count]  9.74 us
    ppermute x2, waiting for transfers between devices, shifted(): return lax.ppermute(value, axis, pairs)  9.37 us
    gather x2, local copies, waits for them, and re-layouts, per_device(): key_rows = window_pairs[0][:, window_index]  7.01 us
    ppermute x2, starting transfers between devices, with_halo(): lax.ppermute(tail, axis, [(i, (i + 1) % count) for i in range(ends)])  5.84 us
    gather x2, local copies, waits for them, and re-layouts, per_device(): value_rows = window_pairs[1][:, window_index]  5.81 us
  transfers between devices with their start and end apart: 6, of which 4 were waited for; matrix products, arithmetic and copies ran while one was open for 20% of the time, Pallas kernels for 0%

commit v1 on v0

v1 whole, which is shorter than its diff:
```python
import functools

import jax
import jax.numpy as jnp
from jax import lax
from jax.experimental import pallas as pl
from jax.experimental.pallas import tpu as pltpu
from jax.sharding import PartitionSpec as P

HEAD_DIM = 128
BLOCK = 128
REACH = 2


EPSILON = 1e-05

NT = (((1,), (1,)), ((), ()))
TN = (((0,), (0,)), ((), ()))


def shifted(value, axis, steps):
    count = lax.axis_size(axis)
    pairs = [(source, (source + steps) % count) for source in range(count)]
    return lax.ppermute(value, axis, pairs)


def from_left(value, axis):
    count = lax.axis_size(axis)
    return lax.ppermute(value, axis, [(i, i + 1) for i in range(count - 1)])


def from_right(value, axis):
    count = lax.axis_size(axis)
    return lax.ppermute(value, axis, [(i + 1, i) for i in range(count - 1)])


def normalize(rows):
    values = rows.astype(jnp.float32)
    factor = lax.rsqrt(jnp.mean(values * values, axis=-1, keepdims=True) + EPSILON)
    return values, factor, values * factor


def attention_kernel(
    q_ref, ko_ref, vo_ref, kh_ref, vh_ref, do_ref, live_ref,
    out_ref, dq_ref, dk_ref, dv_ref, dkh_ref, dvh_ref,
):
    rows = q_ref.shape[0]
    margin = kh_ref.shape[0] // 2
    scaling = HEAD_DIM ** (-0.5)
    queries = q_ref[...]
    keys = jnp.concatenate([kh_ref[:margin], ko_ref[...], kh_ref[margin:]], axis=0)
    values = jnp.concatenate([vh_ref[:margin], vo_ref[...], vh_ref[margin:]], axis=0)
    grad_out = do_ref[...]
    live = live_ref[...] > 0
    scores = lax.dot_general(queries, keys, NT, preferred_element_type=jnp.float32) * scaling
    scores = jnp.where(live, scores, -1e30)
    row_max = jnp.max(scores, axis=1, keepdims=True)
    raw = jnp.where(live, jnp.exp(scores - row_max), 0.0)
    weights = raw / jnp.sum(raw, axis=1, keepdims=True)
    weights_bf = weights.astype(jnp.bfloat16)
    out_ref[...] = jnp.dot(weights_bf, values, preferred_element_type=jnp.float32).astype(
        out_ref.dtype
    )
    weight_grad = lax.dot_general(grad_out, values, NT, preferred_element_type=jnp.float32)
    weight_mean = jnp.sum(weights * weight_grad, axis=1, keepdims=True)
    score_grad = (weights * (weight_grad - weight_mean) * scaling).astype(jnp.bfloat16)
    dq_ref[...] = jnp.dot(score_grad, keys, preferred_element_type=jnp.float32).astype(dq_ref.dtype)
    key_grad = lax.dot_general(score_grad, queries, TN, preferred_element_type=jnp.float32)
    value_grad = lax.dot_general(weights_bf, grad_out, TN, preferred_element_type=jnp.float32)
    dtype = dk_ref.dtype
    dk_ref[...] = key_grad[margin : margin + rows].astype(dtype)
    dv_ref[...] = value_grad[margin : margin + rows].astype(dtype)
    dkh_ref[:margin] = key_grad[:margin].astype(dtype)
    dkh_ref[margin:] = key_grad[margin + rows :].astype(dtype)
    dvh_ref[:margin] = value_grad[:margin].astype(dtype)
    dvh_ref[margin:] = value_grad[margin + rows :].astype(dtype)


def attention(projected, halo_kv, attended_grad, live):
    rows, width = attended_grad.shape
    heads = width // HEAD_DIM
    halo_rows = halo_kv.shape[0]
    window = live.shape[1]
    own = lambda offset: pl.BlockSpec((rows, HEAD_DIM), lambda h: (0, offset + h))
    side = lambda offset: pl.BlockSpec((halo_rows, HEAD_DIM), lambda h: (0, offset + h))
    flops = heads * 5 * 2 * rows * window * HEAD_DIM
    moved = 2 * (2 * projected.size + 2 * halo_kv.size + 2 * attended_grad.size) + 4 * live.size
    own_shape = jax.ShapeDtypeStruct((rows, width), jnp.bfloat16)
    side_shape = jax.ShapeDtypeStruct((halo_rows, width), jnp.bfloat16)
    return pl.pallas_call(
        attention_kernel,
        grid=(heads,),
        in_specs=[
            own(0),
            own(heads),
            own(2 * heads),
            side(0),
            side(heads),
            own(0),
            pl.BlockSpec((rows, window), lambda h: (0, 0)),
        ],
        out_specs=[own(0), own(0), own(0), own(0), side(0), side(0)],
        out_shape=[own_shape, own_shape, own_shape, own_shape, side_shape, side_shape],
        compiler_params=pltpu.CompilerParams(dimension_semantics=("arbitrary",)),
        cost_estimate=pl.CostEstimate(
            flops=flops, transcendentals=heads * rows * window, bytes_accessed=moved
        ),
    )(projected, projected, projected, halo_kv, halo_kv, attended_grad, live)


def per_device(activations, cotangent, input_weights, output_weights, key_blocks, block_counts):
    arrived = shifted(activations[0], "section", 1)
    upstream = shifted(cotangent[0], "section", -1)
    weights_in = input_weights[0]
    weights_out = output_weights[0]
    width = weights_out.shape[0]
    rows = arrived.shape[0]
    nblock = rows // BLOCK
    slot_count = key_blocks.shape[1]
    margin = REACH * BLOCK
    assert margin <= rows
    span_blocks = nblock + 2 * REACH
    first_block = lax.axis_index("seq") * nblock

    halo_rows = jnp.concatenate(
        [from_left(arrived[rows - margin :], "seq"), from_right(arrived[:margin], "seq")], axis=0
    )
    values, factor, normed = normalize(arrived)
    projected = jnp.dot(
        normed.astype(jnp.bfloat16), weights_in, preferred_element_type=jnp.float32
    ).astype(jnp.bfloat16)
    attended_grad = jnp.einsum(
        "rd,wd->rw", upstream, weights_out, preferred_element_type=jnp.float32
    ).astype(jnp.bfloat16)
    _, _, halo_normed = normalize(halo_rows)
    weights_kv = weights_in[:, width:]
    halo_kv = jnp.dot(
        halo_normed.astype(jnp.bfloat16), weights_kv, preferred_element_type=jnp.float32
    ).astype(jnp.bfloat16)

    window_index = key_blocks - first_block + REACH
    live_slots = jnp.arange(slot_count)[None, :] < block_counts[:, None]
    live_blocks = jnp.any(
        live_slots[:, :, None] & (window_index[:, :, None] == jnp.arange(span_blocks)[None, None, :]),
        axis=1,
    )
    live = jnp.repeat(jnp.repeat(live_blocks, BLOCK, axis=0), BLOCK, axis=1).astype(jnp.float32)

    attended, query_grad, key_grad, value_grad, halo_key_grad, halo_value_grad = attention(
        projected, halo_kv, attended_grad, live
    )
    result = (values + jnp.dot(attended, weights_out, preferred_element_type=jnp.float32)).astype(
        jnp.bfloat16
    )

    halo_grads = jnp.concatenate([halo_key_grad, halo_value_grad], axis=1)
    halo_normed_grad = jnp.einsum(
        "rc,dc->rd", halo_grads, weights_kv, preferred_element_type=jnp.float32
    ).astype(jnp.bfloat16)
    head_part = from_left(halo_normed_grad[margin:], "seq")
    tail_part = from_right(halo_normed_grad[:margin], "seq")
    own_grads = jnp.concatenate([query_grad, key_grad, value_grad], axis=1)
    normed_grad = jnp.einsum("rc,dc->rd", own_grads, weights_in, preferred_element_type=jnp.float32)
    normed_grad = normed_grad + jnp.pad(head_part.astype(jnp.float32), ((0, rows - margin), (0, 0)))
    normed_grad = normed_grad + jnp.pad(tail_part.astype(jnp.float32), ((rows - margin, 0), (0, 0)))
    correction = jnp.mean(normed_grad * normed, axis=-1, keepdims=True)
    input_grad = (
        upstream.astype(jnp.float32) + factor * (normed_grad - normed * correction)
    ).astype(jnp.bfloat16)
    return (result[None], input_grad[None])


def solution(mesh):
    in_specs = (
        P("section", "seq", None),
        P("section", "seq", None),
        P("section", None, None),
        P("section", None, None),
        P("seq", None),
        P("seq"),
    )
    out_specs = (P("section", "seq", None), P("section", "seq", None))
    return jax.shard_map(
        per_device, mesh=mesh, in_specs=in_specs, out_specs=out_specs, check_vma=False
    )
```

time: 141 us -> 87.1 us (0.62)
  local copies, waits for them, and re-layouts: 45.6 us -> 1.53 us
  waiting for transfers between devices: 37.3 us -> 20.4 us
  Pallas kernels: 0 us -> 14 us
  matrix products: 27 us -> 21.4 us
  other arithmetic: 8.26 us -> 4.28 us
  starting transfers between devices: 21.1 us -> 24.2 us
    slice x9 -> x1, local copies, waits for them, and re-layouts: 21.6 us -> 0.07 us  [per_device(): head_part = from_left(halo_normed_grad[margin:], 'seq')]
    pallas_call x0 -> x1, Pallas kernels: none -> 14 us  [attention(): pl.pallas_call(attention_kernel, grid=(heads,), in_specs=[own(0), own(hea...]
    ppermute x4, waiting for transfers between devices: 27.9 us -> 13.9 us  [the longest x2 12.7 us: from_left(): return lax.ppermute(value, axis, [(i, i + 1) for i in range(count - 1)])]
    gather x4 -> x0, local copies, waits for them, and re-layouts: 12.8 us -> none  [the longest x2 7.01 us: per_device(): key_rows = window_pairs[0][:, window_index]]
    dot_general x8 -> x3, matrix products: 18.7 us -> 11.2 us  [the longest x1 5.33 us: per_device(): jnp.einsum('rc,dc->rd', halo_grads, weights_kv, preferred_element_type=jn...]
    unnamed x39 -> x20, local copies, waits for them, and re-layouts: 4.43 us -> 0.13 us
    ppermute x4, starting transfers between devices: 17.8 us -> 20.8 us  [the longest x2 16.9 us: from_right(): return lax.ppermute(value, axis, [(i + 1, i) for i in range(count - 1)])]
    ppermute x2, waiting for transfers between devices: 9.37 us -> 6.44 us  [shifted(): return lax.ppermute(value, axis, pairs)]
  transfers between devices with their start and end apart: 6 -> 6, of which waited for: 4 -> 4; matrix products, arithmetic and copies ran while one was open for 20% -> 15% of each run, Pallas kernels for 0% -> 0%
where the time goes in v1:
time: 87.1 us; the launch traced here: 86.6 us
  starting transfers between devices  24.2 us (28%)
  matrix products  21.4 us (25%)
  waiting for transfers between devices  20.4 us (23%)
  Pallas kernels  14 us (16%)
  other arithmetic  4.28 us (5%)
  local copies, waits for them, and re-layouts  1.53 us (2%)
    ppermute x2, starting transfers between devices, from_right(): return lax.ppermute(value, axis, [(i + 1, i) for i in range(count - 1)])  16.9 us
    pallas_call x1, Pallas kernels, attention(): pl.pallas_call(attention_kernel, grid=(heads,), in_specs=[own(0), own(hea...  14 us
    ppermute x2, waiting for transfers between devices, from_left(): return lax.ppermute(value, axis, [(i, i + 1) for i in range(count - 1)])  12.7 us
    ppermute x2, waiting for transfers between devices, shifted(): return lax.ppermute(value, axis, pairs)  6.44 us
    dot_general x1, matrix products, per_device(): jnp.dot(normed.astype(jnp.bfloat16), weights_in, preferred_element_type=j...  5.98 us
    dot_general x1, matrix products, per_device(): jnp.einsum('rc,dc->rd', halo_grads, weights_kv, preferred_element_type=jn...  5.33 us
    ppermute x2, starting transfers between devices, from_left(): return lax.ppermute(value, axis, [(i, i + 1) for i in range(count - 1)])  3.97 us
    dot_general x1, matrix products, per_device(): jnp.dot(halo_normed.astype(jnp.bfloat16), weights_kv, preferred_element_t...  3.76 us
  transfers between devices with their start and end apart: 6, of which 4 were waited for; matrix products, arithmetic and copies ran while one was open for 15% of the time, Pallas kernels for 0%

profile of v1, /device:TPU:24, one launch (start us, length us, event | category | flops | bytes accessed | tf_op | source)
XLA Modules:
  0.0 86.6 jit_solution(16729713554525813358)
XLA Ops:
  0.6 0.0 copy-start
  0.6 0.1 collective-permute-start
  0.7 3.2 %collective-permute-start.3 = (bf16[256,1024]{1,0:T(8,128)(2,1)}, bf16[256,1024]{1,0:T(8,128)(2,1)}, u32[]{:S(2)}, u32[]{:S(2)}) collective-permute-start(bf16[256,1024]{1,0:T(8,128)(2,1)} %bitcast.45), channel_id=1, source_target_pairs={{0,192},{64,0},{128,64},{192,128},{1,193},{65,1},{129,65},{193,129... | collective-permute-start | bytes 1572872 | tf_op jit(solution)/shard_map/ppermute | solution.py:24
  4.0 0.7 subtract_add_fusion
  4.7 0.7 iota_compare_fusion.1
  5.4 0.1 fusion.53
  5.5 0.1 copy.9
  5.6 0.1 broadcast_bitcast_fusion
  5.7 0.1 broadcast_in_dim.9
  5.7 1.2 %copy.10.live_ref = f32[256,768]{1,0:T(8,128)} copy(f32[256,768]{0,1:T(8,128)S(1)} %bitcast.36) | data formatting | bytes 1572864 | tf_op jit(solution)/shard_map/convert_element_type | solution.py:147
  6.9 6.4 %collective-permute-done = bf16[256,1024]{1,0:T(8,128)(2,1)S(1)} collective-permute-done((bf16[256,1024]{1,0:T(8,128)(2,1)}, bf16[256,1024]{1,0:T(8,128)(2,1)S(1)}, u32[]{:S(2)}, u32[]{:S(2)}) %collective-permute-start) | collective-permute-done | bytes 524320 | tf_op jit(solution)/shard_map/ppermute | solution.py:24
  13.3 9.8 %collective-permute-start.2 = (bf16[256,1024]{1,0:T(8,128)(2,1)S(1)}, bf16[256,1024]{1,0:T(8,128)(2,1)S(1)}, u32[]{:S(2)}, u32[]{:S(2)}) collective-permute-start(bf16[256,1024]{1,0:T(8,128)(2,1)S(1)} %collective-permute-done), channel_id=1, source_target_pairs={{1,0},{2,1},{3,2},{4,3},{5,4},{6,5},{7,6},{8,7},{9,8},{10,9},{11,1... | collective-permute-start | bytes 1572872 | tf_op jit(solution)/shard_map/ppermute | solution.py:34
  23.1 1.9 %collective-permute-start.1 = (bf16[256,1024]{1,0:T(8,128)(2,1)S(1)}, bf16[256,1024]{1,0:T(8,128)(2,1)S(1)}, u32[]{:S(2)}, u32[]{:S(2)}) collective-permute-start(bf16[256,1024]{1,0:T(8,128)(2,1)S(1)} %collective-permute-done), channel_id=1, source_target_pairs={{0,1},{1,2},{2,3},{3,4},{4,5},{5,6},{6,7},{7,8},{8,9},{9,10},{10,1... | collective-permute-start | bytes 1572872 | tf_op jit(solution)/shard_map/ppermute | solution.py:29
  25.0 0.2 fusion.46
  25.2 0.0 slice-start
  25.3 2.7 %fusion.35.do_ref = bf16[256,1024]{1,0:T(8,128)(2,1)} fusion(bf16[256,1024]{1,0:T(8,128)(2,1)} %collective-permute-done.3, bf16[1,1024,1024]{2,1,0:T(8,128)(2,1)S(1)} %copy-done), kind=kOutput, calls=%fused_computation.31 | convolution fusion | flops 537133056 | bytes 3145728 | tf_op jit(solution)/shard_map/rd,wd->rw/dot_general | solution.py:132
  28.0 6.0 %convolution_convert_fusion.q_ref.ko_ref.vo_ref = bf16[256,3072]{1,0:T(8,128)(2,1)} fusion(bf16[256,1024]{1,0:T(8,128)(2,1)S(1)} %collective-permute-done, f32[256]{0:T(256)S(1)} %add_rsqrt_fusion.1, bf16[1,1024,3072]{2,1,0:T(8,128)(2,1)} %param.8), kind=kOutput, calls=%fused_computation | convolution fusion | flops 1612185600 | bytes 8389632 | tf_op jit(solution)/shard_map/dot_general | solution.py:129
  34.0 6.7 %collective-permute-done.1 = bf16[256,1024]{1,0:T(8,128)(2,1)S(1)} collective-permute-done((bf16[256,1024]{1,0:T(8,128)(2,1)S(1)}, bf16[256,1024]{1,0:T(8,128)(2,1)S(1)}, u32[]{:S(2)}, u32[]{:S(2)}) %collective-permute-start.1) | collective-permute-done | bytes 524320 | tf_op jit(solution)/shard_map/ppermute | solution.py:29
  40.6 0.3 fusion.7
  41.0 3.8 %fusion.4.kh_ref.vh_ref = bf16[512,2048]{1,0:T(8,128)(2,1)} fusion(bf16[1024,3072]{1,0:T(8,128)(2,1)S(1)} %bitcast.41, f32[512]{0:T(512)S(1)} %add_rsqrt_fusion, bf16[256,1024]{1,0:T(8,128)(2,1)S(1)} %collective-permute-done.2, bf16[256,1024]{1,0:T(8,128)(2,1)S(1)} %collective-permute-done.1), kind=kOutput, calls=%fused_computation.5 | convolution fusion | flops 2151677952 | bytes 7342080 | tf_op jit(solution)/shard_map/dot_general | solution.py:137
  44.7 14.0 %shard_map.77 = (bf16[256,1024]{1,0:T(8,128)(2,1)}, bf16[256,1024]{1,0:T(8,128)(2,1)}, bf16[256,1024]{1,0:T(8,128)(2,1)}, bf16[256,1024]{1,0:T(8,128)(2,1)}, bf1...) custom-call(bf16[256,3072]{1,0:T(8,128)(2,1)} %convolution_convert_fusion.q_ref.ko_ref.vo_ref, ...), custom_call_target="tpu_custom_call" | custom-call | flops 2013265920 | bytes 9175040 | tf_op jit(solution)/shard_map/pallas_call | solution.py:90
  58.7 0.0 slice-start.2
  58.7 5.3 %fusion.22 = bf16[512,1024]{1,0:T(8,128)(2,1)S(1)} fusion(bf16[1024,3072]{1,0:T(8,128)(2,1)} %bitcast.38, bf16[512,1024]{1,0:T(8,128)(2,1)} %get-tuple-element.13, bf16[512,1024]{1,0:T(8,128)(2,1)} %get-tuple-element.12), kind=kOutput, calls=%fused_computation.26 | convolution fusion | flops 2152202240 | bytes 7340032 | tf_op jit(solution)/shard_map/rc,dc->rd/dot_general | solution.py:157
  64.1 0.0 copy-start.4
  64.1 0.1 fusion.59
  64.2 2.1 %collective-permute-start.4 = (bf16[256,1024]{1,0:T(8,128)(2,1)S(1)}, bf16[256,1024]{1,0:T(8,128)(2,1)S(1)}, u32[]{:S(2)}, u32[]{:S(2)}) collective-permute-start(bf16[256,1024]{1,0:T(8,128)(2,1)S(1)} %get-tuple-element.14), channel_id=1, source_target_pairs={{0,1},{1,2},{2,3},{3,4},{4,5},{5,6},{6,7},{7,8},{8,9},{9,10},{10,1... | collective-permute-start | bytes 1572872 | tf_op jit(solution)/shard_map/ppermute | solution.py:29
  66.2 7.1 %collective-permute-start.5 = (bf16[256,1024]{1,0:T(8,128)(2,1)S(1)}, bf16[256,1024]{1,0:T(8,128)(2,1)S(1)}, u32[]{:S(2)}, u32[]{:S(2)}) collective-permute-start(bf16[256,1024]{1,0:T(8,128)(2,1)S(1)} %get-tuple-element.15), channel_id=1, source_target_pairs={{1,0},{2,1},{3,2},{4,3},{5,4},{6,5},{7,6},{8,7},{9,8},{10,9},{11,1... | collective-permute-start | bytes 1572872 | tf_op jit(solution)/shard_map/ppermute | solution.py:34
  73.4 1.5 %fusion.38 = bf16[1,256,1024]{2,1,0:T(8,128)(2,1)} fusion(bf16[256,1024]{1,0:T(8,128)(2,1)S(1)} %copy-done.4, bf16[1,1024,1024]{2,1,0:T(8,128)(2,1)S(1)} %copy-done, bf16[256,1024]{1,0:T(8,128)(2,1)S(1)} %collective-permute-done), kind=kOutput, calls=%fused_computation.32 | convolution fusion | flops 537657344 | bytes 3670016 | tf_op jit(solution)/shard_map/dot_general | solution.py:152
  74.9 6.1 %collective-permute-done.4 = bf16[256,1024]{1,0:T(8,128)(2,1)S(1)} collective-permute-done((bf16[256,1024]{1,0:T(8,128)(2,1)S(1)}, bf16[256,1024]{1,0:T(8,128)(2,1)S(1)}, u32[]{:S(2)}, u32[]{:S(2)}) %collective-permute-start.4) | collective-permute-done | bytes 524320 | tf_op jit(solution)/shard_map/ppermute | solution.py:29
  81.0 1.2 %collective-permute-done.5 = bf16[256,1024]{1,0:T(8,128)(2,1)S(1)} collective-permute-done((bf16[256,1024]{1,0:T(8,128)(2,1)S(1)}, bf16[256,1024]{1,0:T(8,128)(2,1)S(1)}, u32[]{:S(2)}, u32[]{:S(2)}) %collective-permute-start.5) | collective-permute-done | bytes 524320 | tf_op jit(solution)/shard_map/ppermute | solution.py:34
  82.2 2.1 %fusion.41 = (f32[256]{0:T(256)S(1)}, f32[256,1024]{1,0:T(8,128)S(1)}) fusion(bf16[256,1024]{1,0:T(8,128)(2,1)S(1)} %collective-permute-done, f32[256]{0:T(256)S(1)} %add_rsqrt_fusion.1, bf16[256,1024]{1,0:T(8,128)(2,1)S(1)} %collective-permute-done.5, bf16[256,1024]{1,0:T(8,128)(2,1)S(1)} %collective-permute-done.4, ...), kind=kOutput, calls=%fused_computation.33 | convolution fusion | flops 1617428224 | bytes 10487808 | tf_op jit(solution)/shard_map/rc,dc->rd/dot_general | solution.py:163
  84.3 2.3 %fusion.49 = bf16[1,256,1024]{2,1,0:T(8,128)(2,1)} fusion(bf16[256,1024]{1,0:T(8,128)(2,1)S(1)} %collective-permute-done, bf16[256,1024]{1,0:T(8,128)(2,1)} %collective-permute-done.3, f32[256]{0:T(256)S(1)} %broadcast_multiply_fusion, f32[256]{0:T(256)S(1)} %add_rsqrt_fusion.1, bf16[256,1024]{1,0:T(8,128)(2,1)S(1)} %collective-permute-done.5, ...), kind=kLoop, calls=%fused_computation.42 | loop fusion | flops 3145728 | bytes 3672064 | tf_op jit(solution)/shard_map/broadcast_in_dim | solution.py:170
  (23 shorter events, 0.1 us)
Async XLA Ops:
  0.6 24.6 %copy-start = (bf16[1,1024,1024]{2,1,0:T(8,128)(2,1)S(1)}, bf16[1,1024,1024]{2,1,0:T(8,128)(2,1)}, u32[]{:S(2)}) copy-start(bf16[1,1024,1024]{2,1,0:T(8,128)(2,1)} %param.9) | copy-start | bytes 6291460
  0.6 12.7 %collective-permute-start = (bf16[256,1024]{1,0:T(8,128)(2,1)}, bf16[256,1024]{1,0:T(8,128)(2,1)S(1)}, u32[]{:S(2)}, u32[]{:S(2)}) collective-permute-start(bf16[256,1024]{1,0:T(8,128)(2,1)} %bitcast.44), channel_id=1, source_target_pairs={{0,64},{64,128},{128,192},{192,0},{1,65},{65,129},{129,193},{193,1... | collective-permute-start | bytes 1572872 | tf_op jit(solution)/shard_map/ppermute | solution.py:24
  0.7 24.5 %collective-permute-start.3 = (bf16[256,1024]{1,0:T(8,128)(2,1)}, bf16[256,1024]{1,0:T(8,128)(2,1)}, u32[]{:S(2)}, u32[]{:S(2)}) collective-permute-start(bf16[256,1024]{1,0:T(8,128)(2,1)} %bitcast.45), channel_id=1, source_target_pairs={{0,192},{64,0},{128,64},{192,128},{1,193},{65,1},{129,65},{193,129... | collective-permute-start | bytes 1572872 | tf_op jit(solution)/shard_map/ppermute | solution.py:24
  13.3 20.6 %collective-permute-start.2 = (bf16[256,1024]{1,0:T(8,128)(2,1)S(1)}, bf16[256,1024]{1,0:T(8,128)(2,1)S(1)}, u32[]{:S(2)}, u32[]{:S(2)}) collective-permute-start(bf16[256,1024]{1,0:T(8,128)(2,1)S(1)} %collective-permute-done), channel_id=1, source_target_pairs={{1,0},{2,1},{3,2},{4,3},{5,4},{6,5},{7,6},{8,7},{9,8},{10,9},{11,1... | collective-permute-start | bytes 1572872 | tf_op jit(solution)/shard_map/ppermute | solution.py:34
  23.1 17.5 %collective-permute-start.1 = (bf16[256,1024]{1,0:T(8,128)(2,1)S(1)}, bf16[256,1024]{1,0:T(8,128)(2,1)S(1)}, u32[]{:S(2)}, u32[]{:S(2)}) collective-permute-start(bf16[256,1024]{1,0:T(8,128)(2,1)S(1)} %collective-permute-done), channel_id=1, source_target_pairs={{0,1},{1,2},{2,3},{3,4},{4,5},{5,6},{6,7},{7,8},{8,9},{9,10},{10,1... | collective-permute-start | bytes 1572872 | tf_op jit(solution)/shard_map/ppermute | solution.py:29
  25.2 15.7 %slice-start = ((s8[6291456]{0:T(1024)(128)(4,1)}), s8[4194304]{0:T(1024)(128)(4,1)S(1)}, s32[]{:S(2)}) async-start(s8[6291456]{0:T(1024)(128)(4,1)} %bitcast.39), calls=%async_computation | async-start | bytes 8388608
  28.0 13.0 %slice-start.1 = ((s8[6291456]{0:T(1024)(128)(4,1)}), s8[2097152]{0:T(1024)(128)(4,1)S(1)}, s32[]{:S(2)}) async-start(s8[6291456]{0:T(1024)(128)(4,1)} %bitcast.39), calls=%async_computation.1 | async-start | bytes 4194304
  58.7 23.5 %slice-start.2 = ((s8[6291456]{0:T(1024)(128)(4,1)}), s8[4194304]{0:T(1024)(128)(4,1)S(1)}, s32[]{:S(2)}) async-start(s8[6291456]{0:T(1024)(128)(4,1)} %bitcast.42), calls=%async_computation.2 | async-start | bytes 8388608
  58.7 23.5 %slice-start.3 = ((s8[6291456]{0:T(1024)(128)(4,1)}), s8[2097152]{0:T(1024)(128)(4,1)S(1)}, s32[]{:S(2)}) async-start(s8[6291456]{0:T(1024)(128)(4,1)} %bitcast.42), calls=%async_computation.3 | async-start | bytes 4194304
  64.1 9.3 %copy-start.4 = (bf16[256,1024]{1,0:T(8,128)(2,1)S(1)}, bf16[256,1024]{1,0:T(8,128)(2,1)}, u32[]{:S(2)}) copy-start(bf16[256,1024]{1,0:T(8,128)(2,1)} %get-tuple-element.8) | copy-start | bytes 1572868
  64.2 18.0 %copy-start.1 = (bf16[256,1024]{1,0:T(8,128)(2,1)S(1)}, bf16[256,1024]{1,0:T(8,128)(2,1)}, u32[]{:S(2)}) copy-start(bf16[256,1024]{1,0:T(8,128)(2,1)} %get-tuple-element.9) | copy-start | bytes 1572868
  64.2 18.0 %copy-start.2 = (bf16[256,1024]{1,0:T(8,128)(2,1)S(1)}, bf16[256,1024]{1,0:T(8,128)(2,1)}, u32[]{:S(2)}) copy-start(bf16[256,1024]{1,0:T(8,128)(2,1)} %get-tuple-element.10) | copy-start | bytes 1572868
  64.2 18.0 %copy-start.3 = (bf16[256,1024]{1,0:T(8,128)(2,1)S(1)}, bf16[256,1024]{1,0:T(8,128)(2,1)}, u32[]{:S(2)}) copy-start(bf16[256,1024]{1,0:T(8,128)(2,1)} %get-tuple-element.11) | copy-start | bytes 1572868
  64.2 16.8 %collective-permute-start.4 = (bf16[256,1024]{1,0:T(8,128)(2,1)S(1)}, bf16[256,1024]{1,0:T(8,128)(2,1)S(1)}, u32[]{:S(2)}, u32[]{:S(2)}) collective-permute-start(bf16[256,1024]{1,0:T(8,128)(2,1)S(1)} %get-tuple-element.14), channel_id=1, source_target_pairs={{0,1},{1,2},{2,3},{3,4},{4,5},{5,6},{6,7},{7,8},{8,9},{9,10},{10,1... | collective-permute-start | bytes 1572872 | tf_op jit(solution)/shard_map/ppermute | solution.py:29
  66.2 15.9 %collective-permute-start.5 = (bf16[256,1024]{1,0:T(8,128)(2,1)S(1)}, bf16[256,1024]{1,0:T(8,128)(2,1)S(1)}, u32[]{:S(2)}, u32[]{:S(2)}) collective-permute-start(bf16[256,1024]{1,0:T(8,128)(2,1)S(1)} %get-tuple-element.15), channel_id=1, source_target_pairs={{1,0},{2,1},{3,2},{4,3},{5,4},{6,5},{7,6},{8,7},{9,8},{10,9},{11,1... | collective-permute-start | bytes 1572872 | tf_op jit(solution)/shard_map/ppermute | solution.py:34

commit v2 on v1

--- a/solution.py
+++ b/solution.py
@@ -51,12 +51,11 @@
     keys = jnp.concatenate([kh_ref[:margin], ko_ref[...], kh_ref[margin:]], axis=0)
     values = jnp.concatenate([vh_ref[:margin], vo_ref[...], vh_ref[margin:]], axis=0)
     grad_out = do_ref[...]
-    live = live_ref[...] > 0
     scores = lax.dot_general(queries, keys, NT, preferred_element_type=jnp.float32) * scaling
-    scores = jnp.where(live, scores, -1e30)
+    scores = scores + live_ref[...]
     row_max = jnp.max(scores, axis=1, keepdims=True)
-    raw = jnp.where(live, jnp.exp(scores - row_max), 0.0)
-    weights = raw / jnp.sum(raw, axis=1, keepdims=True)
+    raw = jnp.exp(scores - row_max)
+    weights = raw * (1.0 / jnp.sum(raw, axis=1, keepdims=True))
     weights_bf = weights.astype(jnp.bfloat16)
     out_ref[...] = jnp.dot(weights_bf, values, preferred_element_type=jnp.float32).astype(
         out_ref.dtype
@@ -144,7 +143,7 @@
         live_slots[:, :, None] & (window_index[:, :, None] == jnp.arange(span_blocks)[None, None, :]),
         axis=1,
     )
-    live = jnp.repeat(jnp.repeat(live_blocks, BLOCK, axis=0), BLOCK, axis=1).astype(jnp.float32)
+    live = jnp.where(jnp.repeat(jnp.repeat(live_blocks, BLOCK, axis=0), BLOCK, axis=1), 0.0, -1e30)
 
     attended, query_grad, key_grad, value_grad, halo_key_grad, halo_value_grad = attention(
         projected, halo_kv, attended_grad, live
@@ -160,7 +159,9 @@
     head_part = from_left(halo_normed_grad[margin:], "seq")
     tail_part = from_right(halo_normed_grad[:margin], "seq")
     own_grads = jnp.concatenate([query_grad, key_grad, value_grad], axis=1)
-    normed_grad = jnp.einsum("rc,dc->rd", own_grads, weights_in, preferred_element_type=jnp.float32)
+    normed_grad = lax.optimization_barrier(
+        jnp.einsum("rc,dc->rd", own_grads, weights_in, preferred_element_type=jnp.float32)
+    )
     normed_grad = normed_grad + jnp.pad(head_part.astype(jnp.float32), ((0, rows - margin), (0, 0)))
     normed_grad = normed_grad + jnp.pad(tail_part.astype(jnp.float32), ((rows - margin, 0), (0, 0)))
     correction = jnp.mean(normed_grad * normed, axis=-1, keepdims=True)

time: 87.1 us -> 84.6 us (0.971)
  waiting for transfers between devices: 20.4 us -> 15.7 us
  matrix products: 21.4 us -> 23.8 us
    ppermute x2, waiting for transfers between devices: 12.7 us -> 8.07 us  [from_left(): return lax.ppermute(value, axis, [(i, i + 1) for i in range(count - 1)])]
    dot_general x1, matrix products: 2.11 us -> 4.66 us  [per_device(): jnp.einsum('rc,dc->rd', own_grads, weights_in, preferred_element_type=jnp...]
    convert_element_type x2 -> x0, local copies, waits for them, and re-layouts: 1.27 us -> none  [per_device(): jnp.repeat(jnp.repeat(live_blocks, BLOCK, axis=0), BLOCK, axis=1)]
    select_n x0 -> x2, local copies, waits for them, and re-layouts: none -> 1.26 us  [per_device(): jnp.where(jnp.repeat(jnp.repeat(live_blocks, BLOCK, axis=0), BLOCK, axis=...]
  transfers between devices with their start and end apart: 6 -> 6, of which waited for: 4 -> 4; matrix products, arithmetic and copies ran while one was open for 15% -> 21% of each run, Pallas kernels for 0% -> 0%
where the time goes in v2:
time: 84.6 us; the launch traced here: 84.1 us
  starting transfers between devices  24.2 us (29%)
  matrix products  23.8 us (28%)
  waiting for transfers between devices  15.7 us (19%)
  Pallas kernels  13.4 us (16%)
  other arithmetic  4.65 us (5%)
  local copies, waits for them, and re-layouts  1.51 us (2%)
    ppermute x2, starting transfers between devices, from_right(): return lax.ppermute(value, axis, [(i + 1, i) for i in range(count - 1)])  16.9 us
    pallas_call x1, Pallas kernels, attention(): pl.pallas_call(attention_kernel, grid=(heads,), in_specs=[own(0), own(hea...  13.4 us
    ppermute x2, waiting for transfers between devices, from_left(): return lax.ppermute(value, axis, [(i, i + 1) for i in range(count - 1)])  8.07 us
    ppermute x2, waiting for transfers between devices, shifted(): return lax.ppermute(value, axis, pairs)  6.45 us
    dot_general x1, matrix products, per_device(): jnp.dot(normed.astype(jnp.bfloat16), weights_in, preferred_element_type=j...  5.97 us
    dot_general x1, matrix products, per_device(): jnp.einsum('rc,dc->rd', halo_grads, weights_kv, preferred_element_type=jn...  5.2 us
    dot_general x1, matrix products, per_device(): jnp.einsum('rc,dc->rd', own_grads, weights_in, preferred_element_type=jnp...  4.66 us
    ppermute x2, starting transfers between devices, from_left(): return lax.ppermute(value, axis, [(i, i + 1) for i in range(count - 1)])  3.97 us
  transfers between devices with their start and end apart: 6, of which 4 were waited for; matrix products, arithmetic and copies ran while one was open for 21% of the time, Pallas kernels for 0%

profile of v2, /device:TPU:24, one launch (start us, length us, event | category | flops | bytes accessed | tf_op | source)
XLA Modules:
  0.0 84.1 jit_solution(6776263698578711698)
XLA Ops:
  0.6 0.0 copy-start
  0.6 0.1 collective-permute-start
  0.7 3.2 %collective-permute-start.3 = (bf16[256,1024]{1,0:T(8,128)(2,1)}, bf16[256,1024]{1,0:T(8,128)(2,1)}, u32[]{:S(2)}, u32[]{:S(2)}) collective-permute-start(bf16[256,1024]{1,0:T(8,128)(2,1)} %bitcast.41), channel_id=1, source_target_pairs={{0,192},{64,0},{128,64},{192,128},{1,193},{65,1},{129,65},{193,129... | collective-permute-start | bytes 1572872 | tf_op jit(solution)/shard_map/ppermute | solution.py:24
  4.0 0.7 iota_compare_fusion.1
  4.7 0.7 subtract_add_fusion
  5.4 0.1 fusion.53
  5.5 0.1 copy.9
  5.6 0.1 broadcast_bitcast_fusion
  5.7 0.1 broadcast_in_dim.31
  5.7 1.2 %copy.10.live_ref = f32[256,768]{1,0:T(8,128)} copy(f32[256,768]{0,1:T(8,128)S(1)} %bitcast.34) | data formatting | bytes 1572864 | tf_op jit(solution)/shard_map/jit(_where)/select_n | solution.py:146
  6.9 6.5 %collective-permute-done = bf16[256,1024]{1,0:T(8,128)(2,1)S(1)} collective-permute-done((bf16[256,1024]{1,0:T(8,128)(2,1)}, bf16[256,1024]{1,0:T(8,128)(2,1)S(1)}, u32[]{:S(2)}, u32[]{:S(2)}) %collective-permute-start) | collective-permute-done | bytes 524320 | tf_op jit(solution)/shard_map/ppermute | solution.py:24
  13.3 9.8 %collective-permute-start.2 = (bf16[256,1024]{1,0:T(8,128)(2,1)S(1)}, bf16[256,1024]{1,0:T(8,128)(2,1)S(1)}, u32[]{:S(2)}, u32[]{:S(2)}) collective-permute-start(bf16[256,1024]{1,0:T(8,128)(2,1)S(1)} %collective-permute-done), channel_id=1, source_target_pairs={{1,0},{2,1},{3,2},{4,3},{5,4},{6,5},{7,6},{8,7},{9,8},{10,9},{11,1... | collective-permute-start | bytes 1572872 | tf_op jit(solution)/shard_map/ppermute | solution.py:34
  23.1 1.9 %collective-permute-start.1 = (bf16[256,1024]{1,0:T(8,128)(2,1)S(1)}, bf16[256,1024]{1,0:T(8,128)(2,1)S(1)}, u32[]{:S(2)}, u32[]{:S(2)}) collective-permute-start(bf16[256,1024]{1,0:T(8,128)(2,1)S(1)} %collective-permute-done), channel_id=1, source_target_pairs={{0,1},{1,2},{2,3},{3,4},{4,5},{5,6},{6,7},{7,8},{8,9},{9,10},{10,1... | collective-permute-start | bytes 1572872 | tf_op jit(solution)/shard_map/ppermute | solution.py:29
  25.0 0.2 fusion.46
  25.2 0.0 slice-start
  25.3 2.7 %fusion.35.do_ref = bf16[256,1024]{1,0:T(8,128)(2,1)} fusion(bf16[256,1024]{1,0:T(8,128)(2,1)} %collective-permute-done.3, bf16[1,1024,1024]{2,1,0:T(8,128)(2,1)S(1)} %copy-done), kind=kOutput, calls=%fused_computation.31 | convolution fusion | flops 537133056 | bytes 3145728 | tf_op jit(solution)/shard_map/rd,wd->rw/dot_general | solution.py:131
  28.0 6.0 %convolution_convert_fusion.q_ref.ko_ref.vo_ref = bf16[256,3072]{1,0:T(8,128)(2,1)} fusion(bf16[256,1024]{1,0:T(8,128)(2,1)S(1)} %collective-permute-done, f32[256]{0:T(256)S(1)} %add_rsqrt_fusion.1, bf16[1,1024,3072]{2,1,0:T(8,128)(2,1)} %param.8), kind=kOutput, calls=%fused_computation | convolution fusion | flops 1612185600 | bytes 8389632 | tf_op jit(solution)/shard_map/dot_general | solution.py:128
  34.0 6.7 %collective-permute-done.1 = bf16[256,1024]{1,0:T(8,128)(2,1)S(1)} collective-permute-done((bf16[256,1024]{1,0:T(8,128)(2,1)S(1)}, bf16[256,1024]{1,0:T(8,128)(2,1)S(1)}, u32[]{:S(2)}, u32[]{:S(2)}) %collective-permute-start.1) | collective-permute-done | bytes 524320 | tf_op jit(solution)/shard_map/ppermute | solution.py:29
  40.6 0.3 fusion.7
  41.0 3.8 %fusion.4.kh_ref.vh_ref = bf16[512,2048]{1,0:T(8,128)(2,1)} fusion(bf16[1024,3072]{1,0:T(8,128)(2,1)S(1)} %bitcast.39, f32[512]{0:T(512)S(1)} %add_rsqrt_fusion, bf16[256,1024]{1,0:T(8,128)(2,1)S(1)} %collective-permute-done.2, bf16[256,1024]{1,0:T(8,128)(2,1)S(1)} %collective-permute-done.1), kind=kOutput, calls=%fused_computation.5 | convolution fusion | flops 2151677952 | bytes 7342080 | tf_op jit(solution)/shard_map/dot_general | solution.py:136
  44.7 13.4 %shard_map.77 = (bf16[256,1024]{1,0:T(8,128)(2,1)}, bf16[256,1024]{1,0:T(8,128)(2,1)}, bf16[256,1024]{1,0:T(8,128)(2,1)}, bf16[256,1024]{1,0:T(8,128)(2,1)}, bf1...) custom-call(bf16[256,3072]{1,0:T(8,128)(2,1)} %convolution_convert_fusion.q_ref.ko_ref.vo_ref, ...), custom_call_target="tpu_custom_call" | custom-call | flops 2013265920 | bytes 9175040 | tf_op jit(solution)/shard_map/pallas_call | solution.py:89
  58.1 5.2 %fusion.22 = bf16[512,1024]{1,0:T(8,128)(2,1)S(1)} fusion(bf16[1024,3072]{1,0:T(8,128)(2,1)} %bitcast.36, bf16[512,1024]{1,0:T(8,128)(2,1)} %get-tuple-element.13, bf16[512,1024]{1,0:T(8,128)(2,1)} %get-tuple-element.12), kind=kOutput, calls=%fused_computation.26 | convolution fusion | flops 2152202240 | bytes 7340032 | tf_op jit(solution)/shard_map/rc,dc->rd/dot_general | solution.py:156
  63.4 0.1 fusion.59
  63.5 2.1 %collective-permute-start.4 = (bf16[256,1024]{1,0:T(8,128)(2,1)S(1)}, bf16[256,1024]{1,0:T(8,128)(2,1)S(1)}, u32[]{:S(2)}, u32[]{:S(2)}) collective-permute-start(bf16[256,1024]{1,0:T(8,128)(2,1)S(1)} %get-tuple-element.14), channel_id=1, source_target_pairs={{0,1},{1,2},{2,3},{3,4},{4,5},{5,6},{6,7},{7,8},{8,9},{9,10},{10,1... | collective-permute-start | bytes 1572872 | tf_op jit(solution)/shard_map/ppermute | solution.py:29
  65.5 7.1 %collective-permute-start.5 = (bf16[256,1024]{1,0:T(8,128)(2,1)S(1)}, bf16[256,1024]{1,0:T(8,128)(2,1)S(1)}, u32[]{:S(2)}, u32[]{:S(2)}) collective-permute-start(bf16[256,1024]{1,0:T(8,128)(2,1)S(1)} %get-tuple-element.15), channel_id=1, source_target_pairs={{1,0},{2,1},{3,2},{4,3},{5,4},{6,5},{7,6},{8,7},{9,8},{10,9},{11,1... | collective-permute-start | bytes 1572872 | tf_op jit(solution)/shard_map/ppermute | solution.py:34
  72.7 0.0 copy-start.1
  72.7 4.7 %fusion.16 = f32[256,1024]{1,0:T(8,128)S(1)} fusion(bf16[256,1024]{1,0:T(8,128)(2,1)S(1)} %copy-done.4, bf16[256,1024]{1,0:T(8,128)(2,1)S(1)} %copy-done.3, bf16[256,1024]{1,0:T(8,128)(2,1)S(1)} %copy-done.2, bf16[1,1024,3072]{2,1,0:T(8,128)(2,1)} %param.8), kind=kOutput, calls=%fused_computation.17 | convolution fusion | flops 1615331328 | bytes 8912896 | tf_op jit(solution)/shard_map/rc,dc->rd/dot_general | solution.py:163
  77.4 1.5 %fusion.38 = bf16[1,256,1024]{2,1,0:T(8,128)(2,1)} fusion(bf16[256,1024]{1,0:T(8,128)(2,1)S(1)} %copy-done.1, bf16[1,1024,1024]{2,1,0:T(8,128)(2,1)S(1)} %copy-done, bf16[256,1024]{1,0:T(8,128)(2,1)S(1)} %collective-permute-done), kind=kOutput, calls=%fused_computation.32 | convolution fusion | flops 537657344 | bytes 3670016 | tf_op jit(solution)/shard_map/dot_general | solution.py:151
  78.9 1.4 %collective-permute-done.4 = bf16[256,1024]{1,0:T(8,128)(2,1)S(1)} collective-permute-done((bf16[256,1024]{1,0:T(8,128)(2,1)S(1)}, bf16[256,1024]{1,0:T(8,128)(2,1)S(1)}, u32[]{:S(2)}, u32[]{:S(2)}) %collective-permute-start.4) | collective-permute-done | bytes 524320 | tf_op jit(solution)/shard_map/ppermute | solution.py:29
  80.3 1.2 %collective-permute-done.5 = bf16[256,1024]{1,0:T(8,128)(2,1)S(1)} collective-permute-done((bf16[256,1024]{1,0:T(8,128)(2,1)S(1)}, bf16[256,1024]{1,0:T(8,128)(2,1)S(1)}, u32[]{:S(2)}, u32[]{:S(2)}) %collective-permute-start.5) | collective-permute-done | bytes 524320 | tf_op jit(solution)/shard_map/ppermute | solution.py:34
  81.4 0.4 fusion.41
  81.8 2.3 %fusion.49 = bf16[1,256,1024]{2,1,0:T(8,128)(2,1)} fusion(bf16[256,1024]{1,0:T(8,128)(2,1)S(1)} %collective-permute-done, bf16[256,1024]{1,0:T(8,128)(2,1)} %collective-permute-done.3, f32[256]{0:T(256)S(1)} %broadcast_multiply_fusion, f32[256]{0:T(256)S(1)} %add_rsqrt_fusion.1, bf16[256,1024]{1,0:T(8,128)(2,1)S(1)} %collective-permute-done.5, ...), kind=kLoop, calls=%fused_computation.42 | loop fusion | flops 3145728 | bytes 3672064 | tf_op jit(solution)/shard_map/broadcast_in_dim | solution.py:171
  (19 shorter events, 0.1 us)
Async XLA Ops:
  0.6 24.6 %copy-start = (bf16[1,1024,1024]{2,1,0:T(8,128)(2,1)S(1)}, bf16[1,1024,1024]{2,1,0:T(8,128)(2,1)}, u32[]{:S(2)}) copy-start(bf16[1,1024,1024]{2,1,0:T(8,128)(2,1)} %param.9) | copy-start | bytes 6291460
  0.6 12.7 %collective-permute-start = (bf16[256,1024]{1,0:T(8,128)(2,1)}, bf16[256,1024]{1,0:T(8,128)(2,1)S(1)}, u32[]{:S(2)}, u32[]{:S(2)}) collective-permute-start(bf16[256,1024]{1,0:T(8,128)(2,1)} %bitcast.40), channel_id=1, source_target_pairs={{0,64},{64,128},{128,192},{192,0},{1,65},{65,129},{129,193},{193,1... | collective-permute-start | bytes 1572872 | tf_op jit(solution)/shard_map/ppermute | solution.py:24
  0.7 24.5 %collective-permute-start.3 = (bf16[256,1024]{1,0:T(8,128)(2,1)}, bf16[256,1024]{1,0:T(8,128)(2,1)}, u32[]{:S(2)}, u32[]{:S(2)}) collective-permute-start(bf16[256,1024]{1,0:T(8,128)(2,1)} %bitcast.41), channel_id=1, source_target_pairs={{0,192},{64,0},{128,64},{192,128},{1,193},{65,1},{129,65},{193,129... | collective-permute-start | bytes 1572872 | tf_op jit(solution)/shard_map/ppermute | solution.py:24
  13.3 20.6 %collective-permute-start.2 = (bf16[256,1024]{1,0:T(8,128)(2,1)S(1)}, bf16[256,1024]{1,0:T(8,128)(2,1)S(1)}, u32[]{:S(2)}, u32[]{:S(2)}) collective-permute-start(bf16[256,1024]{1,0:T(8,128)(2,1)S(1)} %collective-permute-done), channel_id=1, source_target_pairs={{1,0},{2,1},{3,2},{4,3},{5,4},{6,5},{7,6},{8,7},{9,8},{10,9},{11,1... | collective-permute-start | bytes 1572872 | tf_op jit(solution)/shard_map/ppermute | solution.py:34
  23.1 17.5 %collective-permute-start.1 = (bf16[256,1024]{1,0:T(8,128)(2,1)S(1)}, bf16[256,1024]{1,0:T(8,128)(2,1)S(1)}, u32[]{:S(2)}, u32[]{:S(2)}) collective-permute-start(bf16[256,1024]{1,0:T(8,128)(2,1)S(1)} %collective-permute-done), channel_id=1, source_target_pairs={{0,1},{1,2},{2,3},{3,4},{4,5},{5,6},{6,7},{7,8},{8,9},{9,10},{10,1... | collective-permute-start | bytes 1572872 | tf_op jit(solution)/shard_map/ppermute | solution.py:29
  25.2 15.7 %slice-start = ((s8[6291456]{0:T(1024)(128)(4,1)}), s8[4194304]{0:T(1024)(128)(4,1)S(1)}, s32[]{:S(2)}) async-start(s8[6291456]{0:T(1024)(128)(4,1)} %bitcast.37), calls=%async_computation | async-start | bytes 8388608
  28.0 13.0 %slice-start.1 = ((s8[6291456]{0:T(1024)(128)(4,1)}), s8[2097152]{0:T(1024)(128)(4,1)S(1)}, s32[]{:S(2)}) async-start(s8[6291456]{0:T(1024)(128)(4,1)} %bitcast.37), calls=%async_computation.1 | async-start | bytes 4194304
  63.3 9.3 %copy-start.2 = (bf16[256,1024]{1,0:T(8,128)(2,1)S(1)}, bf16[256,1024]{1,0:T(8,128)(2,1)}, u32[]{:S(2)}) copy-start(bf16[256,1024]{1,0:T(8,128)(2,1)} %get-tuple-element.9) | copy-start | bytes 1572868
  63.4 9.3 %copy-start.3 = (bf16[256,1024]{1,0:T(8,128)(2,1)S(1)}, bf16[256,1024]{1,0:T(8,128)(2,1)}, u32[]{:S(2)}) copy-start(bf16[256,1024]{1,0:T(8,128)(2,1)} %get-tuple-element.10) | copy-start | bytes 1572868
  63.4 9.3 %copy-start.4 = (bf16[256,1024]{1,0:T(8,128)(2,1)S(1)}, bf16[256,1024]{1,0:T(8,128)(2,1)}, u32[]{:S(2)}) copy-start(bf16[256,1024]{1,0:T(8,128)(2,1)} %get-tuple-element.11) | copy-start | bytes 1572868
  63.5 16.8 %collective-permute-start.4 = (bf16[256,1024]{1,0:T(8,128)(2,1)S(1)}, bf16[256,1024]{1,0:T(8,128)(2,1)S(1)}, u32[]{:S(2)}, u32[]{:S(2)}) collective-permute-start(bf16[256,1024]{1,0:T(8,128)(2,1)S(1)} %get-tuple-element.14), channel_id=1, source_target_pairs={{0,1},{1,2},{2,3},{3,4},{4,5},{5,6},{6,7},{7,8},{8,9},{9,10},{10,1... | collective-permute-start | bytes 1572872 | tf_op jit(solution)/shard_map/ppermute | solution.py:29
  65.5 15.9 %collective-permute-start.5 = (bf16[256,1024]{1,0:T(8,128)(2,1)S(1)}, bf16[256,1024]{1,0:T(8,128)(2,1)S(1)}, u32[]{:S(2)}, u32[]{:S(2)}) collective-permute-start(bf16[256,1024]{1,0:T(8,128)(2,1)S(1)} %get-tuple-element.15), channel_id=1, source_target_pairs={{1,0},{2,1},{3,2},{4,3},{5,4},{6,5},{7,6},{8,7},{9,8},{10,9},{11,1... | collective-permute-start | bytes 1572872 | tf_op jit(solution)/shard_map/ppermute | solution.py:34
  72.7 4.7 %copy-start.1 = (bf16[256,1024]{1,0:T(8,128)(2,1)S(1)}, bf16[256,1024]{1,0:T(8,128)(2,1)}, u32[]{:S(2)}) copy-start(bf16[256,1024]{1,0:T(8,128)(2,1)} %get-tuple-element.8) | copy-start | bytes 1572868

commit v3 on v2

--- a/solution.py
+++ b/solution.py
@@ -126,7 +126,9 @@
     )
     values, factor, normed = normalize(arrived)
     projected = jnp.dot(
-        normed.astype(jnp.bfloat16), weights_in, preferred_element_type=jnp.float32
+        lax.optimization_barrier(normed.astype(jnp.bfloat16)),
+        weights_in,
+        preferred_element_type=jnp.float32,
     ).astype(jnp.bfloat16)
     attended_grad = jnp.einsum(
         "rd,wd->rw", upstream, weights_out, preferred_element_type=jnp.float32
@@ -134,7 +136,9 @@
     _, _, halo_normed = normalize(halo_rows)
     weights_kv = weights_in[:, width:]
     halo_kv = jnp.dot(
-        halo_normed.astype(jnp.bfloat16), weights_kv, preferred_element_type=jnp.float32
+        lax.optimization_barrier(halo_normed.astype(jnp.bfloat16)),
+        weights_kv,
+        preferred_element_type=jnp.float32,
     ).astype(jnp.bfloat16)
 
     window_index = key_blocks - first_block + REACH

time: 84.6 us -> 85.2 us (level)
  no operation moved by 1% of the time
where the time goes in v3:
time: 85.2 us; the launch traced here: 84.7 us
  starting transfers between devices  24.2 us (28%)
  matrix products  23.7 us (28%)
  waiting for transfers between devices  16 us (19%)
  Pallas kernels  13.4 us (16%)
  other arithmetic  5.06 us (6%)
  local copies, waits for them, and re-layouts  1.51 us (2%)
    ppermute x2, starting transfers between devices, from_right(): return lax.ppermute(value, axis, [(i + 1, i) for i in range(count - 1)])  16.9 us
    pallas_call x1, Pallas kernels, attention(): pl.pallas_call(attention_kernel, grid=(heads,), in_specs=[own(0), own(hea...  13.4 us
    ppermute x2, waiting for transfers between devices, from_left(): return lax.ppermute(value, axis, [(i, i + 1) for i in range(count - 1)])  8.32 us
    ppermute x2, waiting for transfers between devices, shifted(): return lax.ppermute(value, axis, pairs)  6.45 us
    dot_general x1, matrix products, per_device(): jnp.dot(lax.optimization_barrier(normed.astype(jnp.bfloat16)), weights_in...  5.89 us
    dot_general x1, matrix products, per_device(): jnp.einsum('rc,dc->rd', halo_grads, weights_kv, preferred_element_type=jn...  5.2 us
    dot_general x1, matrix products, per_device(): jnp.einsum('rc,dc->rd', own_grads, weights_in, preferred_element_type=jnp...  4.66 us
    ppermute x2, starting transfers between devices, from_left(): return lax.ppermute(value, axis, [(i, i + 1) for i in range(count - 1)])  3.97 us
  transfers between devices with their start and end apart: 6, of which 4 were waited for; matrix products, arithmetic and copies ran while one was open for 21% of the time, Pallas kernels for 0%

profile of v3, /device:TPU:24, one launch (start us, length us, event | category | flops | bytes accessed | tf_op | source)
XLA Modules:
  0.0 84.7 jit_solution(2765093740766506102)
XLA Ops:
  0.6 0.0 copy-start
  0.6 0.1 collective-permute-start
  0.7 3.2 %collective-permute-start.3 = (bf16[256,1024]{1,0:T(8,128)(2,1)}, bf16[256,1024]{1,0:T(8,128)(2,1)}, u32[]{:S(2)}, u32[]{:S(2)}) collective-permute-start(bf16[256,1024]{1,0:T(8,128)(2,1)} %bitcast.43), channel_id=1, source_target_pairs={{0,192},{64,0},{128,64},{192,128},{1,193},{65,1},{129,65},{193,129... | collective-permute-start | bytes 1572872 | tf_op jit(solution)/shard_map/ppermute | solution.py:24
  4.0 0.7 iota_compare_fusion.1
  4.7 0.7 subtract_add_fusion
  5.4 0.1 fusion.49
  5.5 0.1 copy.9
  5.6 0.1 broadcast_bitcast_fusion
  5.7 0.1 broadcast_in_dim.31
  5.7 1.2 %copy.10.live_ref = f32[256,768]{1,0:T(8,128)} copy(f32[256,768]{0,1:T(8,128)S(1)} %bitcast.36) | data formatting | bytes 1572864 | tf_op jit(solution)/shard_map/jit(_where)/select_n | solution.py:150
  6.9 6.5 %collective-permute-done = bf16[256,1024]{1,0:T(8,128)(2,1)S(1)} collective-permute-done((bf16[256,1024]{1,0:T(8,128)(2,1)}, bf16[256,1024]{1,0:T(8,128)(2,1)S(1)}, u32[]{:S(2)}, u32[]{:S(2)}) %collective-permute-start) | collective-permute-done | bytes 524320 | tf_op jit(solution)/shard_map/ppermute | solution.py:24
  13.3 0.2 fusion.46
  13.5 0.2 fusion.29
  13.7 9.8 %collective-permute-start.2 = (bf16[256,1024]{1,0:T(8,128)(2,1)S(1)}, bf16[256,1024]{1,0:T(8,128)(2,1)S(1)}, u32[]{:S(2)}, u32[]{:S(2)}) collective-permute-start(bf16[256,1024]{1,0:T(8,128)(2,1)S(1)} %collective-permute-done), channel_id=1, source_target_pairs={{1,0},{2,1},{3,2},{4,3},{5,4},{6,5},{7,6},{8,7},{9,8},{10,9},{11,1... | collective-permute-start | bytes 1572872 | tf_op jit(solution)/shard_map/ppermute | solution.py:34
  23.5 1.9 %collective-permute-start.1 = (bf16[256,1024]{1,0:T(8,128)(2,1)S(1)}, bf16[256,1024]{1,0:T(8,128)(2,1)S(1)}, u32[]{:S(2)}, u32[]{:S(2)}) collective-permute-start(bf16[256,1024]{1,0:T(8,128)(2,1)S(1)} %collective-permute-done), channel_id=1, source_target_pairs={{0,1},{1,2},{2,3},{3,4},{4,5},{5,6},{6,7},{7,8},{8,9},{9,10},{10,1... | collective-permute-start | bytes 1572872 | tf_op jit(solution)/shard_map/ppermute | solution.py:29
  25.4 2.7 %fusion.35.do_ref = bf16[256,1024]{1,0:T(8,128)(2,1)} fusion(bf16[256,1024]{1,0:T(8,128)(2,1)} %collective-permute-done.3, bf16[1,1024,1024]{2,1,0:T(8,128)(2,1)S(1)} %copy-done), kind=kOutput, calls=%fused_computation.31 | convolution fusion | flops 537133056 | bytes 3145728 | tf_op jit(solution)/shard_map/rd,wd->rw/dot_general | solution.py:133
  28.2 5.9 %convolution_convert_fusion.q_ref.ko_ref.vo_ref = bf16[256,3072]{1,0:T(8,128)(2,1)} fusion(bf16[256,1024]{1,0:T(8,128)(2,1)S(1)} %fusion.29, bf16[1,1024,3072]{2,1,0:T(8,128)(2,1)} %param.8), kind=kOutput, calls=%fused_computation | convolution fusion | flops 1611399168 | bytes 8388608 | tf_op jit(solution)/shard_map/dot_general | solution.py:128
  34.1 6.9 %collective-permute-done.1 = bf16[256,1024]{1,0:T(8,128)(2,1)S(1)} collective-permute-done((bf16[256,1024]{1,0:T(8,128)(2,1)S(1)}, bf16[256,1024]{1,0:T(8,128)(2,1)S(1)}, u32[]{:S(2)}, u32[]{:S(2)}) %collective-permute-start.1) | collective-permute-done | bytes 524320 | tf_op jit(solution)/shard_map/ppermute | solution.py:29
  41.0 0.3 fusion.7
  41.3 0.2 fusion.8
  41.6 3.7 %fusion.4.kh_ref.vh_ref = bf16[512,2048]{1,0:T(8,128)(2,1)} fusion(bf16[512,1024]{1,0:T(8,128)(2,1)S(1)} %fusion.8, bf16[1024,3072]{1,0:T(8,128)(2,1)S(1)} %bitcast.41), kind=kOutput, calls=%fused_computation.5 | convolution fusion | flops 2148532224 | bytes 7340032 | tf_op jit(solution)/shard_map/dot_general | solution.py:138
  45.3 13.4 %shard_map.77 = (bf16[256,1024]{1,0:T(8,128)(2,1)}, bf16[256,1024]{1,0:T(8,128)(2,1)}, bf16[256,1024]{1,0:T(8,128)(2,1)}, bf16[256,1024]{1,0:T(8,128)(2,1)}, bf1...) custom-call(bf16[256,3072]{1,0:T(8,128)(2,1)} %convolution_convert_fusion.q_ref.ko_ref.vo_ref, ...), custom_call_target="tpu_custom_call" | custom-call | flops 2013265920 | bytes 9175040 | tf_op jit(solution)/shard_map/pallas_call | solution.py:89
  58.7 5.2 %fusion.22 = bf16[512,1024]{1,0:T(8,128)(2,1)S(1)} fusion(bf16[1024,3072]{1,0:T(8,128)(2,1)} %bitcast.38, bf16[512,1024]{1,0:T(8,128)(2,1)} %get-tuple-element.13, bf16[512,1024]{1,0:T(8,128)(2,1)} %get-tuple-element.12), kind=kOutput, calls=%fused_computation.26 | convolution fusion | flops 2152202240 | bytes 7340032 | tf_op jit(solution)/shard_map/rc,dc->rd/dot_general | solution.py:160
  63.9 0.1 fusion.54
  64.0 2.1 %collective-permute-start.4 = (bf16[256,1024]{1,0:T(8,128)(2,1)S(1)}, bf16[256,1024]{1,0:T(8,128)(2,1)S(1)}, u32[]{:S(2)}, u32[]{:S(2)}) collective-permute-start(bf16[256,1024]{1,0:T(8,128)(2,1)S(1)} %get-tuple-element.14), channel_id=1, source_target_pairs={{0,1},{1,2},{2,3},{3,4},{4,5},{5,6},{6,7},{7,8},{8,9},{9,10},{10,1... | collective-permute-start | bytes 1572872 | tf_op jit(solution)/shard_map/ppermute | solution.py:29
  66.1 7.1 %collective-permute-start.5 = (bf16[256,1024]{1,0:T(8,128)(2,1)S(1)}, bf16[256,1024]{1,0:T(8,128)(2,1)S(1)}, u32[]{:S(2)}, u32[]{:S(2)}) collective-permute-start(bf16[256,1024]{1,0:T(8,128)(2,1)S(1)} %get-tuple-element.15), channel_id=1, source_target_pairs={{1,0},{2,1},{3,2},{4,3},{5,4},{6,5},{7,6},{8,7},{9,8},{10,9},{11,1... | collective-permute-start | bytes 1572872 | tf_op jit(solution)/shard_map/ppermute | solution.py:34
  73.2 4.7 %fusion.16 = f32[256,1024]{1,0:T(8,128)S(1)} fusion(bf16[256,1024]{1,0:T(8,128)(2,1)S(1)} %copy-done.4, bf16[256,1024]{1,0:T(8,128)(2,1)S(1)} %copy-done.3, bf16[256,1024]{1,0:T(8,128)(2,1)S(1)} %copy-done.2, bf16[1,1024,3072]{2,1,0:T(8,128)(2,1)} %param.8), kind=kOutput, calls=%fused_computation.17 | convolution fusion | flops 1615331328 | bytes 8912896 | tf_op jit(solution)/shard_map/rc,dc->rd/dot_general | solution.py:167
  77.9 1.5 %fusion.38 = bf16[1,256,1024]{2,1,0:T(8,128)(2,1)} fusion(bf16[256,1024]{1,0:T(8,128)(2,1)S(1)} %copy-done.1, bf16[1,1024,1024]{2,1,0:T(8,128)(2,1)S(1)} %copy-done, bf16[256,1024]{1,0:T(8,128)(2,1)S(1)} %collective-permute-done), kind=kOutput, calls=%fused_computation.32 | convolution fusion | flops 537657344 | bytes 3670016 | tf_op jit(solution)/shard_map/dot_general | solution.py:155
  79.4 1.4 %collective-permute-done.4 = bf16[256,1024]{1,0:T(8,128)(2,1)S(1)} collective-permute-done((bf16[256,1024]{1,0:T(8,128)(2,1)S(1)}, bf16[256,1024]{1,0:T(8,128)(2,1)S(1)}, u32[]{:S(2)}, u32[]{:S(2)}) %collective-permute-start.4) | collective-permute-done | bytes 524320 | tf_op jit(solution)/shard_map/ppermute | solution.py:29
  80.8 1.2 %collective-permute-done.5 = bf16[256,1024]{1,0:T(8,128)(2,1)S(1)} collective-permute-done((bf16[256,1024]{1,0:T(8,128)(2,1)S(1)}, bf16[256,1024]{1,0:T(8,128)(2,1)S(1)}, u32[]{:S(2)}, u32[]{:S(2)}) %collective-permute-start.5) | collective-permute-done | bytes 524320 | tf_op jit(solution)/shard_map/ppermute | solution.py:34
  82.0 0.4 fusion.41
  82.4 2.3 %fusion.47 = bf16[1,256,1024]{2,1,0:T(8,128)(2,1)} fusion(bf16[256,1024]{1,0:T(8,128)(2,1)S(1)} %collective-permute-done, bf16[256,1024]{1,0:T(8,128)(2,1)} %collective-permute-done.3, f32[256]{0:T(256)S(1)} %broadcast_multiply_fusion, f32[256]{0:T(256)S(1)} %add_rsqrt_fusion.1, bf16[256,1024]{1,0:T(8,128)(2,1)S(1)} %collective-permute-done.5, ...), kind=kLoop, calls=%fused_computation.41 | loop fusion | flops 3145728 | bytes 3672064 | tf_op jit(solution)/shard_map/broadcast_in_dim | solution.py:175
  (21 shorter events, 0.1 us)
Async XLA Ops:
  0.6 24.8 %copy-start = (bf16[1,1024,1024]{2,1,0:T(8,128)(2,1)S(1)}, bf16[1,1024,1024]{2,1,0:T(8,128)(2,1)}, u32[]{:S(2)}) copy-start(bf16[1,1024,1024]{2,1,0:T(8,128)(2,1)} %param.9) | copy-start | bytes 6291460
  0.6 12.7 %collective-permute-start = (bf16[256,1024]{1,0:T(8,128)(2,1)}, bf16[256,1024]{1,0:T(8,128)(2,1)S(1)}, u32[]{:S(2)}, u32[]{:S(2)}) collective-permute-start(bf16[256,1024]{1,0:T(8,128)(2,1)} %bitcast.42), channel_id=1, source_target_pairs={{0,64},{64,128},{128,192},{192,0},{1,65},{65,129},{129,193},{193,1... | collective-permute-start | bytes 1572872 | tf_op jit(solution)/shard_map/ppermute | solution.py:24
  0.7 24.7 %collective-permute-start.3 = (bf16[256,1024]{1,0:T(8,128)(2,1)}, bf16[256,1024]{1,0:T(8,128)(2,1)}, u32[]{:S(2)}, u32[]{:S(2)}) collective-permute-start(bf16[256,1024]{1,0:T(8,128)(2,1)} %bitcast.43), channel_id=1, source_target_pairs={{0,192},{64,0},{128,64},{192,128},{1,193},{65,1},{129,65},{193,129... | collective-permute-start | bytes 1572872 | tf_op jit(solution)/shard_map/ppermute | solution.py:24
  13.7 20.4 %collective-permute-start.2 = (bf16[256,1024]{1,0:T(8,128)(2,1)S(1)}, bf16[256,1024]{1,0:T(8,128)(2,1)S(1)}, u32[]{:S(2)}, u32[]{:S(2)}) collective-permute-start(bf16[256,1024]{1,0:T(8,128)(2,1)S(1)} %collective-permute-done), channel_id=1, source_target_pairs={{1,0},{2,1},{3,2},{4,3},{5,4},{6,5},{7,6},{8,7},{9,8},{10,9},{11,1... | collective-permute-start | bytes 1572872 | tf_op jit(solution)/shard_map/ppermute | solution.py:34
  23.5 17.5 %collective-permute-start.1 = (bf16[256,1024]{1,0:T(8,128)(2,1)S(1)}, bf16[256,1024]{1,0:T(8,128)(2,1)S(1)}, u32[]{:S(2)}, u32[]{:S(2)}) collective-permute-start(bf16[256,1024]{1,0:T(8,128)(2,1)S(1)} %collective-permute-done), channel_id=1, source_target_pairs={{0,1},{1,2},{2,3},{3,4},{4,5},{5,6},{6,7},{7,8},{8,9},{9,10},{10,1... | collective-permute-start | bytes 1572872 | tf_op jit(solution)/shard_map/ppermute | solution.py:29
  25.4 16.1 %slice-start = ((s8[6291456]{0:T(1024)(128)(4,1)}), s8[4194304]{0:T(1024)(128)(4,1)S(1)}, s32[]{:S(2)}) async-start(s8[6291456]{0:T(1024)(128)(4,1)} %bitcast.39), calls=%async_computation | async-start | bytes 8388608
  28.2 13.4 %slice-start.1 = ((s8[6291456]{0:T(1024)(128)(4,1)}), s8[2097152]{0:T(1024)(128)(4,1)S(1)}, s32[]{:S(2)}) async-start(s8[6291456]{0:T(1024)(128)(4,1)} %bitcast.39), calls=%async_computation.1 | async-start | bytes 4194304
  63.9 9.3 %copy-start.2 = (bf16[256,1024]{1,0:T(8,128)(2,1)S(1)}, bf16[256,1024]{1,0:T(8,128)(2,1)}, u32[]{:S(2)}) copy-start(bf16[256,1024]{1,0:T(8,128)(2,1)} %get-tuple-element.9) | copy-start | bytes 1572868
  63.9 9.3 %copy-start.3 = (bf16[256,1024]{1,0:T(8,128)(2,1)S(1)}, bf16[256,1024]{1,0:T(8,128)(2,1)}, u32[]{:S(2)}) copy-start(bf16[256,1024]{1,0:T(8,128)(2,1)} %get-tuple-element.10) | copy-start | bytes 1572868
  63.9 9.3 %copy-start.4 = (bf16[256,1024]{1,0:T(8,128)(2,1)S(1)}, bf16[256,1024]{1,0:T(8,128)(2,1)}, u32[]{:S(2)}) copy-start(bf16[256,1024]{1,0:T(8,128)(2,1)} %get-tuple-element.11) | copy-start | bytes 1572868
  64.0 16.8 %collective-permute-start.4 = (bf16[256,1024]{1,0:T(8,128)(2,1)S(1)}, bf16[256,1024]{1,0:T(8,128)(2,1)S(1)}, u32[]{:S(2)}, u32[]{:S(2)}) collective-permute-start(bf16[256,1024]{1,0:T(8,128)(2,1)S(1)} %get-tuple-element.14), channel_id=1, source_target_pairs={{0,1},{1,2},{2,3},{3,4},{4,5},{5,6},{6,7},{7,8},{8,9},{9,10},{10,1... | collective-permute-start | bytes 1572872 | tf_op jit(solution)/shard_map/ppermute | solution.py:29
  66.1 15.9 %collective-permute-start.5 = (bf16[256,1024]{1,0:T(8,128)(2,1)S(1)}, bf16[256,1024]{1,0:T(8,128)(2,1)S(1)}, u32[]{:S(2)}, u32[]{:S(2)}) collective-permute-start(bf16[256,1024]{1,0:T(8,128)(2,1)S(1)} %get-tuple-element.15), channel_id=1, source_target_pairs={{1,0},{2,1},{3,2},{4,3},{5,4},{6,5},{7,6},{8,7},{9,8},{10,9},{11,1... | collective-permute-start | bytes 1572872 | tf_op jit(solution)/shard_map/ppermute | solution.py:34
  73.2 4.7 %copy-start.1 = (bf16[256,1024]{1,0:T(8,128)(2,1)S(1)}, bf16[256,1024]{1,0:T(8,128)(2,1)}, u32[]{:S(2)}) copy-start(bf16[256,1024]{1,0:T(8,128)(2,1)} %get-tuple-element.8) | copy-start | bytes 1572868

commit v4 on v3

--- a/solution.py
+++ b/solution.py
@@ -41,53 +41,76 @@
 
 
 def attention_kernel(
-    q_ref, ko_ref, vo_ref, kh_ref, vh_ref, do_ref, live_ref,
+    slot_ref, q_ref, ko_ref, vo_ref, kh_ref, vh_ref, do_ref, bias_ref,
     out_ref, dq_ref, dk_ref, dv_ref, dkh_ref, dvh_ref,
+    key_window, value_window, key_acc, value_acc,
 ):
     rows = q_ref.shape[0]
     margin = kh_ref.shape[0] // 2
+    nblock, slot_count = slot_ref.shape
     scaling = HEAD_DIM ** (-0.5)
-    queries = q_ref[...]
-    keys = jnp.concatenate([kh_ref[:margin], ko_ref[...], kh_ref[margin:]], axis=0)
-    values = jnp.concatenate([vh_ref[:margin], vo_ref[...], vh_ref[margin:]], axis=0)
-    grad_out = do_ref[...]
-    scores = lax.dot_general(queries, keys, NT, preferred_element_type=jnp.float32) * scaling
-    scores = scores + live_ref[...]
-    row_max = jnp.max(scores, axis=1, keepdims=True)
-    raw = jnp.exp(scores - row_max)
-    weights = raw * (1.0 / jnp.sum(raw, axis=1, keepdims=True))
-    weights_bf = weights.astype(jnp.bfloat16)
-    out_ref[...] = jnp.dot(weights_bf, values, preferred_element_type=jnp.float32).astype(
-        out_ref.dtype
-    )
-    weight_grad = lax.dot_general(grad_out, values, NT, preferred_element_type=jnp.float32)
-    weight_mean = jnp.sum(weights * weight_grad, axis=1, keepdims=True)
-    score_grad = (weights * (weight_grad - weight_mean) * scaling).astype(jnp.bfloat16)
-    dq_ref[...] = jnp.dot(score_grad, keys, preferred_element_type=jnp.float32).astype(dq_ref.dtype)
-    key_grad = lax.dot_general(score_grad, queries, TN, preferred_element_type=jnp.float32)
-    value_grad = lax.dot_general(weights_bf, grad_out, TN, preferred_element_type=jnp.float32)
+    key_window[:margin] = kh_ref[:margin]
+    key_window[margin : margin + rows] = ko_ref[...]
+    key_window[margin + rows :] = kh_ref[margin:]
+    value_window[:margin] = vh_ref[:margin]
+    value_window[margin : margin + rows] = vo_ref[...]
+    value_window[margin + rows :] = vh_ref[margin:]
+    key_acc[...] = jnp.zeros_like(key_acc)
+    value_acc[...] = jnp.zeros_like(value_acc)
+    for block in range(nblock):
+        here = slice(block * BLOCK, (block + 1) * BLOCK)
+        starts = [
+            pl.multiple_of(slot_ref[block, slot] * BLOCK, BLOCK) for slot in range(slot_count)
+        ]
+        queries = q_ref[here]
+        grad_out = do_ref[here]
+        keys = jnp.concatenate([key_window[pl.ds(start, BLOCK)] for start in starts], axis=0)
+        values = jnp.concatenate([value_window[pl.ds(start, BLOCK)] for start in starts], axis=0)
+        scores = lax.dot_general(queries, keys, NT, preferred_element_type=jnp.float32) * scaling
+        scores = scores + bias_ref[block : block + 1, :]
+        row_max = jnp.max(scores, axis=1, keepdims=True)
+        raw = jnp.exp(scores - row_max)
+        weights = raw * (1.0 / jnp.sum(raw, axis=1, keepdims=True))
+        weights_bf = weights.astype(jnp.bfloat16)
+        out_ref[here] = jnp.dot(weights_bf, values, preferred_element_type=jnp.float32).astype(
+            out_ref.dtype
+        )
+        weight_grad = lax.dot_general(grad_out, values, NT, preferred_element_type=jnp.float32)
+        weight_mean = jnp.sum(weights * weight_grad, axis=1, keepdims=True)
+        score_grad = (weights * (weight_grad - weight_mean) * scaling).astype(jnp.bfloat16)
+        dq_ref[here] = jnp.dot(score_grad, keys, preferred_element_type=jnp.float32).astype(
+            dq_ref.dtype
+        )
+        key_grad = lax.dot_general(score_grad, queries, TN, preferred_element_type=jnp.float32)
+        value_grad = lax.dot_general(weights_bf, grad_out, TN, preferred_element_type=jnp.float32)
+        for slot, start in enumerate(starts):
+            part = slice(slot * BLOCK, (slot + 1) * BLOCK)
+            key_acc[pl.ds(start, BLOCK)] += key_grad[part]
+            value_acc[pl.ds(start, BLOCK)] += value_grad[part]
     dtype = dk_ref.dtype
-    dk_ref[...] = key_grad[margin : margin + rows].astype(dtype)
-    dv_ref[...] = value_grad[margin : margin + rows].astype(dtype)
-    dkh_ref[:margin] = key_grad[:margin].astype(dtype)
-    dkh_ref[margin:] = key_grad[margin + rows :].astype(dtype)
-    dvh_ref[:margin] = value_grad[:margin].astype(dtype)
-    dvh_ref[margin:] = value_grad[margin + rows :].astype(dtype)
-
-
-def attention(projected, halo_kv, attended_grad, live):
+    dk_ref[...] = key_acc[margin : margin + rows].astype(dtype)
+    dv_ref[...] = value_acc[margin : margin + rows].astype(dtype)
+    dkh_ref[:margin] = key_acc[:margin].astype(dtype)
+    dkh_ref[margin:] = key_acc[margin + rows :].astype(dtype)
+    dvh_ref[:margin] = value_acc[:margin].astype(dtype)
+    dvh_ref[margin:] = value_acc[margin + rows :].astype(dtype)
+
+
+def attention(projected, halo_kv, attended_grad, slot_window, slot_bias):
     rows, width = attended_grad.shape
     heads = width // HEAD_DIM
     halo_rows = halo_kv.shape[0]
-    window = live.shape[1]
-    own = lambda offset: pl.BlockSpec((rows, HEAD_DIM), lambda h: (0, offset + h))
-    side = lambda offset: pl.BlockSpec((halo_rows, HEAD_DIM), lambda h: (0, offset + h))
-    flops = heads * 5 * 2 * rows * window * HEAD_DIM
-    moved = 2 * (2 * projected.size + 2 * halo_kv.size + 2 * attended_grad.size) + 4 * live.size
+    window_rows = rows + halo_rows
+    nblock, slot_count = slot_window.shape
+    keys = slot_count * BLOCK
+    own = lambda offset: pl.BlockSpec((rows, HEAD_DIM), lambda h, s: (0, offset + h))
+    side = lambda offset: pl.BlockSpec((halo_rows, HEAD_DIM), lambda h, s: (0, offset + h))
+    flops = heads * 5 * 2 * rows * keys * HEAD_DIM
+    moved = 2 * (2 * projected.size + 2 * halo_kv.size + 2 * attended_grad.size) + 4 * slot_bias.size
     own_shape = jax.ShapeDtypeStruct((rows, width), jnp.bfloat16)
     side_shape = jax.ShapeDtypeStruct((halo_rows, width), jnp.bfloat16)
-    return pl.pallas_call(
-        attention_kernel,
+    grid_spec = pltpu.PrefetchScalarGridSpec(
+        num_scalar_prefetch=1,
         grid=(heads,),
         in_specs=[
             own(0),
@@ -96,15 +119,25 @@
             side(0),
             side(heads),
             own(0),
-            pl.BlockSpec((rows, window), lambda h: (0, 0)),
+            pl.BlockSpec((nblock, keys), lambda h, s: (0, 0)),
         ],
         out_specs=[own(0), own(0), own(0), own(0), side(0), side(0)],
+        scratch_shapes=[
+            pltpu.VMEM((window_rows, HEAD_DIM), jnp.bfloat16),
+            pltpu.VMEM((window_rows, HEAD_DIM), jnp.bfloat16),
+            pltpu.VMEM((window_rows, HEAD_DIM), jnp.float32),
+            pltpu.VMEM((window_rows, HEAD_DIM), jnp.float32),
+        ],
+    )
+    return pl.pallas_call(
+        attention_kernel,
+        grid_spec=grid_spec,
         out_shape=[own_shape, own_shape, own_shape, own_shape, side_shape, side_shape],
         compiler_params=pltpu.CompilerParams(dimension_semantics=("arbitrary",)),
         cost_estimate=pl.CostEstimate(
-            flops=flops, transcendentals=heads * rows * window, bytes_accessed=moved
+            flops=flops, transcendentals=heads * rows * keys, bytes_accessed=moved
         ),
-    )(projected, projected, projected, halo_kv, halo_kv, attended_grad, live)
+    )(slot_window, projected, projected, projected, halo_kv, halo_kv, attended_grad, slot_bias)
 
 
 def per_device(activations, cotangent, input_weights, output_weights, key_blocks, block_counts):
@@ -141,16 +174,12 @@
         preferred_element_type=jnp.float32,
     ).astype(jnp.bfloat16)
 
-    window_index = key_blocks - first_block + REACH
+    window_index = jnp.clip(key_blocks - first_block + REACH, 0, span_blocks - 1)
     live_slots = jnp.arange(slot_count)[None, :] < block_counts[:, None]
-    live_blocks = jnp.any(
-        live_slots[:, :, None] & (window_index[:, :, None] == jnp.arange(span_blocks)[None, None, :]),
-        axis=1,
-    )
-    live = jnp.where(jnp.repeat(jnp.repeat(live_blocks, BLOCK, axis=0), BLOCK, axis=1), 0.0, -1e30)
+    slot_bias = jnp.repeat(jnp.where(live_slots, 0.0, -1e30), BLOCK, axis=1)
 
     attended, query_grad, key_grad, value_grad, halo_key_grad, halo_value_grad = attention(
-        projected, halo_kv, attended_grad, live
+        projected, halo_kv, attended_grad, window_index.astype(jnp.int32), slot_bias
     )
     result = (values + jnp.dot(attended, weights_out, preferred_element_type=jnp.float32)).astype(
         jnp.bfloat16

time: 85.2 us -> 86.5 us (1.015)
  Pallas kernels: 13.4 us -> 15.8 us
  waiting for transfers between devices: 16 us -> 17.4 us
  matrix products: 23.7 us -> 22.5 us
    pallas_call x1, Pallas kernels: 13.4 us -> 15.8 us  [attention(): pl.pallas_call(attention_kernel, grid_spec=grid_spec, out_shape=[own_shap...]
    min x0 -> x1, other arithmetic: none -> 1.26 us  [per_device(): jnp.clip(key_blocks - first_block + REACH, 0, span_blocks - 1)]
    select_n x2 -> x0, local copies, waits for them, and re-layouts: 1.26 us -> none  [per_device(): jnp.where(jnp.repeat(jnp.repeat(live_blocks, BLOCK, axis=0), BLOCK, axis=...]
    dot_general x1, matrix products: 2.73 us -> 1.54 us  [per_device(): jnp.einsum('rd,wd->rw', upstream, weights_out, preferred_element_type=jnp...]
    broadcast_in_dim x1, other arithmetic: 2.28 us -> 1.23 us  [per_device(): return (result[None], input_grad[None])]
    ppermute x2, waiting for transfers between devices: 1.18 us -> 2.21 us  [from_right(): return lax.ppermute(value, axis, [(i + 1, i) for i in range(count - 1)])]
  transfers between devices with their start and end apart: 6 -> 6, of which waited for: 4 -> 5; matrix products, arithmetic and copies ran while one was open for 21% -> 19% of each run, Pallas kernels for 0% -> 0%
where the time goes in v4:
time: 86.5 us; the launch traced here: 86 us
  starting transfers between devices  24.2 us (28%)
  matrix products  22.5 us (26%)
  waiting for transfers between devices  17.4 us (20%)
  Pallas kernels  15.8 us (18%)
  other arithmetic  4.49 us (5%)
    ppermute x2, starting transfers between devices, from_right(): return lax.ppermute(value, axis, [(i + 1, i) for i in range(count - 1)])  16.9 us
    pallas_call x1, Pallas kernels, attention(): pl.pallas_call(attention_kernel, grid_spec=grid_spec, out_shape=[own_shap...  15.8 us
    ppermute x2, waiting for transfers between devices, from_left(): return lax.ppermute(value, axis, [(i, i + 1) for i in range(count - 1)])  8.51 us
    ppermute x2, waiting for transfers between devices, shifted(): return lax.ppermute(value, axis, pairs)  6.73 us
    dot_general x1, matrix products, per_device(): jnp.dot(lax.optimization_barrier(normed.astype(jnp.bfloat16)), weights_in...  5.88 us
    dot_general x1, matrix products, per_device(): jnp.einsum('rc,dc->rd', halo_grads, weights_kv, preferred_element_type=jn...  5.2 us
    dot_general x1, matrix products, per_device(): jnp.einsum('rc,dc->rd', own_grads, weights_in, preferred_element_type=jnp...  4.66 us
    ppermute x2, starting transfers between devices, from_left(): return lax.ppermute(value, axis, [(i, i + 1) for i in range(count - 1)])  3.97 us
  transfers between devices with their start and end apart: 6, of which 5 were waited for; matrix products, arithmetic and copies ran while one was open for 19% of the time, Pallas kernels for 0%

profile of v4, /device:TPU:24, one launch (start us, length us, event | category | flops | bytes accessed | tf_op | source)
XLA Modules:
  0.0 86.0 jit_solution(15198394266902131484)
XLA Ops:
  0.6 0.0 copy-start
  0.6 0.1 collective-permute-start
  0.7 3.2 %collective-permute-start.3 = (bf16[256,1024]{1,0:T(8,128)(2,1)}, bf16[256,1024]{1,0:T(8,128)(2,1)S(1)}, u32[]{:S(2)}, u32[]{:S(2)}) collective-permute-start(bf16[256,1024]{1,0:T(8,128)(2,1)} %bitcast.39), channel_id=1, source_target_pairs={{0,192},{64,0},{128,64},{192,128},{1,193},{65,1},{129,65},{193,129... | collective-permute-start | bytes 1572872 | tf_op jit(solution)/shard_map/ppermute | solution.py:24
  4.0 0.7 compare_select_fusion
  4.7 0.1 broadcast_bitcast_fusion
  4.8 0.6 copy.10
  5.4 1.3 %add_clamp_fusion.slot_ref = s32[2,4]{1,0:T(2,128)} fusion(s32[2,4]{1,0:T(2,128)} %param.10, s32[]{:T(128)S(6)} %mul.42), kind=kLoop, calls=%fused_computation.47 | loop fusion | flops 24 | bytes 68 | tf_op jit(solution)/shard_map/jit(clip)/min | solution.py:177
  6.6 6.7 %collective-permute-done = bf16[256,1024]{1,0:T(8,128)(2,1)S(1)} collective-permute-done((bf16[256,1024]{1,0:T(8,128)(2,1)}, bf16[256,1024]{1,0:T(8,128)(2,1)S(1)}, u32[]{:S(2)}, u32[]{:S(2)}) %collective-permute-start) | collective-permute-done | bytes 524320 | tf_op jit(solution)/shard_map/ppermute | solution.py:24
  13.3 0.2 fusion.46
  13.5 0.2 fusion.29
  13.7 9.8 %collective-permute-start.2 = (bf16[256,1024]{1,0:T(8,128)(2,1)S(1)}, bf16[256,1024]{1,0:T(8,128)(2,1)S(1)}, u32[]{:S(2)}, u32[]{:S(2)}) collective-permute-start(bf16[256,1024]{1,0:T(8,128)(2,1)S(1)} %collective-permute-done), channel_id=1, source_target_pairs={{1,0},{2,1},{3,2},{4,3},{5,4},{6,5},{7,6},{8,7},{9,8},{10,9},{11,1... | collective-permute-start | bytes 1572872 | tf_op jit(solution)/shard_map/ppermute | solution.py:34
  23.5 1.9 %collective-permute-start.1 = (bf16[256,1024]{1,0:T(8,128)(2,1)S(1)}, bf16[256,1024]{1,0:T(8,128)(2,1)S(1)}, u32[]{:S(2)}, u32[]{:S(2)}) collective-permute-start(bf16[256,1024]{1,0:T(8,128)(2,1)S(1)} %collective-permute-done), channel_id=1, source_target_pairs={{0,1},{1,2},{2,3},{3,4},{4,5},{5,6},{6,7},{7,8},{8,9},{9,10},{10,1... | collective-permute-start | bytes 1572872 | tf_op jit(solution)/shard_map/ppermute | solution.py:29
  25.4 0.0 slice-start
  25.4 1.5 %fusion.35.do_ref = bf16[256,1024]{1,0:T(8,128)(2,1)} fusion(bf16[256,1024]{1,0:T(8,128)(2,1)S(1)} %collective-permute-done.3, bf16[1,1024,1024]{2,1,0:T(8,128)(2,1)S(1)} %copy-done), kind=kOutput, calls=%fused_computation.31 | convolution fusion | flops 537133056 | bytes 3145728 | tf_op jit(solution)/shard_map/rd,wd->rw/dot_general | solution.py:166
  27.0 5.9 %convolution_convert_fusion.q_ref.ko_ref.vo_ref = bf16[256,3072]{1,0:T(8,128)(2,1)} fusion(bf16[256,1024]{1,0:T(8,128)(2,1)S(1)} %fusion.29, bf16[1,1024,3072]{2,1,0:T(8,128)(2,1)} %param.8), kind=kOutput, calls=%fused_computation | convolution fusion | flops 1611399168 | bytes 8388608 | tf_op jit(solution)/shard_map/dot_general | solution.py:161
  32.9 1.0 %collective-permute-done.2 = bf16[256,1024]{1,0:T(8,128)(2,1)S(1)} collective-permute-done((bf16[256,1024]{1,0:T(8,128)(2,1)S(1)}, bf16[256,1024]{1,0:T(8,128)(2,1)S(1)}, u32[]{:S(2)}, u32[]{:S(2)}) %collective-permute-start.2) | collective-permute-done | bytes 524320 | tf_op jit(solution)/shard_map/ppermute | solution.py:34
  33.9 7.1 %collective-permute-done.1 = bf16[256,1024]{1,0:T(8,128)(2,1)S(1)} collective-permute-done((bf16[256,1024]{1,0:T(8,128)(2,1)S(1)}, bf16[256,1024]{1,0:T(8,128)(2,1)S(1)}, u32[]{:S(2)}, u32[]{:S(2)}) %collective-permute-start.1) | collective-permute-done | bytes 524320 | tf_op jit(solution)/shard_map/ppermute | solution.py:29
  41.0 0.3 fusion.7
  41.3 0.2 fusion.8
  41.6 3.7 %fusion.4.kh_ref.vh_ref = bf16[512,2048]{1,0:T(8,128)(2,1)} fusion(bf16[512,1024]{1,0:T(8,128)(2,1)S(1)} %fusion.8, bf16[1024,3072]{1,0:T(8,128)(2,1)S(1)} %bitcast.37), kind=kOutput, calls=%fused_computation.5 | convolution fusion | flops 2148532224 | bytes 7340032 | tf_op jit(solution)/shard_map/dot_general | solution.py:171
  45.3 15.8 %shard_map.77 = (bf16[256,1024]{1,0:T(8,128)(2,1)}, bf16[256,1024]{1,0:T(8,128)(2,1)}, bf16[256,1024]{1,0:T(8,128)(2,1)}, bf16[256,1024]{1,0:T(8,128)(2,1)}, bf1...) custom-call(s32[2,4]{1,0:T(2,128)} %add_clamp_fusion.slot_ref, ...), custom_call_target="tpu_custom_call" | custom-call | flops 1342177280 | bytes 8392704 | tf_op jit(solution)/shard_map/pallas_call | solution.py:132
  61.1 5.2 %fusion.22 = bf16[512,1024]{1,0:T(8,128)(2,1)S(1)} fusion(bf16[1024,3072]{1,0:T(8,128)(2,1)} %bitcast.34, bf16[512,1024]{1,0:T(8,128)(2,1)} %get-tuple-element.13, bf16[512,1024]{1,0:T(8,128)(2,1)} %get-tuple-element.12), kind=kOutput, calls=%fused_computation.26 | convolution fusion | flops 2152202240 | bytes 7340032 | tf_op jit(solution)/shard_map/rc,dc->rd/dot_general | solution.py:189
  66.3 0.1 fusion.52
  66.4 2.1 %collective-permute-start.4 = (bf16[256,1024]{1,0:T(8,128)(2,1)S(1)}, bf16[256,1024]{1,0:T(8,128)(2,1)S(1)}, u32[]{:S(2)}, u32[]{:S(2)}) collective-permute-start(bf16[256,1024]{1,0:T(8,128)(2,1)S(1)} %get-tuple-element.14), channel_id=1, source_target_pairs={{0,1},{1,2},{2,3},{3,4},{4,5},{5,6},{6,7},{7,8},{8,9},{9,10},{10,1... | collective-permute-start | bytes 1572872 | tf_op jit(solution)/shard_map/ppermute | solution.py:29
  68.5 7.1 %collective-permute-start.5 = (bf16[256,1024]{1,0:T(8,128)(2,1)S(1)}, bf16[256,1024]{1,0:T(8,128)(2,1)S(1)}, u32[]{:S(2)}, u32[]{:S(2)}) collective-permute-start(bf16[256,1024]{1,0:T(8,128)(2,1)S(1)} %get-tuple-element.15), channel_id=1, source_target_pairs={{1,0},{2,1},{3,2},{4,3},{5,4},{6,5},{7,6},{8,7},{9,8},{10,9},{11,1... | collective-permute-start | bytes 1572872 | tf_op jit(solution)/shard_map/ppermute | solution.py:34
  75.6 0.0 copy-start.1
  75.6 4.7 %fusion.16 = f32[256,1024]{1,0:T(8,128)S(1)} fusion(bf16[256,1024]{1,0:T(8,128)(2,1)S(1)} %copy-done.4, bf16[256,1024]{1,0:T(8,128)(2,1)S(1)} %copy-done.3, bf16[256,1024]{1,0:T(8,128)(2,1)S(1)} %copy-done.2, bf16[1,1024,3072]{2,1,0:T(8,128)(2,1)} %param.8), kind=kOutput, calls=%fused_computation.17 | convolution fusion | flops 1615331328 | bytes 8912896 | tf_op jit(solution)/shard_map/rc,dc->rd/dot_general | solution.py:196
  80.3 1.5 %fusion.38 = bf16[1,256,1024]{2,1,0:T(8,128)(2,1)} fusion(bf16[256,1024]{1,0:T(8,128)(2,1)S(1)} %copy-done.1, bf16[1,1024,1024]{2,1,0:T(8,128)(2,1)S(1)} %copy-done, bf16[256,1024]{1,0:T(8,128)(2,1)S(1)} %collective-permute-done), kind=kOutput, calls=%fused_computation.32 | convolution fusion | flops 537657344 | bytes 3670016 | tf_op jit(solution)/shard_map/dot_general | solution.py:184
  81.9 1.4 %collective-permute-done.4 = bf16[256,1024]{1,0:T(8,128)(2,1)S(1)} collective-permute-done((bf16[256,1024]{1,0:T(8,128)(2,1)S(1)}, bf16[256,1024]{1,0:T(8,128)(2,1)S(1)}, u32[]{:S(2)}, u32[]{:S(2)}) %collective-permute-start.4) | collective-permute-done | bytes 524320 | tf_op jit(solution)/shard_map/ppermute | solution.py:29
  83.2 1.2 %collective-permute-done.5 = bf16[256,1024]{1,0:T(8,128)(2,1)S(1)} collective-permute-done((bf16[256,1024]{1,0:T(8,128)(2,1)S(1)}, bf16[256,1024]{1,0:T(8,128)(2,1)S(1)}, u32[]{:S(2)}, u32[]{:S(2)}) %collective-permute-start.5) | collective-permute-done | bytes 524320 | tf_op jit(solution)/shard_map/ppermute | solution.py:34
  84.4 0.4 fusion.41
  84.8 1.2 %fusion.47 = bf16[1,256,1024]{2,1,0:T(8,128)(2,1)} fusion(bf16[256,1024]{1,0:T(8,128)(2,1)S(1)} %collective-permute-done, bf16[256,1024]{1,0:T(8,128)(2,1)S(1)} %collective-permute-done.3, f32[256]{0:T(256)S(1)} %broadcast_multiply_fusion, f32[256]{0:T(256)S(1)} %add_rsqrt_fusion.1, bf16[256,1024]{1,0:T(8,128)(2,1)S(1)} %collective-permute-done.5, ...), kind=kLoop, calls=%fused_computation.41 | loop fusion | flops 3145728 | bytes 3672064 | tf_op jit(solution)/shard_map/broadcast_in_dim | solution.py:204
  (16 shorter events, 0.0 us)
Async XLA Ops:
  0.6 24.8 %copy-start = (bf16[1,1024,1024]{2,1,0:T(8,128)(2,1)S(1)}, bf16[1,1024,1024]{2,1,0:T(8,128)(2,1)}, u32[]{:S(2)}) copy-start(bf16[1,1024,1024]{2,1,0:T(8,128)(2,1)} %param.9) | copy-start | bytes 6291460
  0.6 12.7 %collective-permute-start = (bf16[256,1024]{1,0:T(8,128)(2,1)}, bf16[256,1024]{1,0:T(8,128)(2,1)S(1)}, u32[]{:S(2)}, u32[]{:S(2)}) collective-permute-start(bf16[256,1024]{1,0:T(8,128)(2,1)} %bitcast.38), channel_id=1, source_target_pairs={{0,64},{64,128},{128,192},{192,0},{1,65},{65,129},{129,193},{193,1... | collective-permute-start | bytes 1572872 | tf_op jit(solution)/shard_map/ppermute | solution.py:24
  0.7 24.7 %collective-permute-start.3 = (bf16[256,1024]{1,0:T(8,128)(2,1)}, bf16[256,1024]{1,0:T(8,128)(2,1)S(1)}, u32[]{:S(2)}, u32[]{:S(2)}) collective-permute-start(bf16[256,1024]{1,0:T(8,128)(2,1)} %bitcast.39), channel_id=1, source_target_pairs={{0,192},{64,0},{128,64},{192,128},{1,193},{65,1},{129,65},{193,129... | collective-permute-start | bytes 1572872 | tf_op jit(solution)/shard_map/ppermute | solution.py:24
  13.7 20.2 %collective-permute-start.2 = (bf16[256,1024]{1,0:T(8,128)(2,1)S(1)}, bf16[256,1024]{1,0:T(8,128)(2,1)S(1)}, u32[]{:S(2)}, u32[]{:S(2)}) collective-permute-start(bf16[256,1024]{1,0:T(8,128)(2,1)S(1)} %collective-permute-done), channel_id=1, source_target_pairs={{1,0},{2,1},{3,2},{4,3},{5,4},{6,5},{7,6},{8,7},{9,8},{10,9},{11,1... | collective-permute-start | bytes 1572872 | tf_op jit(solution)/shard_map/ppermute | solution.py:34
  23.5 17.5 %collective-permute-start.1 = (bf16[256,1024]{1,0:T(8,128)(2,1)S(1)}, bf16[256,1024]{1,0:T(8,128)(2,1)S(1)}, u32[]{:S(2)}, u32[]{:S(2)}) collective-permute-start(bf16[256,1024]{1,0:T(8,128)(2,1)S(1)} %collective-permute-done), channel_id=1, source_target_pairs={{0,1},{1,2},{2,3},{3,4},{4,5},{5,6},{6,7},{7,8},{8,9},{9,10},{10,1... | collective-permute-start | bytes 1572872 | tf_op jit(solution)/shard_map/ppermute | solution.py:29
  25.4 16.1 %slice-start = ((s8[6291456]{0:T(1024)(128)(4,1)}), s8[4194304]{0:T(1024)(128)(4,1)S(1)}, s32[]{:S(2)}) async-start(s8[6291456]{0:T(1024)(128)(4,1)} %bitcast.35), calls=%async_computation | async-start | bytes 8388608
  27.0 14.6 %slice-start.1 = ((s8[6291456]{0:T(1024)(128)(4,1)}), s8[2097152]{0:T(1024)(128)(4,1)S(1)}, s32[]{:S(2)}) async-start(s8[6291456]{0:T(1024)(128)(4,1)} %bitcast.35), calls=%async_computation.1 | async-start | bytes 4194304
  66.3 9.3 %copy-start.2 = (bf16[256,1024]{1,0:T(8,128)(2,1)S(1)}, bf16[256,1024]{1,0:T(8,128)(2,1)}, u32[]{:S(2)}) copy-start(bf16[256,1024]{1,0:T(8,128)(2,1)} %get-tuple-element.9) | copy-start | bytes 1572868
  66.3 9.3 %copy-start.3 = (bf16[256,1024]{1,0:T(8,128)(2,1)S(1)}, bf16[256,1024]{1,0:T(8,128)(2,1)}, u32[]{:S(2)}) copy-start(bf16[256,1024]{1,0:T(8,128)(2,1)} %get-tuple-element.10) | copy-start | bytes 1572868
  66.3 9.3 %copy-start.4 = (bf16[256,1024]{1,0:T(8,128)(2,1)S(1)}, bf16[256,1024]{1,0:T(8,128)(2,1)}, u32[]{:S(2)}) copy-start(bf16[256,1024]{1,0:T(8,128)(2,1)} %get-tuple-element.11) | copy-start | bytes 1572868
  66.4 16.8 %collective-permute-start.4 = (bf16[256,1024]{1,0:T(8,128)(2,1)S(1)}, bf16[256,1024]{1,0:T(8,128)(2,1)S(1)}, u32[]{:S(2)}, u32[]{:S(2)}) collective-permute-start(bf16[256,1024]{1,0:T(8,128)(2,1)S(1)} %get-tuple-element.14), channel_id=1, source_target_pairs={{0,1},{1,2},{2,3},{3,4},{4,5},{5,6},{6,7},{7,8},{8,9},{9,10},{10,1... | collective-permute-start | bytes 1572872 | tf_op jit(solution)/shard_map/ppermute | solution.py:29
  68.5 15.9 %collective-permute-start.5 = (bf16[256,1024]{1,0:T(8,128)(2,1)S(1)}, bf16[256,1024]{1,0:T(8,128)(2,1)S(1)}, u32[]{:S(2)}, u32[]{:S(2)}) collective-permute-start(bf16[256,1024]{1,0:T(8,128)(2,1)S(1)} %get-tuple-element.15), channel_id=1, source_target_pairs={{1,0},{2,1},{3,2},{4,3},{5,4},{6,5},{7,6},{8,7},{9,8},{10,9},{11,1... | collective-permute-start | bytes 1572872 | tf_op jit(solution)/shard_map/ppermute | solution.py:34
  75.6 4.7 %copy-start.1 = (bf16[256,1024]{1,0:T(8,128)(2,1)S(1)}, bf16[256,1024]{1,0:T(8,128)(2,1)}, u32[]{:S(2)}) copy-start(bf16[256,1024]{1,0:T(8,128)(2,1)} %get-tuple-element.8) | copy-start | bytes 1572868

commit v5 on v2

--- a/solution.py
+++ b/solution.py
@@ -41,9 +41,10 @@
 
 
 def attention_kernel(
-    q_ref, ko_ref, vo_ref, kh_ref, vh_ref, do_ref, live_ref,
-    out_ref, dq_ref, dk_ref, dv_ref, dkh_ref, dvh_ref,
+    q_ref, ko_ref, vo_ref, kh_ref, vh_ref, do_ref, live_ref, wk_ref, wv_ref,
+    out_ref, dq_ref, dk_ref, dv_ref, halo_ref, halo_acc,
 ):
+    head = pl.program_id(0)
     rows = q_ref.shape[0]
     margin = kh_ref.shape[0] // 2
     scaling = HEAD_DIM ** (-0.5)
@@ -69,13 +70,28 @@
     dtype = dk_ref.dtype
     dk_ref[...] = key_grad[margin : margin + rows].astype(dtype)
     dv_ref[...] = value_grad[margin : margin + rows].astype(dtype)
-    dkh_ref[:margin] = key_grad[:margin].astype(dtype)
-    dkh_ref[margin:] = key_grad[margin + rows :].astype(dtype)
-    dvh_ref[:margin] = value_grad[:margin].astype(dtype)
-    dvh_ref[margin:] = value_grad[margin + rows :].astype(dtype)
-
-
-def attention(projected, halo_kv, attended_grad, live):
+    halo_key = jnp.concatenate([key_grad[:margin], key_grad[margin + rows :]], axis=0)
+    halo_value = jnp.concatenate([value_grad[:margin], value_grad[margin + rows :]], axis=0)
+    partial = lax.dot_general(
+        halo_key.astype(dtype), wk_ref[...], NT, preferred_element_type=jnp.float32
+    ) + lax.dot_general(
+        halo_value.astype(dtype), wv_ref[...], NT, preferred_element_type=jnp.float32
+    )
+
+    @pl.when(head == 0)
+    def _():
+        halo_acc[...] = partial
+
+    @pl.when(head > 0)
+    def _():
+        halo_acc[...] += partial
+
+    @pl.when(head == pl.num_programs(0) - 1)
+    def _():
+        halo_ref[...] = halo_acc[...].astype(halo_ref.dtype)
+
+
+def attention(projected, halo_kv, attended_grad, live, weights_in):
     rows, width = attended_grad.shape
     heads = width // HEAD_DIM
     halo_rows = halo_kv.shape[0]
@@ -85,7 +101,10 @@
     flops = heads * 5 * 2 * rows * window * HEAD_DIM
     moved = 2 * (2 * projected.size + 2 * halo_kv.size + 2 * attended_grad.size) + 4 * live.size
     own_shape = jax.ShapeDtypeStruct((rows, width), jnp.bfloat16)
-    side_shape = jax.ShapeDtypeStruct((halo_rows, width), jnp.bfloat16)
+    features = weights_in.shape[0]
+    column = lambda offset: pl.BlockSpec((features, HEAD_DIM), lambda h: (0, offset + h))
+    flops += heads * 2 * 2 * halo_rows * HEAD_DIM * features
+    moved += 2 * 2 * features * width + 2 * halo_rows * features
     return pl.pallas_call(
         attention_kernel,
         grid=(heads,),
@@ -97,14 +116,22 @@
             side(heads),
             own(0),
             pl.BlockSpec((rows, window), lambda h: (0, 0)),
+            column(heads),
+            column(2 * heads),
         ],
-        out_specs=[own(0), own(0), own(0), own(0), side(0), side(0)],
-        out_shape=[own_shape, own_shape, own_shape, own_shape, side_shape, side_shape],
+        out_specs=[
+            own(0), own(0), own(0), own(0), pl.BlockSpec((halo_rows, features), lambda h: (0, 0))
+        ],
+        out_shape=[
+            own_shape, own_shape, own_shape, own_shape,
+            jax.ShapeDtypeStruct((halo_rows, features), jnp.bfloat16),
+        ],
+        scratch_shapes=[pltpu.VMEM((halo_rows, features), jnp.float32)],
         compiler_params=pltpu.CompilerParams(dimension_semantics=("arbitrary",)),
         cost_estimate=pl.CostEstimate(
             flops=flops, transcendentals=heads * rows * window, bytes_accessed=moved
         ),
-    )(projected, projected, projected, halo_kv, halo_kv, attended_grad, live)
+    )(projected, projected, projected, halo_kv, halo_kv, attended_grad, live, weights_in, weights_in)
 
 
 def per_device(activations, cotangent, input_weights, output_weights, key_blocks, block_counts):
@@ -145,17 +172,13 @@
     )
     live = jnp.where(jnp.repeat(jnp.repeat(live_blocks, BLOCK, axis=0), BLOCK, axis=1), 0.0, -1e30)
 
-    attended, query_grad, key_grad, value_grad, halo_key_grad, halo_value_grad = attention(
-        projected, halo_kv, attended_grad, live
+    attended, query_grad, key_grad, value_grad, halo_normed_grad = attention(
+        projected, halo_kv, attended_grad, live, weights_in
     )
     result = (values + jnp.dot(attended, weights_out, preferred_element_type=jnp.float32)).astype(
         jnp.bfloat16
     )
 
-    halo_grads = jnp.concatenate([halo_key_grad, halo_value_grad], axis=1)
-    halo_normed_grad = jnp.einsum(
-        "rc,dc->rd", halo_grads, weights_kv, preferred_element_type=jnp.float32
-    ).astype(jnp.bfloat16)
     head_part = from_left(halo_normed_grad[margin:], "seq")
     tail_part = from_right(halo_normed_grad[:margin], "seq")
     own_grads = jnp.concatenate([query_grad, key_grad, value_grad], axis=1)

time: 84.6 us -> 87.3 us (1.032)
  Pallas kernels: 13.4 us -> 20.1 us
  matrix products: 23.8 us -> 18.6 us
  local copies, waits for them, and re-layouts: 1.51 us -> 2.83 us
    pallas_call x1, Pallas kernels: 13.4 us -> 20.1 us  [attention(): pl.pallas_call(attention_kernel, grid=(heads,), in_specs=[own(0), own(hea...]
    dot_general x1 -> x0, matrix products: 5.2 us -> none  [per_device(): jnp.einsum('rc,dc->rd', halo_grads, weights_kv, preferred_element_type=jn...]
    slice x1, local copies, waits for them, and re-layouts: 0.07 us -> 1.38 us  [per_device(): head_part = from_left(halo_normed_grad[margin:], 'seq')]
where the time goes in v5:
time: 87.3 us; the launch traced here: 86.8 us
  starting transfers between devices  24 us (27%)
  Pallas kernels  20.1 us (23%)
  matrix products  18.6 us (21%)
  waiting for transfers between devices  15.7 us (18%)
  other arithmetic  4.65 us (5%)
  local copies, waits for them, and re-layouts  2.83 us (3%)
    pallas_call x1, Pallas kernels, attention(): pl.pallas_call(attention_kernel, grid=(heads,), in_specs=[own(0), own(hea...  20.1 us
    ppermute x2, starting transfers between devices, from_right(): return lax.ppermute(value, axis, [(i + 1, i) for i in range(count - 1)])  16.9 us
    ppermute x2, waiting for transfers between devices, from_left(): return lax.ppermute(value, axis, [(i, i + 1) for i in range(count - 1)])  8.08 us
    ppermute x2, waiting for transfers between devices, shifted(): return lax.ppermute(value, axis, pairs)  6.44 us
    dot_general x1, matrix products, per_device(): jnp.dot(normed.astype(jnp.bfloat16), weights_in, preferred_element_type=j...  5.97 us
    dot_general x1, matrix products, per_device(): jnp.einsum('rc,dc->rd', own_grads, weights_in, preferred_element_type=jnp...  4.66 us
    ppermute x2, starting transfers between devices, from_left(): return lax.ppermute(value, axis, [(i, i + 1) for i in range(count - 1)])  3.84 us
    dot_general x1, matrix products, per_device(): jnp.dot(halo_normed.astype(jnp.bfloat16), weights_kv, preferred_element_t...  3.76 us
  transfers between devices with their start and end apart: 6, of which 4 were waited for; matrix products, arithmetic and copies ran while one was open for 21% of the time, Pallas kernels for 0%

profile of v5, /device:TPU:24, one launch (start us, length us, event | category | flops | bytes accessed | tf_op | source)
XLA Modules:
  0.0 86.8 jit_solution(9465306910710826503)
XLA Ops:
  0.6 0.0 copy-start
  0.6 0.1 collective-permute-start
  0.7 3.2 %collective-permute-start.3 = (bf16[256,1024]{1,0:T(8,128)(2,1)}, bf16[256,1024]{1,0:T(8,128)(2,1)}, u32[]{:S(2)}, u32[]{:S(2)}) collective-permute-start(bf16[256,1024]{1,0:T(8,128)(2,1)} %bitcast.42), channel_id=1, source_target_pairs={{0,192},{64,0},{128,64},{192,128},{1,193},{65,1},{129,65},{193,129... | collective-permute-start | bytes 1572872 | tf_op jit(solution)/shard_map/ppermute | solution.py:24
  4.0 0.7 iota_compare_fusion.1
  4.7 0.7 subtract_add_fusion
  5.4 0.1 fusion.43
  5.5 0.1 copy.9
  5.6 0.1 broadcast_bitcast_fusion
  5.7 0.1 broadcast_in_dim.31
  5.7 1.2 %copy.10.live_ref = f32[256,768]{1,0:T(8,128)} copy(f32[256,768]{0,1:T(8,128)S(1)} %bitcast.39) | data formatting | bytes 1572864 | tf_op jit(solution)/shard_map/jit(_where)/select_n | solution.py:173
  6.9 6.4 %collective-permute-done = bf16[256,1024]{1,0:T(8,128)(2,1)S(1)} collective-permute-done((bf16[256,1024]{1,0:T(8,128)(2,1)}, bf16[256,1024]{1,0:T(8,128)(2,1)S(1)}, u32[]{:S(2)}, u32[]{:S(2)}) %collective-permute-start) | collective-permute-done | bytes 524320 | tf_op jit(solution)/shard_map/ppermute | solution.py:24
  13.3 9.8 %collective-permute-start.2 = (bf16[256,1024]{1,0:T(8,128)(2,1)S(1)}, bf16[256,1024]{1,0:T(8,128)(2,1)S(1)}, u32[]{:S(2)}, u32[]{:S(2)}) collective-permute-start(bf16[256,1024]{1,0:T(8,128)(2,1)S(1)} %collective-permute-done), channel_id=1, source_target_pairs={{1,0},{2,1},{3,2},{4,3},{5,4},{6,5},{7,6},{8,7},{9,8},{10,9},{11,1... | collective-permute-start | bytes 1572872 | tf_op jit(solution)/shard_map/ppermute | solution.py:34
  23.1 1.9 %collective-permute-start.1 = (bf16[256,1024]{1,0:T(8,128)(2,1)S(1)}, bf16[256,1024]{1,0:T(8,128)(2,1)S(1)}, u32[]{:S(2)}, u32[]{:S(2)}) collective-permute-start(bf16[256,1024]{1,0:T(8,128)(2,1)S(1)} %collective-permute-done), channel_id=1, source_target_pairs={{0,1},{1,2},{2,3},{3,4},{4,5},{5,6},{6,7},{7,8},{8,9},{9,10},{10,1... | collective-permute-start | bytes 1572872 | tf_op jit(solution)/shard_map/ppermute | solution.py:29
  25.0 0.2 fusion.36
  25.2 0.0 collective-permute-done.3
  25.2 0.0 slice-start
  25.3 2.7 %fusion.25.do_ref = bf16[256,1024]{1,0:T(8,128)(2,1)} fusion(bf16[256,1024]{1,0:T(8,128)(2,1)} %collective-permute-done.3, bf16[1,1024,1024]{2,1,0:T(8,128)(2,1)S(1)} %copy-done), kind=kOutput, calls=%fused_computation.25 | convolution fusion | flops 537133056 | bytes 3145728 | tf_op jit(solution)/shard_map/rd,wd->rw/dot_general | solution.py:158
  28.0 6.0 %convolution_convert_fusion.q_ref.ko_ref.vo_ref = bf16[256,3072]{1,0:T(8,128)(2,1)} fusion(bf16[256,1024]{1,0:T(8,128)(2,1)S(1)} %collective-permute-done, f32[256]{0:T(256)S(1)} %add_rsqrt_fusion.1, bf16[1,1024,3072]{2,1,0:T(8,128)(2,1)} %param.8), kind=kOutput, calls=%fused_computation.2 | convolution fusion | flops 1612185600 | bytes 8389632 | tf_op jit(solution)/shard_map/dot_general | solution.py:155
  34.0 6.7 %collective-permute-done.1 = bf16[256,1024]{1,0:T(8,128)(2,1)S(1)} collective-permute-done((bf16[256,1024]{1,0:T(8,128)(2,1)S(1)}, bf16[256,1024]{1,0:T(8,128)(2,1)S(1)}, u32[]{:S(2)}, u32[]{:S(2)}) %collective-permute-start.1) | collective-permute-done | bytes 524320 | tf_op jit(solution)/shard_map/ppermute | solution.py:29
  40.6 0.3 fusion.5
  41.0 3.8 %fusion.2.kh_ref.vh_ref = bf16[512,2048]{1,0:T(8,128)(2,1)} fusion(bf16[1024,3072]{1,0:T(8,128)(2,1)S(1)} %bitcast.38, f32[512]{0:T(512)S(1)} %add_rsqrt_fusion, bf16[256,1024]{1,0:T(8,128)(2,1)S(1)} %collective-permute-done.2, bf16[256,1024]{1,0:T(8,128)(2,1)S(1)} %collective-permute-done.1), kind=kOutput, calls=%fused_computation.3 | convolution fusion | flops 2151677952 | bytes 7342080 | tf_op jit(solution)/shard_map/dot_general | solution.py:163
  44.7 20.1 %shard_map.77 = (bf16[256,1024]{1,0:T(8,128)(2,1)}, bf16[256,1024]{1,0:T(8,128)(2,1)}, bf16[256,1024]{1,0:T(8,128)(2,1)}, bf16[256,1024]{1,0:T(8,128)(2,1)}, bf16[512,1024]{1,0:T(8,128)(2,1)}) custom-call(bf16[256,3072]{1,0:T(8,128)(2,1)} %convolution_convert_fusion.q_ref.ko_ref.vo_ref, bf16[256,3072]{1,0:T(8,128)(2,1)} %convolution_convert_fusion.q_ref.ko_ref.vo_ref, ...), custom_call_target="tpu_custom_call" | custom-call | flops 4160749568 | bytes 14417920 | tf_op jit(solution)/shard_map/pallas_call | solution.py:108
  64.8 1.4 %fusion.48 = (bf16[256,1024]{1,0:T(8,128)(2,1)S(1)}, bf16[256,1024]{1,0:T(8,128)(2,1)S(1)}) fusion(bf16[512,1024]{1,0:T(8,128)(2,1)} %get-tuple-element.11), kind=kLoop, calls=%fused_computation.53 | loop fusion | bytes 2097152 | tf_op jit(solution)/shard_map/slice | solution.py:182
  66.2 1.9 %collective-permute-start.4 = (bf16[256,1024]{1,0:T(8,128)(2,1)S(1)}, bf16[256,1024]{1,0:T(8,128)(2,1)S(1)}, u32[]{:S(2)}, u32[]{:S(2)}) collective-permute-start(bf16[256,1024]{1,0:T(8,128)(2,1)S(1)} %get-tuple-element.12), channel_id=1, source_target_pairs={{0,1},{1,2},{2,3},{3,4},{4,5},{5,6},{6,7},{7,8},{8,9},{9,10},{10,1... | collective-permute-start | bytes 1572872 | tf_op jit(solution)/shard_map/ppermute | solution.py:29
  68.2 7.1 %collective-permute-start.5 = (bf16[256,1024]{1,0:T(8,128)(2,1)S(1)}, bf16[256,1024]{1,0:T(8,128)(2,1)S(1)}, u32[]{:S(2)}, u32[]{:S(2)}) collective-permute-start(bf16[256,1024]{1,0:T(8,128)(2,1)S(1)} %get-tuple-element.13), channel_id=1, source_target_pairs={{1,0},{2,1},{3,2},{4,3},{5,4},{6,5},{7,6},{8,7},{9,8},{10,9},{11,1... | collective-permute-start | bytes 1572872 | tf_op jit(solution)/shard_map/ppermute | solution.py:34
  75.3 0.0 copy-start.1
  75.3 4.7 %fusion.11 = f32[256,1024]{1,0:T(8,128)S(1)} fusion(bf16[256,1024]{1,0:T(8,128)(2,1)S(1)} %copy-done.4, bf16[256,1024]{1,0:T(8,128)(2,1)S(1)} %copy-done.3, bf16[256,1024]{1,0:T(8,128)(2,1)S(1)} %copy-done.2, bf16[1,1024,3072]{2,1,0:T(8,128)(2,1)} %param.8), kind=kOutput, calls=%fused_computation.12 | convolution fusion | flops 1615331328 | bytes 8912896 | tf_op jit(solution)/shard_map/rc,dc->rd/dot_general | solution.py:186
  80.0 1.5 %fusion.28 = bf16[1,256,1024]{2,1,0:T(8,128)(2,1)} fusion(bf16[256,1024]{1,0:T(8,128)(2,1)S(1)} %copy-done.1, bf16[1,1024,1024]{2,1,0:T(8,128)(2,1)S(1)} %copy-done, bf16[256,1024]{1,0:T(8,128)(2,1)S(1)} %collective-permute-done), kind=kOutput, calls=%fused_computation.26 | convolution fusion | flops 537657344 | bytes 3670016 | tf_op jit(solution)/shard_map/dot_general | solution.py:178
  81.5 1.4 %collective-permute-done.4 = bf16[256,1024]{1,0:T(8,128)(2,1)S(1)} collective-permute-done((bf16[256,1024]{1,0:T(8,128)(2,1)S(1)}, bf16[256,1024]{1,0:T(8,128)(2,1)S(1)}, u32[]{:S(2)}, u32[]{:S(2)}) %collective-permute-start.4) | collective-permute-done | bytes 524320 | tf_op jit(solution)/shard_map/ppermute | solution.py:29
  82.9 1.2 %collective-permute-done.5 = bf16[256,1024]{1,0:T(8,128)(2,1)S(1)} collective-permute-done((bf16[256,1024]{1,0:T(8,128)(2,1)S(1)}, bf16[256,1024]{1,0:T(8,128)(2,1)S(1)}, u32[]{:S(2)}, u32[]{:S(2)}) %collective-permute-start.5) | collective-permute-done | bytes 524320 | tf_op jit(solution)/shard_map/ppermute | solution.py:34
  84.1 0.4 fusion.31
  84.5 2.3 %fusion.39 = bf16[1,256,1024]{2,1,0:T(8,128)(2,1)} fusion(bf16[256,1024]{1,0:T(8,128)(2,1)S(1)} %collective-permute-done, bf16[256,1024]{1,0:T(8,128)(2,1)} %collective-permute-done.3, f32[256]{0:T(256)S(1)} %broadcast_multiply_fusion, f32[256]{0:T(256)S(1)} %add_rsqrt_fusion.1, bf16[256,1024]{1,0:T(8,128)(2,1)S(1)} %collective-permute-done.5, ...), kind=kLoop, calls=%fused_computation.36 | loop fusion | flops 3145728 | bytes 3672064 | tf_op jit(solution)/shard_map/broadcast_in_dim | solution.py:194
  (18 shorter events, 0.1 us)
Async XLA Ops:
  0.6 24.6 %copy-start = (bf16[1,1024,1024]{2,1,0:T(8,128)(2,1)S(1)}, bf16[1,1024,1024]{2,1,0:T(8,128)(2,1)}, u32[]{:S(2)}) copy-start(bf16[1,1024,1024]{2,1,0:T(8,128)(2,1)} %param.9) | copy-start | bytes 6291460
  0.6 12.7 %collective-permute-start = (bf16[256,1024]{1,0:T(8,128)(2,1)}, bf16[256,1024]{1,0:T(8,128)(2,1)S(1)}, u32[]{:S(2)}, u32[]{:S(2)}) collective-permute-start(bf16[256,1024]{1,0:T(8,128)(2,1)} %bitcast.41), channel_id=1, source_target_pairs={{0,64},{64,128},{128,192},{192,0},{1,65},{65,129},{129,193},{193,1... | collective-permute-start | bytes 1572872 | tf_op jit(solution)/shard_map/ppermute | solution.py:24
  0.7 24.5 %collective-permute-start.3 = (bf16[256,1024]{1,0:T(8,128)(2,1)}, bf16[256,1024]{1,0:T(8,128)(2,1)}, u32[]{:S(2)}, u32[]{:S(2)}) collective-permute-start(bf16[256,1024]{1,0:T(8,128)(2,1)} %bitcast.42), channel_id=1, source_target_pairs={{0,192},{64,0},{128,64},{192,128},{1,193},{65,1},{129,65},{193,129... | collective-permute-start | bytes 1572872 | tf_op jit(solution)/shard_map/ppermute | solution.py:24
  13.3 20.6 %collective-permute-start.2 = (bf16[256,1024]{1,0:T(8,128)(2,1)S(1)}, bf16[256,1024]{1,0:T(8,128)(2,1)S(1)}, u32[]{:S(2)}, u32[]{:S(2)}) collective-permute-start(bf16[256,1024]{1,0:T(8,128)(2,1)S(1)} %collective-permute-done), channel_id=1, source_target_pairs={{1,0},{2,1},{3,2},{4,3},{5,4},{6,5},{7,6},{8,7},{9,8},{10,9},{11,1... | collective-permute-start | bytes 1572872 | tf_op jit(solution)/shard_map/ppermute | solution.py:34
  23.1 17.5 %collective-permute-start.1 = (bf16[256,1024]{1,0:T(8,128)(2,1)S(1)}, bf16[256,1024]{1,0:T(8,128)(2,1)S(1)}, u32[]{:S(2)}, u32[]{:S(2)}) collective-permute-start(bf16[256,1024]{1,0:T(8,128)(2,1)S(1)} %collective-permute-done), channel_id=1, source_target_pairs={{0,1},{1,2},{2,3},{3,4},{4,5},{5,6},{6,7},{7,8},{8,9},{9,10},{10,1... | collective-permute-start | bytes 1572872 | tf_op jit(solution)/shard_map/ppermute | solution.py:29
  25.2 15.7 %slice-start = ((s8[6291456]{0:T(1024)(128)(4,1)}), s8[4194304]{0:T(1024)(128)(4,1)S(1)}, s32[]{:S(2)}) async-start(s8[6291456]{0:T(1024)(128)(4,1)} %bitcast.36), calls=%async_computation | async-start | bytes 8388608
  28.0 13.0 %slice-start.1 = ((s8[6291456]{0:T(1024)(128)(4,1)}), s8[2097152]{0:T(1024)(128)(4,1)S(1)}, s32[]{:S(2)}) async-start(s8[6291456]{0:T(1024)(128)(4,1)} %bitcast.36), calls=%async_computation.1 | async-start | bytes 4194304
  64.8 10.5 %copy-start.2 = (bf16[256,1024]{1,0:T(8,128)(2,1)S(1)}, bf16[256,1024]{1,0:T(8,128)(2,1)}, u32[]{:S(2)}) copy-start(bf16[256,1024]{1,0:T(8,128)(2,1)} %get-tuple-element.8) | copy-start | bytes 1572868
  64.8 10.5 %copy-start.3 = (bf16[256,1024]{1,0:T(8,128)(2,1)S(1)}, bf16[256,1024]{1,0:T(8,128)(2,1)}, u32[]{:S(2)}) copy-start(bf16[256,1024]{1,0:T(8,128)(2,1)} %get-tuple-element.9) | copy-start | bytes 1572868
  64.8 10.5 %copy-start.4 = (bf16[256,1024]{1,0:T(8,128)(2,1)S(1)}, bf16[256,1024]{1,0:T(8,128)(2,1)}, u32[]{:S(2)}) copy-start(bf16[256,1024]{1,0:T(8,128)(2,1)} %get-tuple-element.10) | copy-start | bytes 1572868
  66.2 16.7 %collective-permute-start.4 = (bf16[256,1024]{1,0:T(8,128)(2,1)S(1)}, bf16[256,1024]{1,0:T(8,128)(2,1)S(1)}, u32[]{:S(2)}, u32[]{:S(2)}) collective-permute-start(bf16[256,1024]{1,0:T(8,128)(2,1)S(1)} %get-tuple-element.12), channel_id=1, source_target_pairs={{0,1},{1,2},{2,3},{3,4},{4,5},{5,6},{6,7},{7,8},{8,9},{9,10},{10,1... | collective-permute-start | bytes 1572872 | tf_op jit(solution)/shard_map/ppermute | solution.py:29
  68.2 15.9 %collective-permute-start.5 = (bf16[256,1024]{1,0:T(8,128)(2,1)S(1)}, bf16[256,1024]{1,0:T(8,128)(2,1)S(1)}, u32[]{:S(2)}, u32[]{:S(2)}) collective-permute-start(bf16[256,1024]{1,0:T(8,128)(2,1)S(1)} %get-tuple-element.13), channel_id=1, source_target_pairs={{1,0},{2,1},{3,2},{4,3},{5,4},{6,5},{7,6},{8,7},{9,8},{10,9},{11,1... | collective-permute-start | bytes 1572872 | tf_op jit(solution)/shard_map/ppermute | solution.py:34
  75.3 4.7 %copy-start.1 = (bf16[256,1024]{1,0:T(8,128)(2,1)S(1)}, bf16[256,1024]{1,0:T(8,128)(2,1)}, u32[]{:S(2)}) copy-start(bf16[256,1024]{1,0:T(8,128)(2,1)} %get-tuple-element.7) | copy-start | bytes 1572868

commit v6 on v2

--- a/solution.py
+++ b/solution.py
@@ -32,6 +32,34 @@
 def from_right(value, axis):
     count = lax.axis_size(axis)
     return lax.ppermute(value, axis, [(i + 1, i) for i in range(count - 1)])
+
+
+def grid_permute(value, moves):
+    sections = lax.axis_size("section")
+    count = lax.axis_size("seq")
+    pairs = [
+        (s * count + q, t * count + r)
+        for s in range(0, sections, 2)
+        for q in range(count)
+        for t, r in [moves(s, q)]
+        if 0 <= r < count
+    ]
+    return lax.ppermute(value, ("section", "seq"), pairs)
+
+
+def halo_of(local, arrived, margin):
+    rows = local.shape[0]
+    if lax.axis_size("section") % 2:
+        return jnp.concatenate(
+            [from_left(arrived[rows - margin :], "seq"), from_right(arrived[:margin], "seq")], axis=0
+        )
+    left = grid_permute(local[rows - margin :], lambda s, q: (s + 1, q + 1)) + grid_permute(
+        arrived[rows - margin :], lambda s, q: (s, q + 1)
+    )
+    right = grid_permute(local[:margin], lambda s, q: (s + 1, q - 1)) + grid_permute(
+        arrived[:margin], lambda s, q: (s, q - 1)
+    )
+    return jnp.concatenate([left, right], axis=0)
 
 
 def normalize(rows):
@@ -121,9 +149,7 @@
     span_blocks = nblock + 2 * REACH
     first_block = lax.axis_index("seq") * nblock
 
-    halo_rows = jnp.concatenate(
-        [from_left(arrived[rows - margin :], "seq"), from_right(arrived[:margin], "seq")], axis=0
-    )
+    halo_rows = halo_of(activations[0], arrived, margin)
     values, factor, normed = normalize(arrived)
     projected = jnp.dot(
         normed.astype(jnp.bfloat16), weights_in, preferred_element_type=jnp.float32

time: 84.6 us -> 91.5 us (1.082)
  starting transfers between devices: 24.2 us -> 29.6 us
  other arithmetic: 4.65 us -> 7.02 us
    ppermute x0 -> x4, starting transfers between devices: none -> 17.1 us  [grid_permute(): return lax.ppermute(value, ('section', 'seq'), pairs)]
    ppermute x2 -> x1, starting transfers between devices: 16.9 us -> 7.11 us  [from_right(): return lax.ppermute(value, axis, [(i + 1, i) for i in range(count - 1)])]
    ppermute x2 -> x1, waiting for transfers between devices: 8.07 us -> 0.01 us  [from_left(): return lax.ppermute(value, axis, [(i, i + 1) for i in range(count - 1)])]
    ppermute x2, waiting for transfers between devices: 6.45 us -> 13.9 us  [shifted(): return lax.ppermute(value, axis, pairs)]
    add x0 -> x2, other arithmetic: none -> 2.36 us  [the longest x1 1.18 us: halo_of(): grid_permute(local[:margin], lambda s, q: (s + 1, q - 1))]
    ppermute x2 -> x1, starting transfers between devices: 3.97 us -> 2.05 us  [from_left(): return lax.ppermute(value, axis, [(i, i + 1) for i in range(count - 1)])]
    ppermute x2 -> x1, waiting for transfers between devices: 1.18 us -> 0.24 us  [from_right(): return lax.ppermute(value, axis, [(i + 1, i) for i in range(count - 1)])]
  transfers between devices with their start and end apart: 6 -> 8, of which waited for: 4 -> 3; matrix products, arithmetic and copies ran while one was open for 21% -> 21% of each run, Pallas kernels for 0% -> 0%
where the time goes in v6:
time: 91.5 us; the launch traced here: 91 us
  starting transfers between devices  29.6 us (32%)
  matrix products  23.9 us (26%)
  waiting for transfers between devices  14.8 us (16%)
  Pallas kernels  13.4 us (15%)
  other arithmetic  7.02 us (8%)
  local copies, waits for them, and re-layouts  1.51 us (2%)
    ppermute x4, starting transfers between devices, grid_permute(): return lax.ppermute(value, ('section', 'seq'), pairs)  17.1 us
    ppermute x2, waiting for transfers between devices, shifted(): return lax.ppermute(value, axis, pairs)  13.9 us
    pallas_call x1, Pallas kernels, attention(): pl.pallas_call(attention_kernel, grid=(heads,), in_specs=[own(0), own(hea...  13.4 us
    ppermute x1, starting transfers between devices, from_right(): return lax.ppermute(value, axis, [(i + 1, i) for i in range(count - 1)])  7.11 us
    dot_general x1, matrix products, per_device(): jnp.dot(normed.astype(jnp.bfloat16), weights_in, preferred_element_type=j...  5.97 us
    dot_general x1, matrix products, per_device(): jnp.einsum('rc,dc->rd', halo_grads, weights_kv, preferred_element_type=jn...  5.2 us
    dot_general x1, matrix products, per_device(): jnp.einsum('rc,dc->rd', own_grads, weights_in, preferred_element_type=jnp...  4.66 us
    dot_general x1, matrix products, per_device(): jnp.dot(halo_normed.astype(jnp.bfloat16), weights_kv, preferred_element_t...  3.8 us
  transfers between devices with their start and end apart: 8, of which 3 were waited for; matrix products, arithmetic and copies ran while one was open for 21% of the time, Pallas kernels for 0%

profile of v6, /device:TPU:24, one launch (start us, length us, event | category | flops | bytes accessed | tf_op | source)
XLA Modules:
  0.0 91.0 jit_solution(1885651078170988676)
XLA Ops:
  0.6 0.0 copy-start
  0.6 9.2 %collective-permute-start.3 = (bf16[256,1024]{1,0:T(8,128)(2,1)}, bf16[256,1024]{1,0:T(8,128)(2,1)}, u32[]{:S(2)}, u32[]{:S(2)}) collective-permute-start(bf16[256,1024]{1,0:T(8,128)(2,1)} %bitcast.41), channel_id=1, source_target_pairs={{1,64},{2,65},{3,66},{4,67},{5,68},{6,69},{7,70},{8,71},{9,72},{10... | collective-permute-start | bytes 1572872 | tf_op jit(solution)/shard_map/ppermute | solution.py:47
  9.9 2.1 %collective-permute-start.1 = (bf16[256,1024]{1,0:T(8,128)(2,1)}, bf16[256,1024]{1,0:T(8,128)(2,1)}, u32[]{:S(2)}, u32[]{:S(2)}) collective-permute-start(bf16[256,1024]{1,0:T(8,128)(2,1)} %bitcast.42), channel_id=1, source_target_pairs={{0,65},{1,66},{2,67},{3,68},{4,69},{5,70},{6,71},{7,72},{8,73},{9,... | collective-permute-start | bytes 1572872 | tf_op jit(solution)/shard_map/ppermute | solution.py:47
  12.0 3.2 %collective-permute-start.5 = (bf16[256,1024]{1,0:T(8,128)(2,1)}, bf16[256,1024]{1,0:T(8,128)(2,1)}, u32[]{:S(2)}, u32[]{:S(2)}) collective-permute-start(bf16[256,1024]{1,0:T(8,128)(2,1)} %bitcast.40), channel_id=1, source_target_pairs={{0,192},{64,0},{128,64},{192,128},{1,193},{65,1},{129,65},{193,129... | collective-permute-start | bytes 1572872 | tf_op jit(solution)/shard_map/ppermute | solution.py:24
  15.2 0.7 iota_compare_fusion.1
  15.9 0.7 subtract_add_fusion
  16.6 0.1 fusion.53
  16.7 0.1 copy.9
  16.8 0.1 broadcast_bitcast_fusion
  16.9 0.1 broadcast_in_dim.31
  17.0 1.2 %copy.10.live_ref = f32[256,768]{1,0:T(8,128)} copy(f32[256,768]{0,1:T(8,128)S(1)} %bitcast.34) | data formatting | bytes 1572864 | tf_op jit(solution)/shard_map/jit(_where)/select_n | solution.py:172
  18.1 13.9 %collective-permute-done = bf16[256,1024]{1,0:T(8,128)(2,1)S(1)} collective-permute-done((bf16[256,1024]{1,0:T(8,128)(2,1)}, bf16[256,1024]{1,0:T(8,128)(2,1)S(1)}, u32[]{:S(2)}, u32[]{:S(2)}) %collective-permute-start) | collective-permute-done | bytes 524320 | tf_op jit(solution)/shard_map/ppermute | solution.py:24
  32.0 2.5 %collective-permute-start.4 = (bf16[256,1024]{1,0:T(8,128)(2,1)S(1)}, bf16[256,1024]{1,0:T(8,128)(2,1)S(1)}, u32[]{:S(2)}, u32[]{:S(2)}) collective-permute-start(bf16[256,1024]{1,0:T(8,128)(2,1)S(1)} %collective-permute-done), channel_id=1, source_target_pairs={{1,0},{2,1},{3,2},{4,3},{5,4},{6,5},{7,6},{8,7},{9,8},{10,9},{11,1... | collective-permute-start | bytes 1572872 | tf_op jit(solution)/shard_map/ppermute | solution.py:47
  34.5 3.3 %collective-permute-start.2 = (bf16[256,1024]{1,0:T(8,128)(2,1)S(1)}, bf16[256,1024]{1,0:T(8,128)(2,1)S(1)}, u32[]{:S(2)}, u32[]{:S(2)}) collective-permute-start(bf16[256,1024]{1,0:T(8,128)(2,1)S(1)} %collective-permute-done), channel_id=1, source_target_pairs={{0,1},{1,2},{2,3},{3,4},{4,5},{5,6},{6,7},{7,8},{8,9},{9,10},{10,1... | collective-permute-start | bytes 1572872 | tf_op jit(solution)/shard_map/ppermute | solution.py:47
  37.9 0.2 fusion.46
  38.1 2.7 %fusion.35.do_ref = bf16[256,1024]{1,0:T(8,128)(2,1)} fusion(bf16[256,1024]{1,0:T(8,128)(2,1)} %collective-permute-done.5, bf16[1,1024,1024]{2,1,0:T(8,128)(2,1)S(1)} %copy-done), kind=kOutput, calls=%fused_computation.31 | convolution fusion | flops 537133056 | bytes 3145728 | tf_op jit(solution)/shard_map/rd,wd->rw/dot_general | solution.py:157
  40.8 6.0 %convolution_convert_fusion.q_ref.ko_ref.vo_ref = bf16[256,3072]{1,0:T(8,128)(2,1)} fusion(bf16[256,1024]{1,0:T(8,128)(2,1)S(1)} %collective-permute-done, f32[256]{0:T(256)S(1)} %add_rsqrt_fusion.1, bf16[1,1024,3072]{2,1,0:T(8,128)(2,1)} %param.8), kind=kOutput, calls=%fused_computation | convolution fusion | flops 1612185600 | bytes 8389632 | tf_op jit(solution)/shard_map/dot_general | solution.py:154
  46.8 1.2 %add.46 = bf16[256,1024]{1,0:T(8,128)(2,1)S(1)} add(bf16[256,1024]{1,0:T(8,128)(2,1)} %collective-permute-done.3, bf16[256,1024]{1,0:T(8,128)(2,1)S(1)} %collective-permute-done.4) | non-fusion elementwise | flops 262144 | bytes 1572864 | tf_op jit(solution)/shard_map/add | solution.py:59
  48.0 0.6 collective-permute-done.2
  48.6 1.2 %add.45 = bf16[256,1024]{1,0:T(8,128)(2,1)S(1)} add(bf16[256,1024]{1,0:T(8,128)(2,1)} %collective-permute-done.1, bf16[256,1024]{1,0:T(8,128)(2,1)S(1)} %collective-permute-done.2) | non-fusion elementwise | flops 262144 | bytes 1572864 | tf_op jit(solution)/shard_map/add | solution.py:56
  49.8 0.3 fusion.7
  50.1 3.8 %fusion.4.kh_ref.vh_ref = bf16[512,2048]{1,0:T(8,128)(2,1)} fusion(bf16[1024,3072]{1,0:T(8,128)(2,1)S(1)} %bitcast.39, f32[512]{0:T(512)S(1)} %add_rsqrt_fusion, bf16[256,1024]{1,0:T(8,128)(2,1)S(1)} %add.46, bf16[256,1024]{1,0:T(8,128)(2,1)S(1)} %add.45), kind=kOutput, calls=%fused_computation.5 | convolution fusion | flops 2151677952 | bytes 7342080 | tf_op jit(solution)/shard_map/dot_general | solution.py:162
  53.9 13.4 %shard_map.77 = (bf16[256,1024]{1,0:T(8,128)(2,1)}, bf16[256,1024]{1,0:T(8,128)(2,1)}, bf16[256,1024]{1,0:T(8,128)(2,1)}, bf16[256,1024]{1,0:T(8,128)(2,1)}, bf1...) custom-call(bf16[256,3072]{1,0:T(8,128)(2,1)} %convolution_convert_fusion.q_ref.ko_ref.vo_ref, ...), custom_call_target="tpu_custom_call" | custom-call | flops 2013265920 | bytes 9175040 | tf_op jit(solution)/shard_map/pallas_call | solution.py:117
  67.4 5.2 %fusion.22 = bf16[512,1024]{1,0:T(8,128)(2,1)S(1)} fusion(bf16[1024,3072]{1,0:T(8,128)(2,1)} %bitcast.36, bf16[512,1024]{1,0:T(8,128)(2,1)} %get-tuple-element.13, bf16[512,1024]{1,0:T(8,128)(2,1)} %get-tuple-element.12), kind=kOutput, calls=%fused_computation.26 | convolution fusion | flops 2152202240 | bytes 7340032 | tf_op jit(solution)/shard_map/rc,dc->rd/dot_general | solution.py:182
  72.6 0.1 fusion.59
  72.7 2.1 %collective-permute-start.6 = (bf16[256,1024]{1,0:T(8,128)(2,1)S(1)}, bf16[256,1024]{1,0:T(8,128)(2,1)S(1)}, u32[]{:S(2)}, u32[]{:S(2)}) collective-permute-start(bf16[256,1024]{1,0:T(8,128)(2,1)S(1)} %get-tuple-element.14), channel_id=1, source_target_pairs={{0,1},{1,2},{2,3},{3,4},{4,5},{5,6},{6,7},{7,8},{8,9},{9,10},{10,1... | collective-permute-start | bytes 1572872 | tf_op jit(solution)/shard_map/ppermute | solution.py:29
  74.7 7.1 %collective-permute-start.7 = (bf16[256,1024]{1,0:T(8,128)(2,1)S(1)}, bf16[256,1024]{1,0:T(8,128)(2,1)S(1)}, u32[]{:S(2)}, u32[]{:S(2)}) collective-permute-start(bf16[256,1024]{1,0:T(8,128)(2,1)S(1)} %get-tuple-element.15), channel_id=1, source_target_pairs={{1,0},{2,1},{3,2},{4,3},{5,4},{6,5},{7,6},{8,7},{9,8},{10,9},{11,1... | collective-permute-start | bytes 1572872 | tf_op jit(solution)/shard_map/ppermute | solution.py:34
  81.9 4.7 %fusion.16 = f32[256,1024]{1,0:T(8,128)S(1)} fusion(bf16[256,1024]{1,0:T(8,128)(2,1)S(1)} %copy-done.4, bf16[256,1024]{1,0:T(8,128)(2,1)S(1)} %copy-done.3, bf16[256,1024]{1,0:T(8,128)(2,1)S(1)} %copy-done.2, bf16[1,1024,3072]{2,1,0:T(8,128)(2,1)} %param.8), kind=kOutput, calls=%fused_computation.17 | convolution fusion | flops 1615331328 | bytes 8912896 | tf_op jit(solution)/shard_map/rc,dc->rd/dot_general | solution.py:189
  86.6 1.5 %fusion.38 = bf16[1,256,1024]{2,1,0:T(8,128)(2,1)} fusion(bf16[256,1024]{1,0:T(8,128)(2,1)S(1)} %copy-done.1, bf16[1,1024,1024]{2,1,0:T(8,128)(2,1)S(1)} %copy-done, bf16[256,1024]{1,0:T(8,128)(2,1)S(1)} %collective-permute-done), kind=kOutput, calls=%fused_computation.32 | convolution fusion | flops 537657344 | bytes 3670016 | tf_op jit(solution)/shard_map/dot_general | solution.py:177
  88.1 0.2 collective-permute-done.7
  88.3 0.4 fusion.41
  88.7 2.3 %fusion.49 = bf16[1,256,1024]{2,1,0:T(8,128)(2,1)} fusion(bf16[256,1024]{1,0:T(8,128)(2,1)S(1)} %collective-permute-done, bf16[256,1024]{1,0:T(8,128)(2,1)} %collective-permute-done.5, f32[256]{0:T(256)S(1)} %broadcast_multiply_fusion, f32[256]{0:T(256)S(1)} %add_rsqrt_fusion.1, bf16[256,1024]{1,0:T(8,128)(2,1)S(1)} %collective-permute-done.7, ...), kind=kLoop, calls=%fused_computation.42 | loop fusion | flops 3145728 | bytes 3672064 | tf_op jit(solution)/shard_map/broadcast_in_dim | solution.py:197
  (25 shorter events, 0.1 us)
Async XLA Ops:
  0.6 37.4 %copy-start = (bf16[1,1024,1024]{2,1,0:T(8,128)(2,1)S(1)}, bf16[1,1024,1024]{2,1,0:T(8,128)(2,1)}, u32[]{:S(2)}) copy-start(bf16[1,1024,1024]{2,1,0:T(8,128)(2,1)} %param.9) | copy-start | bytes 6291460
  0.6 46.1 %collective-permute-start.3 = (bf16[256,1024]{1,0:T(8,128)(2,1)}, bf16[256,1024]{1,0:T(8,128)(2,1)}, u32[]{:S(2)}, u32[]{:S(2)}) collective-permute-start(bf16[256,1024]{1,0:T(8,128)(2,1)} %bitcast.41), channel_id=1, source_target_pairs={{1,64},{2,65},{3,66},{4,67},{5,68},{6,69},{7,70},{8,71},{9,72},{10... | collective-permute-start | bytes 1572872 | tf_op jit(solution)/shard_map/ppermute | solution.py:47
  9.9 38.1 %collective-permute-start.1 = (bf16[256,1024]{1,0:T(8,128)(2,1)}, bf16[256,1024]{1,0:T(8,128)(2,1)}, u32[]{:S(2)}, u32[]{:S(2)}) collective-permute-start(bf16[256,1024]{1,0:T(8,128)(2,1)} %bitcast.42), channel_id=1, source_target_pairs={{0,65},{1,66},{2,67},{3,68},{4,69},{5,70},{6,71},{7,72},{8,73},{9,... | collective-permute-start | bytes 1572872 | tf_op jit(solution)/shard_map/ppermute | solution.py:47
  12.0 20.1 %collective-permute-start = (bf16[256,1024]{1,0:T(8,128)(2,1)}, bf16[256,1024]{1,0:T(8,128)(2,1)S(1)}, u32[]{:S(2)}, u32[]{:S(2)}) collective-permute-start(bf16[256,1024]{1,0:T(8,128)(2,1)} %bitcast.43), channel_id=1, source_target_pairs={{0,64},{64,128},{128,192},{192,0},{1,65},{65,129},{129,193},{193,1... | collective-permute-start | bytes 1572872 | tf_op jit(solution)/shard_map/ppermute | solution.py:24
  12.0 26.1 %collective-permute-start.5 = (bf16[256,1024]{1,0:T(8,128)(2,1)}, bf16[256,1024]{1,0:T(8,128)(2,1)}, u32[]{:S(2)}, u32[]{:S(2)}) collective-permute-start(bf16[256,1024]{1,0:T(8,128)(2,1)} %bitcast.40), channel_id=1, source_target_pairs={{0,192},{64,0},{128,64},{192,128},{1,193},{65,1},{129,65},{193,129... | collective-permute-start | bytes 1572872 | tf_op jit(solution)/shard_map/ppermute | solution.py:24
  32.0 14.8 %collective-permute-start.4 = (bf16[256,1024]{1,0:T(8,128)(2,1)S(1)}, bf16[256,1024]{1,0:T(8,128)(2,1)S(1)}, u32[]{:S(2)}, u32[]{:S(2)}) collective-permute-start(bf16[256,1024]{1,0:T(8,128)(2,1)S(1)} %collective-permute-done), channel_id=1, source_target_pairs={{1,0},{2,1},{3,2},{4,3},{5,4},{6,5},{7,6},{8,7},{9,8},{10,9},{11,1... | collective-permute-start | bytes 1572872 | tf_op jit(solution)/shard_map/ppermute | solution.py:47
  34.5 14.1 %collective-permute-start.2 = (bf16[256,1024]{1,0:T(8,128)(2,1)S(1)}, bf16[256,1024]{1,0:T(8,128)(2,1)S(1)}, u32[]{:S(2)}, u32[]{:S(2)}) collective-permute-start(bf16[256,1024]{1,0:T(8,128)(2,1)S(1)} %collective-permute-done), channel_id=1, source_target_pairs={{0,1},{1,2},{2,3},{3,4},{4,5},{5,6},{6,7},{7,8},{8,9},{9,10},{10,1... | collective-permute-start | bytes 1572872 | tf_op jit(solution)/shard_map/ppermute | solution.py:47
  38.1 12.0 %slice-start = ((s8[6291456]{0:T(1024)(128)(4,1)}), s8[4194304]{0:T(1024)(128)(4,1)S(1)}, s32[]{:S(2)}) async-start(s8[6291456]{0:T(1024)(128)(4,1)} %bitcast.37), calls=%async_computation | async-start | bytes 8388608
  40.8 9.3 %slice-start.1 = ((s8[6291456]{0:T(1024)(128)(4,1)}), s8[2097152]{0:T(1024)(128)(4,1)S(1)}, s32[]{:S(2)}) async-start(s8[6291456]{0:T(1024)(128)(4,1)} %bitcast.37), calls=%async_computation.1 | async-start | bytes 4194304
  72.6 9.3 %copy-start.2 = (bf16[256,1024]{1,0:T(8,128)(2,1)S(1)}, bf16[256,1024]{1,0:T(8,128)(2,1)}, u32[]{:S(2)}) copy-start(bf16[256,1024]{1,0:T(8,128)(2,1)} %get-tuple-element.9) | copy-start | bytes 1572868
  72.6 9.3 %copy-start.3 = (bf16[256,1024]{1,0:T(8,128)(2,1)S(1)}, bf16[256,1024]{1,0:T(8,128)(2,1)}, u32[]{:S(2)}) copy-start(bf16[256,1024]{1,0:T(8,128)(2,1)} %get-tuple-element.10) | copy-start | bytes 1572868
  72.6 9.3 %copy-start.4 = (bf16[256,1024]{1,0:T(8,128)(2,1)S(1)}, bf16[256,1024]{1,0:T(8,128)(2,1)}, u32[]{:S(2)}) copy-start(bf16[256,1024]{1,0:T(8,128)(2,1)} %get-tuple-element.11) | copy-start | bytes 1572868
  72.7 15.4 %collective-permute-start.6 = (bf16[256,1024]{1,0:T(8,128)(2,1)S(1)}, bf16[256,1024]{1,0:T(8,128)(2,1)S(1)}, u32[]{:S(2)}, u32[]{:S(2)}) collective-permute-start(bf16[256,1024]{1,0:T(8,128)(2,1)S(1)} %get-tuple-element.14), channel_id=1, source_target_pairs={{0,1},{1,2},{2,3},{3,4},{4,5},{5,6},{6,7},{7,8},{8,9},{9,10},{10,1... | collective-permute-start | bytes 1572872 | tf_op jit(solution)/shard_map/ppermute | solution.py:29
  74.7 13.6 %collective-permute-start.7 = (bf16[256,1024]{1,0:T(8,128)(2,1)S(1)}, bf16[256,1024]{1,0:T(8,128)(2,1)S(1)}, u32[]{:S(2)}, u32[]{:S(2)}) collective-permute-start(bf16[256,1024]{1,0:T(8,128)(2,1)S(1)} %get-tuple-element.15), channel_id=1, source_target_pairs={{1,0},{2,1},{3,2},{4,3},{5,4},{6,5},{7,6},{8,7},{9,8},{10,9},{11,1... | collective-permute-start | bytes 1572872 | tf_op jit(solution)/shard_map/ppermute | solution.py:34
  81.9 4.7 %copy-start.1 = (bf16[256,1024]{1,0:T(8,128)(2,1)S(1)}, bf16[256,1024]{1,0:T(8,128)(2,1)}, u32[]{:S(2)}) copy-start(bf16[256,1024]{1,0:T(8,128)(2,1)} %get-tuple-element.8) | copy-start | bytes 1572868

commit v7 on v2

--- a/solution.py
+++ b/solution.py
@@ -152,12 +152,23 @@
         jnp.bfloat16
     )
 
-    halo_grads = jnp.concatenate([halo_key_grad, halo_value_grad], axis=1)
-    halo_normed_grad = jnp.einsum(
-        "rc,dc->rd", halo_grads, weights_kv, preferred_element_type=jnp.float32
+    to_right = jnp.einsum(
+        "rc,dc->rd",
+        jnp.concatenate([halo_key_grad[margin:], halo_value_grad[margin:]], axis=1),
+        weights_kv,
+        preferred_element_type=jnp.float32,
     ).astype(jnp.bfloat16)
-    head_part = from_left(halo_normed_grad[margin:], "seq")
-    tail_part = from_right(halo_normed_grad[:margin], "seq")
+    head_part = from_left(to_right, "seq")
+    to_right, halo_key_grad, halo_value_grad = lax.optimization_barrier(
+        (to_right, halo_key_grad, halo_value_grad)
+    )
+    to_left = jnp.einsum(
+        "rc,dc->rd",
+        jnp.concatenate([halo_key_grad[:margin], halo_value_grad[:margin]], axis=1),
+        weights_kv,
+        preferred_element_type=jnp.float32,
+    ).astype(jnp.bfloat16)
+    tail_part = from_right(to_left, "seq")
     own_grads = jnp.concatenate([query_grad, key_grad, value_grad], axis=1)
     normed_grad = lax.optimization_barrier(
         jnp.einsum("rc,dc->rd", own_grads, weights_in, preferred_element_type=jnp.float32)

time: 84.6 us -> 86.8 us (1.026)
  matrix products: 23.8 us -> 20.8 us
  waiting for transfers between devices: 15.7 us -> 18.5 us
  local copies, waits for them, and re-layouts: 1.51 us -> 4.03 us
    ppermute x2, waiting for transfers between devices: 1.18 us -> 5.4 us  [from_right(): return lax.ppermute(value, axis, [(i + 1, i) for i in range(count - 1)])]
    dot_general x1, matrix products: 4.66 us -> 1.82 us  [per_device(): jnp.einsum('rc,dc->rd', own_grads, weights_in, preferred_element_type=jnp...]
    slice x1 -> x4, local copies, waits for them, and re-layouts: 0.07 us -> 2.55 us  [the longest x1 1.25 us: per_device(): halo_value_grad[margin:]]
    ppermute x2, waiting for transfers between devices: 8.07 us -> 6.65 us  [from_left(): return lax.ppermute(value, axis, [(i, i + 1) for i in range(count - 1)])]
    dot_general x1 -> x2, matrix products: 5.2 us -> 4.91 us  [the longest x1 3.62 us: per_device(): jnp.einsum('rc,dc->rd', jnp.concatenate([halo_key_grad[margin:], halo_val...]
  transfers between devices with their start and end apart: 6 -> 6, of which waited for: 4 -> 3; matrix products, arithmetic and copies ran while one was open for 21% -> 19% of each run, Pallas kernels for 0% -> 0%
where the time goes in v7:
time: 86.8 us; the launch traced here: 86.3 us
  starting transfers between devices  24 us (28%)
  matrix products  20.8 us (24%)
  waiting for transfers between devices  18.5 us (21%)
  Pallas kernels  13.4 us (15%)
  other arithmetic  4.66 us (5%)
  local copies, waits for them, and re-layouts  4.03 us (5%)
  between operations  0.93 us (1%)
    ppermute x2, starting transfers between devices, from_right(): return lax.ppermute(value, axis, [(i + 1, i) for i in range(count - 1)])  16.9 us
    pallas_call x1, Pallas kernels, attention(): pl.pallas_call(attention_kernel, grid=(heads,), in_specs=[own(0), own(hea...  13.4 us
    ppermute x2, waiting for transfers between devices, from_left(): return lax.ppermute(value, axis, [(i, i + 1) for i in range(count - 1)])  6.65 us
    ppermute x2, waiting for transfers between devices, shifted(): return lax.ppermute(value, axis, pairs)  6.44 us
    dot_general x1, matrix products, per_device(): jnp.dot(normed.astype(jnp.bfloat16), weights_in, preferred_element_type=j...  5.99 us
    ppermute x2, waiting for transfers between devices, from_right(): return lax.ppermute(value, axis, [(i + 1, i) for i in range(count - 1)])  5.4 us
    ppermute x2, starting transfers between devices, from_left(): return lax.ppermute(value, axis, [(i, i + 1) for i in range(count - 1)])  3.84 us
    dot_general x1, matrix products, per_device(): jnp.dot(halo_normed.astype(jnp.bfloat16), weights_kv, preferred_element_t...  3.79 us
  transfers between devices with their start and end apart: 6, of which 3 were waited for; matrix products, arithmetic and copies ran while one was open for 19% of the time, Pallas kernels for 0%

profile of v7, /device:TPU:24, one launch (start us, length us, event | category | flops | bytes accessed | tf_op | source)
XLA Modules:
  0.0 86.3 jit_solution(13351103967267812061)
XLA Ops:
  0.6 0.0 copy-start
  0.6 0.1 collective-permute-start
  0.7 3.2 %collective-permute-start.3 = (bf16[256,1024]{1,0:T(8,128)(2,1)}, bf16[256,1024]{1,0:T(8,128)(2,1)}, u32[]{:S(2)}, u32[]{:S(2)}) collective-permute-start(bf16[256,1024]{1,0:T(8,128)(2,1)} %bitcast.44), channel_id=1, source_target_pairs={{0,192},{64,0},{128,64},{192,128},{1,193},{65,1},{129,65},{193,129... | collective-permute-start | bytes 1572872 | tf_op jit(solution)/shard_map/ppermute | solution.py:24
  4.0 0.7 iota_compare_fusion.1
  4.7 0.7 subtract_add_fusion
  5.4 0.1 fusion.59
  5.5 0.1 copy.9
  5.6 0.1 broadcast_bitcast_fusion
  5.7 0.1 broadcast_in_dim.31
  5.7 1.2 %copy.10.live_ref = f32[256,768]{1,0:T(8,128)} copy(f32[256,768]{0,1:T(8,128)S(1)} %bitcast.34) | data formatting | bytes 1572864 | tf_op jit(solution)/shard_map/jit(_where)/select_n | solution.py:146
  6.9 6.4 %collective-permute-done = bf16[256,1024]{1,0:T(8,128)(2,1)S(1)} collective-permute-done((bf16[256,1024]{1,0:T(8,128)(2,1)}, bf16[256,1024]{1,0:T(8,128)(2,1)S(1)}, u32[]{:S(2)}, u32[]{:S(2)}) %collective-permute-start) | collective-permute-done | bytes 524320 | tf_op jit(solution)/shard_map/ppermute | solution.py:24
  13.3 9.8 %collective-permute-start.2 = (bf16[256,1024]{1,0:T(8,128)(2,1)S(1)}, bf16[256,1024]{1,0:T(8,128)(2,1)S(1)}, u32[]{:S(2)}, u32[]{:S(2)}) collective-permute-start(bf16[256,1024]{1,0:T(8,128)(2,1)S(1)} %collective-permute-done), channel_id=1, source_target_pairs={{1,0},{2,1},{3,2},{4,3},{5,4},{6,5},{7,6},{8,7},{9,8},{10,9},{11,1... | collective-permute-start | bytes 1572872 | tf_op jit(solution)/shard_map/ppermute | solution.py:34
  23.1 1.9 %collective-permute-start.1 = (bf16[256,1024]{1,0:T(8,128)(2,1)S(1)}, bf16[256,1024]{1,0:T(8,128)(2,1)S(1)}, u32[]{:S(2)}, u32[]{:S(2)}) collective-permute-start(bf16[256,1024]{1,0:T(8,128)(2,1)S(1)} %collective-permute-done), channel_id=1, source_target_pairs={{0,1},{1,2},{2,3},{3,4},{4,5},{5,6},{6,7},{7,8},{8,9},{9,10},{10,1... | collective-permute-start | bytes 1572872 | tf_op jit(solution)/shard_map/ppermute | solution.py:29
  25.0 0.2 fusion.46
  25.3 2.7 %fusion.29.do_ref = bf16[256,1024]{1,0:T(8,128)(2,1)} fusion(bf16[256,1024]{1,0:T(8,128)(2,1)} %collective-permute-done.3, bf16[1,1024,1024]{2,1,0:T(8,128)(2,1)S(1)} %copy-done), kind=kOutput, calls=%fused_computation.29 | convolution fusion | flops 537133056 | bytes 3145728 | tf_op jit(solution)/shard_map/rd,wd->rw/dot_general | solution.py:131
  28.0 6.0 %convolution_convert_fusion.q_ref.ko_ref.vo_ref = bf16[256,3072]{1,0:T(8,128)(2,1)} fusion(bf16[256,1024]{1,0:T(8,128)(2,1)S(1)} %collective-permute-done, f32[256]{0:T(256)S(1)} %add_rsqrt_fusion.1, bf16[1,1024,3072]{2,1,0:T(8,128)(2,1)} %param.8), kind=kOutput, calls=%fused_computation | convolution fusion | flops 1612185600 | bytes 8389632 | tf_op jit(solution)/shard_map/dot_general | solution.py:128
  34.0 6.6 %collective-permute-done.1 = bf16[256,1024]{1,0:T(8,128)(2,1)S(1)} collective-permute-done((bf16[256,1024]{1,0:T(8,128)(2,1)S(1)}, bf16[256,1024]{1,0:T(8,128)(2,1)S(1)}, u32[]{:S(2)}, u32[]{:S(2)}) %collective-permute-start.1) | collective-permute-done | bytes 524320 | tf_op jit(solution)/shard_map/ppermute | solution.py:29
  40.6 0.3 fusion.9
  41.0 3.8 %fusion.6.kh_ref.vh_ref = bf16[512,2048]{1,0:T(8,128)(2,1)} fusion(bf16[1024,3072]{1,0:T(8,128)(2,1)S(1)} %bitcast.39, f32[512]{0:T(512)S(1)} %add_rsqrt_fusion, bf16[256,1024]{1,0:T(8,128)(2,1)S(1)} %collective-permute-done.2, bf16[256,1024]{1,0:T(8,128)(2,1)S(1)} %collective-permute-done.1), kind=kOutput, calls=%fused_computation.7 | convolution fusion | flops 2151677952 | bytes 7342080 | tf_op jit(solution)/shard_map/dot_general | solution.py:136
  44.8 13.4 %shard_map.77 = (bf16[256,1024]{1,0:T(8,128)(2,1)}, bf16[256,1024]{1,0:T(8,128)(2,1)}, bf16[256,1024]{1,0:T(8,128)(2,1)}, bf16[256,1024]{1,0:T(8,128)(2,1)}, bf1...) custom-call(bf16[256,3072]{1,0:T(8,128)(2,1)} %convolution_convert_fusion.q_ref.ko_ref.vo_ref, ...), custom_call_target="tpu_custom_call" | custom-call | flops 2013265920 | bytes 9175040 | tf_op jit(solution)/shard_map/pallas_call | solution.py:89
  58.2 1.2 %slice.16 = bf16[256,1024]{1,0:T(8,128)(2,1)S(1)} slice(bf16[512,1024]{1,0:T(8,128)(2,1)} %get-tuple-element.16), slice={[256:512], [0:1024]} | slice | bytes 1048576 | tf_op jit(solution)/shard_map/slice | solution.py:157
  59.4 1.3 %slice.17 = bf16[256,1024]{1,0:T(8,128)(2,1)S(1)} slice(bf16[512,1024]{1,0:T(8,128)(2,1)} %get-tuple-element.17), slice={[256:512], [0:1024]} | slice | bytes 1048576 | tf_op jit(solution)/shard_map/slice | solution.py:157
  60.7 0.0 slice-start.3
  60.7 3.6 %fusion.32 = bf16[256,1024]{1,0:T(8,128)(2,1)S(1)} fusion(bf16[1024,3072]{1,0:T(8,128)(2,1)} %bitcast.36, bf16[256,1024]{1,0:T(8,128)(2,1)S(1)} %slice.17, bf16[256,1024]{1,0:T(8,128)(2,1)S(1)} %slice.16), kind=kOutput, calls=%fused_computation.30 | convolution fusion | flops 1076101120 | bytes 5767168 | tf_op jit(solution)/shard_map/rc,dc->rd/dot_general | solution.py:155
  64.3 1.9 %collective-permute-start.4 = (bf16[256,1024]{1,0:T(8,128)(2,1)S(1)}, bf16[256,1024]{1,0:T(8,128)(2,1)S(1)}, u32[]{:S(2)}, u32[]{:S(2)}) collective-permute-start(bf16[256,1024]{1,0:T(8,128)(2,1)S(1)} %fusion.32), channel_id=1, source_target_pairs={{0,1},{1,2},{2,3},{3,4},{4,5},{5,6},{6,7},{7,8},{8,9},{9,10},{10,1... | collective-permute-start | bytes 1572872 | tf_op jit(solution)/shard_map/ppermute | solution.py:29
  66.4 1.3 %fusion.35 = bf16[256,1024]{1,0:T(8,128)(2,1)S(1)} fusion(bf16[1024,3072]{1,0:T(8,128)(2,1)S(1)} %bitcast.42, bf16[256,1024]{1,0:T(8,128)(2,1)S(1)} %slice.19, bf16[256,1024]{1,0:T(8,128)(2,1)S(1)} %slice.18), kind=kOutput, calls=%fused_computation.31 | convolution fusion | flops 1076101120 | bytes 5767168 | tf_op jit(solution)/shard_map/rc,dc->rd/dot_general | solution.py:165
  67.7 7.1 %collective-permute-start.5 = (bf16[256,1024]{1,0:T(8,128)(2,1)S(1)}, bf16[256,1024]{1,0:T(8,128)(2,1)S(1)}, u32[]{:S(2)}, u32[]{:S(2)}) collective-permute-start(bf16[256,1024]{1,0:T(8,128)(2,1)S(1)} %fusion.35), channel_id=1, source_target_pairs={{1,0},{2,1},{3,2},{4,3},{5,4},{6,5},{7,6},{8,7},{9,8},{10,9},{11,1... | collective-permute-start | bytes 1572872 | tf_op jit(solution)/shard_map/ppermute | solution.py:34
  74.9 1.8 %fusion.15 = f32[256,1024]{1,0:T(8,128)S(1)} fusion(bf16[256,1024]{1,0:T(8,128)(2,1)S(1)} %copy-done.6, bf16[256,1024]{1,0:T(8,128)(2,1)S(1)} %copy-done.5, bf16[256,1024]{1,0:T(8,128)(2,1)S(1)} %copy-done.4, bf16[1,1024,3072]{2,1,0:T(8,128)(2,1)S(1)} %bitcast.41), kind=kOutput, calls=%fused_computation.16 | convolution fusion | flops 1615331328 | bytes 8912896 | tf_op jit(solution)/shard_map/rc,dc->rd/dot_general | solution.py:174
  76.7 1.5 %fusion.38 = bf16[1,256,1024]{2,1,0:T(8,128)(2,1)} fusion(bf16[256,1024]{1,0:T(8,128)(2,1)S(1)} %copy-done.3, bf16[1,1024,1024]{2,1,0:T(8,128)(2,1)S(1)} %copy-done, bf16[256,1024]{1,0:T(8,128)(2,1)S(1)} %collective-permute-done), kind=kOutput, calls=%fused_computation.32 | convolution fusion | flops 537657344 | bytes 3670016 | tf_op jit(solution)/shard_map/dot_general | solution.py:151
  78.3 5.4 %collective-permute-done.5 = bf16[256,1024]{1,0:T(8,128)(2,1)S(1)} collective-permute-done((bf16[256,1024]{1,0:T(8,128)(2,1)S(1)}, bf16[256,1024]{1,0:T(8,128)(2,1)S(1)}, u32[]{:S(2)}, u32[]{:S(2)}) %collective-permute-start.5) | collective-permute-done | bytes 524320 | tf_op jit(solution)/shard_map/ppermute | solution.py:34
  83.7 0.4 fusion.41
  84.0 2.3 %fusion.55 = bf16[1,256,1024]{2,1,0:T(8,128)(2,1)} fusion(bf16[256,1024]{1,0:T(8,128)(2,1)S(1)} %collective-permute-done, bf16[256,1024]{1,0:T(8,128)(2,1)} %collective-permute-done.3, f32[256]{0:T(256)S(1)} %broadcast_multiply_fusion, f32[256]{0:T(256)S(1)} %add_rsqrt_fusion.1, bf16[256,1024]{1,0:T(8,128)(2,1)S(1)} %collective-permute-done.5, ...), kind=kLoop, calls=%fused_computation.48 | loop fusion | flops 3145728 | bytes 3672064 | tf_op jit(solution)/shard_map/broadcast_in_dim | solution.py:182
  (32 shorter events, 0.2 us)
Async XLA Ops:
  0.6 24.6 %copy-start = (bf16[1,1024,1024]{2,1,0:T(8,128)(2,1)S(1)}, bf16[1,1024,1024]{2,1,0:T(8,128)(2,1)}, u32[]{:S(2)}) copy-start(bf16[1,1024,1024]{2,1,0:T(8,128)(2,1)} %param.9) | copy-start | bytes 6291460
  0.6 12.7 %collective-permute-start = (bf16[256,1024]{1,0:T(8,128)(2,1)}, bf16[256,1024]{1,0:T(8,128)(2,1)S(1)}, u32[]{:S(2)}, u32[]{:S(2)}) collective-permute-start(bf16[256,1024]{1,0:T(8,128)(2,1)} %bitcast.43), channel_id=1, source_target_pairs={{0,64},{64,128},{128,192},{192,0},{1,65},{65,129},{129,193},{193,1... | collective-permute-start | bytes 1572872 | tf_op jit(solution)/shard_map/ppermute | solution.py:24
  0.7 24.5 %collective-permute-start.3 = (bf16[256,1024]{1,0:T(8,128)(2,1)}, bf16[256,1024]{1,0:T(8,128)(2,1)}, u32[]{:S(2)}, u32[]{:S(2)}) collective-permute-start(bf16[256,1024]{1,0:T(8,128)(2,1)} %bitcast.44), channel_id=1, source_target_pairs={{0,192},{64,0},{128,64},{192,128},{1,193},{65,1},{129,65},{193,129... | collective-permute-start | bytes 1572872 | tf_op jit(solution)/shard_map/ppermute | solution.py:24
  13.3 20.7 %collective-permute-start.2 = (bf16[256,1024]{1,0:T(8,128)(2,1)S(1)}, bf16[256,1024]{1,0:T(8,128)(2,1)S(1)}, u32[]{:S(2)}, u32[]{:S(2)}) collective-permute-start(bf16[256,1024]{1,0:T(8,128)(2,1)S(1)} %collective-permute-done), channel_id=1, source_target_pairs={{1,0},{2,1},{3,2},{4,3},{5,4},{6,5},{7,6},{8,7},{9,8},{10,9},{11,1... | collective-permute-start | bytes 1572872 | tf_op jit(solution)/shard_map/ppermute | solution.py:34
  23.1 17.5 %collective-permute-start.1 = (bf16[256,1024]{1,0:T(8,128)(2,1)S(1)}, bf16[256,1024]{1,0:T(8,128)(2,1)S(1)}, u32[]{:S(2)}, u32[]{:S(2)}) collective-permute-start(bf16[256,1024]{1,0:T(8,128)(2,1)S(1)} %collective-permute-done), channel_id=1, source_target_pairs={{0,1},{1,2},{2,3},{3,4},{4,5},{5,6},{6,7},{7,8},{8,9},{9,10},{10,1... | collective-permute-start | bytes 1572872 | tf_op jit(solution)/shard_map/ppermute | solution.py:29
  25.2 15.7 %slice-start = ((s8[6291456]{0:T(1024)(128)(4,1)}), s8[4194304]{0:T(1024)(128)(4,1)S(1)}, s32[]{:S(2)}) async-start(s8[6291456]{0:T(1024)(128)(4,1)} %bitcast.37), calls=%async_computation | async-start | bytes 8388608
  28.0 12.9 %slice-start.1 = ((s8[6291456]{0:T(1024)(128)(4,1)}), s8[2097152]{0:T(1024)(128)(4,1)S(1)}, s32[]{:S(2)}) async-start(s8[6291456]{0:T(1024)(128)(4,1)} %bitcast.37), calls=%async_computation.1 | async-start | bytes 4194304
  58.2 8.2 %slice-start.2 = ((s8[6291456]{0:T(1024)(128)(4,1)}), s8[4194304]{0:T(1024)(128)(4,1)S(1)}, s32[]{:S(2)}) async-start(s8[6291456]{0:T(1024)(128)(4,1)} %bitcast.40), calls=%async_computation.2 | async-start | bytes 8388608
  60.7 5.6 %copy-start.2 = (bf16[512,1024]{1,0:T(8,128)(2,1)S(1)}, bf16[512,1024]{1,0:T(8,128)(2,1)}, u32[]{:S(2)}) copy-start(bf16[512,1024]{1,0:T(8,128)(2,1)} %get-tuple-element.16) | copy-start | bytes 3145732
  60.7 5.6 %copy-start.1 = (bf16[512,1024]{1,0:T(8,128)(2,1)S(1)}, bf16[512,1024]{1,0:T(8,128)(2,1)}, u32[]{:S(2)}) copy-start(bf16[512,1024]{1,0:T(8,128)(2,1)} %get-tuple-element.17) | copy-start | bytes 3145732
  60.7 5.7 %slice-start.3 = ((s8[6291456]{0:T(1024)(128)(4,1)}), s8[2097152]{0:T(1024)(128)(4,1)S(1)}, s32[]{:S(2)}) async-start(s8[6291456]{0:T(1024)(128)(4,1)} %bitcast.40), calls=%async_computation.3 | async-start | bytes 4194304
  64.3 19.3 %collective-permute-start.4 = (bf16[256,1024]{1,0:T(8,128)(2,1)S(1)}, bf16[256,1024]{1,0:T(8,128)(2,1)S(1)}, u32[]{:S(2)}, u32[]{:S(2)}) collective-permute-start(bf16[256,1024]{1,0:T(8,128)(2,1)S(1)} %fusion.32), channel_id=1, source_target_pairs={{0,1},{1,2},{2,3},{3,4},{4,5},{5,6},{6,7},{7,8},{8,9},{9,10},{10,1... | collective-permute-start | bytes 1572872 | tf_op jit(solution)/shard_map/ppermute | solution.py:29
  66.4 8.4 %copy-start.4 = (bf16[256,1024]{1,0:T(8,128)(2,1)S(1)}, bf16[256,1024]{1,0:T(8,128)(2,1)}, u32[]{:S(2)}) copy-start(bf16[256,1024]{1,0:T(8,128)(2,1)} %get-tuple-element.11) | copy-start | bytes 1572868
  66.4 8.4 %copy-start.5 = (bf16[256,1024]{1,0:T(8,128)(2,1)S(1)}, bf16[256,1024]{1,0:T(8,128)(2,1)}, u32[]{:S(2)}) copy-start(bf16[256,1024]{1,0:T(8,128)(2,1)} %get-tuple-element.12) | copy-start | bytes 1572868
  66.4 8.4 %copy-start.6 = (bf16[256,1024]{1,0:T(8,128)(2,1)S(1)}, bf16[256,1024]{1,0:T(8,128)(2,1)}, u32[]{:S(2)}) copy-start(bf16[256,1024]{1,0:T(8,128)(2,1)} %get-tuple-element.13) | copy-start | bytes 1572868
  67.7 15.9 %collective-permute-start.5 = (bf16[256,1024]{1,0:T(8,128)(2,1)S(1)}, bf16[256,1024]{1,0:T(8,128)(2,1)S(1)}, u32[]{:S(2)}, u32[]{:S(2)}) collective-permute-start(bf16[256,1024]{1,0:T(8,128)(2,1)S(1)} %fusion.35), channel_id=1, source_target_pairs={{1,0},{2,1},{3,2},{4,3},{5,4},{6,5},{7,6},{8,7},{9,8},{10,9},{11,1... | collective-permute-start | bytes 1572872 | tf_op jit(solution)/shard_map/ppermute | solution.py:34
  74.9 1.8 %copy-start.3 = (bf16[256,1024]{1,0:T(8,128)(2,1)S(1)}, bf16[256,1024]{1,0:T(8,128)(2,1)}, u32[]{:S(2)}) copy-start(bf16[256,1024]{1,0:T(8,128)(2,1)} %get-tuple-element.10) | copy-start | bytes 1572868

commit v8 on v2

--- a/solution.py
+++ b/solution.py
@@ -51,21 +51,23 @@
     keys = jnp.concatenate([kh_ref[:margin], ko_ref[...], kh_ref[margin:]], axis=0)
     values = jnp.concatenate([vh_ref[:margin], vo_ref[...], vh_ref[margin:]], axis=0)
     grad_out = do_ref[...]
-    scores = lax.dot_general(queries, keys, NT, preferred_element_type=jnp.float32) * scaling
+    scores = lax.dot_general(keys, queries, NT, preferred_element_type=jnp.float32) * scaling
     scores = scores + live_ref[...]
-    row_max = jnp.max(scores, axis=1, keepdims=True)
+    row_max = jnp.max(scores, axis=0, keepdims=True)
     raw = jnp.exp(scores - row_max)
-    weights = raw * (1.0 / jnp.sum(raw, axis=1, keepdims=True))
+    weights = raw * (1.0 / jnp.sum(raw, axis=0, keepdims=True))
     weights_bf = weights.astype(jnp.bfloat16)
-    out_ref[...] = jnp.dot(weights_bf, values, preferred_element_type=jnp.float32).astype(
-        out_ref.dtype
-    )
-    weight_grad = lax.dot_general(grad_out, values, NT, preferred_element_type=jnp.float32)
-    weight_mean = jnp.sum(weights * weight_grad, axis=1, keepdims=True)
+    out_ref[...] = lax.dot_general(
+        weights_bf, values, TN, preferred_element_type=jnp.float32
+    ).astype(out_ref.dtype)
+    weight_grad = lax.dot_general(values, grad_out, NT, preferred_element_type=jnp.float32)
+    weight_mean = jnp.sum(weights * weight_grad, axis=0, keepdims=True)
     score_grad = (weights * (weight_grad - weight_mean) * scaling).astype(jnp.bfloat16)
-    dq_ref[...] = jnp.dot(score_grad, keys, preferred_element_type=jnp.float32).astype(dq_ref.dtype)
-    key_grad = lax.dot_general(score_grad, queries, TN, preferred_element_type=jnp.float32)
-    value_grad = lax.dot_general(weights_bf, grad_out, TN, preferred_element_type=jnp.float32)
+    dq_ref[...] = lax.dot_general(
+        score_grad, keys, TN, preferred_element_type=jnp.float32
+    ).astype(dq_ref.dtype)
+    key_grad = jnp.dot(score_grad, queries, preferred_element_type=jnp.float32)
+    value_grad = jnp.dot(weights_bf, grad_out, preferred_element_type=jnp.float32)
     dtype = dk_ref.dtype
     dk_ref[...] = key_grad[margin : margin + rows].astype(dtype)
     dv_ref[...] = value_grad[margin : margin + rows].astype(dtype)
@@ -79,7 +81,7 @@
     rows, width = attended_grad.shape
     heads = width // HEAD_DIM
     halo_rows = halo_kv.shape[0]
-    window = live.shape[1]
+    window = live.shape[0]
     own = lambda offset: pl.BlockSpec((rows, HEAD_DIM), lambda h: (0, offset + h))
     side = lambda offset: pl.BlockSpec((halo_rows, HEAD_DIM), lambda h: (0, offset + h))
     flops = heads * 5 * 2 * rows * window * HEAD_DIM
@@ -96,7 +98,7 @@
             side(0),
             side(heads),
             own(0),
-            pl.BlockSpec((rows, window), lambda h: (0, 0)),
+            pl.BlockSpec((window, rows), lambda h: (0, 0)),
         ],
         out_specs=[own(0), own(0), own(0), own(0), side(0), side(0)],
         out_shape=[own_shape, own_shape, own_shape, own_shape, side_shape, side_shape],
@@ -143,7 +145,7 @@
         live_slots[:, :, None] & (window_index[:, :, None] == jnp.arange(span_blocks)[None, None, :]),
         axis=1,
     )
-    live = jnp.where(jnp.repeat(jnp.repeat(live_blocks, BLOCK, axis=0), BLOCK, axis=1), 0.0, -1e30)
+    live = jnp.where(jnp.repeat(jnp.repeat(live_blocks.T, BLOCK, axis=0), BLOCK, axis=1), 0.0, -1e30)
 
     attended, query_grad, key_grad, value_grad, halo_key_grad, halo_value_grad = attention(
         projected, halo_kv, attended_grad, live

time: 84.6 us -> 86.7 us (1.025)
  matrix products: 23.8 us -> 19.8 us
  waiting for transfers between devices: 15.7 us -> 19.1 us
  Pallas kernels: 13.4 us -> 16.6 us
  other arithmetic: 4.65 us -> 3.61 us
    ppermute x2, waiting for transfers between devices: 1.18 us -> 4.82 us  [from_right(): return lax.ppermute(value, axis, [(i + 1, i) for i in range(count - 1)])]
    pallas_call x1, Pallas kernels: 13.4 us -> 16.6 us  [attention(): pl.pallas_call(attention_kernel, grid=(heads,), in_specs=[own(0), own(hea...]
    dot_general x1, matrix products: 5.97 us -> 3.08 us  [per_device(): jnp.dot(normed.astype(jnp.bfloat16), weights_in, preferred_element_type=j...]
    dot_general x1, matrix products: 2.73 us -> 1.54 us  [per_device(): jnp.einsum('rd,wd->rw', upstream, weights_out, preferred_element_type=jnp...]
    select_n x2 -> x1, local copies, waits for them, and re-layouts: 1.26 us -> 0.1 us  [per_device(): jnp.where(jnp.repeat(jnp.repeat(live_blocks.T, BLOCK, axis=0), BLOCK, axi...]
    broadcast_in_dim x1, other arithmetic: 2.27 us -> 1.23 us  [per_device(): return (result[None], input_grad[None])]
    broadcast_in_dim x1 -> x2, local copies, waits for them, and re-layouts: 0.06 us -> 1 us  [the longest x1 0.97 us: per_device(): jnp.repeat(jnp.repeat(live_blocks.T, BLOCK, axis=0), BLOCK, axis=1)]
    unnamed x16 -> x13, local copies, waits for them, and re-layouts: 0.12 us -> 0.99 us
  transfers between devices with their start and end apart: 6 -> 6, of which waited for: 4 -> 5; matrix products, arithmetic and copies ran while one was open for 21% -> 17% of each run, Pallas kernels for 0% -> 0%
where the time goes in v8:
time: 86.7 us; the launch traced here: 86.2 us
  starting transfers between devices  24.2 us (28%)
  matrix products  19.8 us (23%)
  waiting for transfers between devices  19.1 us (22%)
  Pallas kernels  16.6 us (19%)
  other arithmetic  3.61 us (4%)
  local copies, waits for them, and re-layouts  2.15 us (2%)
    ppermute x2, starting transfers between devices, from_right(): return lax.ppermute(value, axis, [(i + 1, i) for i in range(count - 1)])  16.9 us
    pallas_call x1, Pallas kernels, attention(): pl.pallas_call(attention_kernel, grid=(heads,), in_specs=[own(0), own(hea...  16.6 us
    ppermute x2, waiting for transfers between devices, from_left(): return lax.ppermute(value, axis, [(i, i + 1) for i in range(count - 1)])  8.52 us
    ppermute x2, waiting for transfers between devices, shifted(): return lax.ppermute(value, axis, pairs)  5.79 us
    dot_general x1, matrix products, per_device(): jnp.einsum('rc,dc->rd', halo_grads, weights_kv, preferred_element_type=jn...  5.2 us
    ppermute x2, waiting for transfers between devices, from_right(): return lax.ppermute(value, axis, [(i + 1, i) for i in range(count - 1)])  4.82 us
    dot_general x1, matrix products, per_device(): jnp.einsum('rc,dc->rd', own_grads, weights_in, preferred_element_type=jnp...  4.66 us
    ppermute x2, starting transfers between devices, from_left(): return lax.ppermute(value, axis, [(i, i + 1) for i in range(count - 1)])  3.97 us
  transfers between devices with their start and end apart: 6, of which 5 were waited for; matrix products, arithmetic and copies ran while one was open for 17% of the time, Pallas kernels for 0%

profile of v8, /device:TPU:24, one launch (start us, length us, event | category | flops | bytes accessed | tf_op | source)
XLA Modules:
  0.0 86.2 jit_solution(4926586287389912843)
XLA Ops:
  0.6 0.0 copy-start
  0.6 0.1 collective-permute-start
  0.7 3.2 %collective-permute-start.3 = (bf16[256,1024]{1,0:T(8,128)(2,1)}, bf16[256,1024]{1,0:T(8,128)(2,1)S(1)}, u32[]{:S(2)}, u32[]{:S(2)}) collective-permute-start(bf16[256,1024]{1,0:T(8,128)(2,1)} %bitcast.39), channel_id=1, source_target_pairs={{0,192},{64,0},{128,64},{192,128},{1,193},{65,1},{129,65},{193,129... | collective-permute-start | bytes 1572872 | tf_op jit(solution)/shard_map/ppermute | solution.py:24
  4.0 0.7 subtract_add_fusion
  4.7 0.7 iota_compare_fusion.1
  5.4 0.1 fusion.53
  5.5 0.1 copy.8
  5.6 0.0 copy-start.1
  5.6 1.0 %broadcast_in_dim.31 = f32[768,2,128]{2,1,0:T(2,128)S(1)} broadcast(f32[768,2]{1,0:T(8,128)S(1)} %bitcast.35), dimensions={0,1} | broadcast | bytes 792576 | tf_op jit(solution)/shard_map/broadcast_in_dim | solution.py:148
  6.6 1.0 %copy.11 = f32[96,8,2,128]{3,1,2,0:T(8,128)} copy(f32[96,8,2,128]{3,2,1,0:T(2,128)S(1)} %bitcast.34) | data formatting | bytes 1572864
  7.6 5.8 %collective-permute-done = bf16[256,1024]{1,0:T(8,128)(2,1)S(1)} collective-permute-done((bf16[256,1024]{1,0:T(8,128)(2,1)}, bf16[256,1024]{1,0:T(8,128)(2,1)S(1)}, u32[]{:S(2)}, u32[]{:S(2)}) %collective-permute-start) | collective-permute-done | bytes 524320 | tf_op jit(solution)/shard_map/ppermute | solution.py:24
  13.3 9.8 %collective-permute-start.2 = (bf16[256,1024]{1,0:T(8,128)(2,1)S(1)}, bf16[256,1024]{1,0:T(8,128)(2,1)S(1)}, u32[]{:S(2)}, u32[]{:S(2)}) collective-permute-start(bf16[256,1024]{1,0:T(8,128)(2,1)S(1)} %collective-permute-done), channel_id=1, source_target_pairs={{1,0},{2,1},{3,2},{4,3},{5,4},{6,5},{7,6},{8,7},{9,8},{10,9},{11,1... | collective-permute-start | bytes 1572872 | tf_op jit(solution)/shard_map/ppermute | solution.py:34
  23.1 1.9 %collective-permute-start.1 = (bf16[256,1024]{1,0:T(8,128)(2,1)S(1)}, bf16[256,1024]{1,0:T(8,128)(2,1)S(1)}, u32[]{:S(2)}, u32[]{:S(2)}) collective-permute-start(bf16[256,1024]{1,0:T(8,128)(2,1)S(1)} %collective-permute-done), channel_id=1, source_target_pairs={{0,1},{1,2},{2,3},{3,4},{4,5},{5,6},{6,7},{7,8},{8,9},{9,10},{10,1... | collective-permute-start | bytes 1572872 | tf_op jit(solution)/shard_map/ppermute | solution.py:29
  25.0 0.2 fusion.46
  25.2 1.5 %fusion.35.do_ref = bf16[256,1024]{1,0:T(8,128)(2,1)} fusion(bf16[256,1024]{1,0:T(8,128)(2,1)S(1)} %collective-permute-done.3, bf16[1,1024,1024]{2,1,0:T(8,128)(2,1)S(1)} %copy-done), kind=kOutput, calls=%fused_computation.31 | convolution fusion | flops 537133056 | bytes 3145728 | tf_op jit(solution)/shard_map/rd,wd->rw/dot_general | solution.py:133
  26.8 3.1 %convolution_convert_fusion.q_ref.ko_ref.vo_ref = bf16[256,3072]{1,0:T(8,128)(2,1)} fusion(bf16[256,1024]{1,0:T(8,128)(2,1)S(1)} %collective-permute-done, f32[256]{0:T(256)S(1)} %add_rsqrt_fusion.1, bf16[1,1024,3072]{2,1,0:T(8,128)(2,1)S(1)} %copy-done.1), kind=kOutput, calls=%fused_computation | convolution fusion | flops 1612185600 | bytes 8389632 | tf_op jit(solution)/shard_map/dot_general | solution.py:130
  29.9 3.6 %collective-permute-done.2 = bf16[256,1024]{1,0:T(8,128)(2,1)S(1)} collective-permute-done((bf16[256,1024]{1,0:T(8,128)(2,1)S(1)}, bf16[256,1024]{1,0:T(8,128)(2,1)S(1)}, u32[]{:S(2)}, u32[]{:S(2)}) %collective-permute-start.2) | collective-permute-done | bytes 524320 | tf_op jit(solution)/shard_map/ppermute | solution.py:34
  33.5 7.1 %collective-permute-done.1 = bf16[256,1024]{1,0:T(8,128)(2,1)S(1)} collective-permute-done((bf16[256,1024]{1,0:T(8,128)(2,1)S(1)}, bf16[256,1024]{1,0:T(8,128)(2,1)S(1)}, u32[]{:S(2)}, u32[]{:S(2)}) %collective-permute-start.1) | collective-permute-done | bytes 524320 | tf_op jit(solution)/shard_map/ppermute | solution.py:29
  40.6 0.3 fusion.7
  40.9 3.8 %fusion.4.kh_ref.vh_ref = bf16[512,2048]{1,0:T(8,128)(2,1)} fusion(bf16[1024,3072]{1,0:T(8,128)(2,1)S(1)} %bitcast.37, f32[512]{0:T(512)S(1)} %add_rsqrt_fusion, bf16[256,1024]{1,0:T(8,128)(2,1)S(1)} %collective-permute-done.2, bf16[256,1024]{1,0:T(8,128)(2,1)S(1)} %collective-permute-done.1), kind=kOutput, calls=%fused_computation.5 | convolution fusion | flops 2151677952 | bytes 7342080 | tf_op jit(solution)/shard_map/dot_general | solution.py:138
  44.7 16.6 %shard_map.77 = (bf16[256,1024]{1,0:T(8,128)(2,1)}, bf16[256,1024]{1,0:T(8,128)(2,1)}, bf16[256,1024]{1,0:T(8,128)(2,1)}, bf16[256,1024]{1,0:T(8,128)(2,1)}, bf1...) custom-call(bf16[256,3072]{1,0:T(8,128)(2,1)} %convolution_convert_fusion.q_ref.ko_ref.vo_ref, ...), custom_call_target="tpu_custom_call" | custom-call | flops 2013265920 | bytes 9175040 | tf_op jit(solution)/shard_map/pallas_call | solution.py:91
  61.3 5.2 %fusion.22 = bf16[512,1024]{1,0:T(8,128)(2,1)S(1)} fusion(bf16[1024,3072]{1,0:T(8,128)(2,1)} %bitcast.36, bf16[512,1024]{1,0:T(8,128)(2,1)} %get-tuple-element.13, bf16[512,1024]{1,0:T(8,128)(2,1)} %get-tuple-element.12), kind=kOutput, calls=%fused_computation.26 | convolution fusion | flops 2152202240 | bytes 7340032 | tf_op jit(solution)/shard_map/rc,dc->rd/dot_general | solution.py:158
  66.5 0.1 fusion.59
  66.6 2.1 %collective-permute-start.4 = (bf16[256,1024]{1,0:T(8,128)(2,1)S(1)}, bf16[256,1024]{1,0:T(8,128)(2,1)S(1)}, u32[]{:S(2)}, u32[]{:S(2)}) collective-permute-start(bf16[256,1024]{1,0:T(8,128)(2,1)S(1)} %get-tuple-element.14), channel_id=1, source_target_pairs={{0,1},{1,2},{2,3},{3,4},{4,5},{5,6},{6,7},{7,8},{8,9},{9,10},{10,1... | collective-permute-start | bytes 1572872 | tf_op jit(solution)/shard_map/ppermute | solution.py:29
  68.7 7.1 %collective-permute-start.5 = (bf16[256,1024]{1,0:T(8,128)(2,1)S(1)}, bf16[256,1024]{1,0:T(8,128)(2,1)S(1)}, u32[]{:S(2)}, u32[]{:S(2)}) collective-permute-start(bf16[256,1024]{1,0:T(8,128)(2,1)S(1)} %get-tuple-element.15), channel_id=1, source_target_pairs={{1,0},{2,1},{3,2},{4,3},{5,4},{6,5},{7,6},{8,7},{9,8},{10,9},{11,1... | collective-permute-start | bytes 1572872 | tf_op jit(solution)/shard_map/ppermute | solution.py:34
  75.8 0.0 copy-start.2
  75.8 4.7 %fusion.16 = f32[256,1024]{1,0:T(8,128)S(1)} fusion(bf16[256,1024]{1,0:T(8,128)(2,1)S(1)} %copy-done.5, bf16[256,1024]{1,0:T(8,128)(2,1)S(1)} %copy-done.4, bf16[256,1024]{1,0:T(8,128)(2,1)S(1)} %copy-done.3, bf16[1,1024,3072]{2,1,0:T(8,128)(2,1)} %param.8), kind=kOutput, calls=%fused_computation.17 | convolution fusion | flops 1615331328 | bytes 8912896 | tf_op jit(solution)/shard_map/rc,dc->rd/dot_general | solution.py:165
  80.5 1.5 %fusion.38 = bf16[1,256,1024]{2,1,0:T(8,128)(2,1)} fusion(bf16[256,1024]{1,0:T(8,128)(2,1)S(1)} %copy-done.2, bf16[1,1024,1024]{2,1,0:T(8,128)(2,1)S(1)} %copy-done, bf16[256,1024]{1,0:T(8,128)(2,1)S(1)} %collective-permute-done), kind=kOutput, calls=%fused_computation.32 | convolution fusion | flops 537657344 | bytes 3670016 | tf_op jit(solution)/shard_map/dot_general | solution.py:153
  82.0 1.4 %collective-permute-done.4 = bf16[256,1024]{1,0:T(8,128)(2,1)S(1)} collective-permute-done((bf16[256,1024]{1,0:T(8,128)(2,1)S(1)}, bf16[256,1024]{1,0:T(8,128)(2,1)S(1)}, u32[]{:S(2)}, u32[]{:S(2)}) %collective-permute-start.4) | collective-permute-done | bytes 524320 | tf_op jit(solution)/shard_map/ppermute | solution.py:29
  83.4 1.2 %collective-permute-done.5 = bf16[256,1024]{1,0:T(8,128)(2,1)S(1)} collective-permute-done((bf16[256,1024]{1,0:T(8,128)(2,1)S(1)}, bf16[256,1024]{1,0:T(8,128)(2,1)S(1)}, u32[]{:S(2)}, u32[]{:S(2)}) %collective-permute-start.5) | collective-permute-done | bytes 524320 | tf_op jit(solution)/shard_map/ppermute | solution.py:34
  84.6 0.4 fusion.41
  85.0 1.2 %fusion.49 = bf16[1,256,1024]{2,1,0:T(8,128)(2,1)} fusion(bf16[256,1024]{1,0:T(8,128)(2,1)S(1)} %collective-permute-done, bf16[256,1024]{1,0:T(8,128)(2,1)S(1)} %collective-permute-done.3, f32[256]{0:T(256)S(1)} %broadcast_multiply_fusion, f32[256]{0:T(256)S(1)} %add_rsqrt_fusion.1, bf16[256,1024]{1,0:T(8,128)(2,1)S(1)} %collective-permute-done.5, ...), kind=kLoop, calls=%fused_computation.43 | loop fusion | flops 3145728 | bytes 3672064 | tf_op jit(solution)/shard_map/broadcast_in_dim | solution.py:173
  (15 shorter events, 0.1 us)
Async XLA Ops:
  0.6 24.6 %copy-start = (bf16[1,1024,1024]{2,1,0:T(8,128)(2,1)S(1)}, bf16[1,1024,1024]{2,1,0:T(8,128)(2,1)}, u32[]{:S(2)}) copy-start(bf16[1,1024,1024]{2,1,0:T(8,128)(2,1)} %param.9) | copy-start | bytes 6291460
  0.6 12.7 %collective-permute-start = (bf16[256,1024]{1,0:T(8,128)(2,1)}, bf16[256,1024]{1,0:T(8,128)(2,1)S(1)}, u32[]{:S(2)}, u32[]{:S(2)}) collective-permute-start(bf16[256,1024]{1,0:T(8,128)(2,1)} %bitcast.38), channel_id=1, source_target_pairs={{0,64},{64,128},{128,192},{192,0},{1,65},{65,129},{129,193},{193,1... | collective-permute-start | bytes 1572872 | tf_op jit(solution)/shard_map/ppermute | solution.py:24
  0.7 24.5 %collective-permute-start.3 = (bf16[256,1024]{1,0:T(8,128)(2,1)}, bf16[256,1024]{1,0:T(8,128)(2,1)S(1)}, u32[]{:S(2)}, u32[]{:S(2)}) collective-permute-start(bf16[256,1024]{1,0:T(8,128)(2,1)} %bitcast.39), channel_id=1, source_target_pairs={{0,192},{64,0},{128,64},{192,128},{1,193},{65,1},{129,65},{193,129... | collective-permute-start | bytes 1572872 | tf_op jit(solution)/shard_map/ppermute | solution.py:24
  5.6 21.2 %copy-start.1 = (bf16[1,1024,3072]{2,1,0:T(8,128)(2,1)S(1)}, bf16[1,1024,3072]{2,1,0:T(8,128)(2,1)}, u32[]{:S(2)}) copy-start(bf16[1,1024,3072]{2,1,0:T(8,128)(2,1)} %param.8) | copy-start | bytes 18874372
  13.3 20.2 %collective-permute-start.2 = (bf16[256,1024]{1,0:T(8,128)(2,1)S(1)}, bf16[256,1024]{1,0:T(8,128)(2,1)S(1)}, u32[]{:S(2)}, u32[]{:S(2)}) collective-permute-start(bf16[256,1024]{1,0:T(8,128)(2,1)S(1)} %collective-permute-done), channel_id=1, source_target_pairs={{1,0},{2,1},{3,2},{4,3},{5,4},{6,5},{7,6},{8,7},{9,8},{10,9},{11,1... | collective-permute-start | bytes 1572872 | tf_op jit(solution)/shard_map/ppermute | solution.py:34
  23.1 17.5 %collective-permute-start.1 = (bf16[256,1024]{1,0:T(8,128)(2,1)S(1)}, bf16[256,1024]{1,0:T(8,128)(2,1)S(1)}, u32[]{:S(2)}, u32[]{:S(2)}) collective-permute-start(bf16[256,1024]{1,0:T(8,128)(2,1)S(1)} %collective-permute-done), channel_id=1, source_target_pairs={{0,1},{1,2},{2,3},{3,4},{4,5},{5,6},{6,7},{7,8},{8,9},{9,10},{10,1... | collective-permute-start | bytes 1572872 | tf_op jit(solution)/shard_map/ppermute | solution.py:29
  66.5 9.3 %copy-start.3 = (bf16[256,1024]{1,0:T(8,128)(2,1)S(1)}, bf16[256,1024]{1,0:T(8,128)(2,1)}, u32[]{:S(2)}) copy-start(bf16[256,1024]{1,0:T(8,128)(2,1)} %get-tuple-element.9) | copy-start | bytes 1572868
  66.5 9.3 %copy-start.4 = (bf16[256,1024]{1,0:T(8,128)(2,1)S(1)}, bf16[256,1024]{1,0:T(8,128)(2,1)}, u32[]{:S(2)}) copy-start(bf16[256,1024]{1,0:T(8,128)(2,1)} %get-tuple-element.10) | copy-start | bytes 1572868
  66.5 9.3 %copy-start.5 = (bf16[256,1024]{1,0:T(8,128)(2,1)S(1)}, bf16[256,1024]{1,0:T(8,128)(2,1)}, u32[]{:S(2)}) copy-start(bf16[256,1024]{1,0:T(8,128)(2,1)} %get-tuple-element.11) | copy-start | bytes 1572868
  66.6 16.8 %collective-permute-start.4 = (bf16[256,1024]{1,0:T(8,128)(2,1)S(1)}, bf16[256,1024]{1,0:T(8,128)(2,1)S(1)}, u32[]{:S(2)}, u32[]{:S(2)}) collective-permute-start(bf16[256,1024]{1,0:T(8,128)(2,1)S(1)} %get-tuple-element.14), channel_id=1, source_target_pairs={{0,1},{1,2},{2,3},{3,4},{4,5},{5,6},{6,7},{7,8},{8,9},{9,10},{10,1... | collective-permute-start | bytes 1572872 | tf_op jit(solution)/shard_map/ppermute | solution.py:29
  68.7 15.9 %collective-permute-start.5 = (bf16[256,1024]{1,0:T(8,128)(2,1)S(1)}, bf16[256,1024]{1,0:T(8,128)(2,1)S(1)}, u32[]{:S(2)}, u32[]{:S(2)}) collective-permute-start(bf16[256,1024]{1,0:T(8,128)(2,1)S(1)} %get-tuple-element.15), channel_id=1, source_target_pairs={{1,0},{2,1},{3,2},{4,3},{5,4},{6,5},{7,6},{8,7},{9,8},{10,9},{11,1... | collective-permute-start | bytes 1572872 | tf_op jit(solution)/shard_map/ppermute | solution.py:34
  75.8 4.7 %copy-start.2 = (bf16[256,1024]{1,0:T(8,128)(2,1)S(1)}, bf16[256,1024]{1,0:T(8,128)(2,1)}, u32[]{:S(2)}) copy-start(bf16[256,1024]{1,0:T(8,128)(2,1)} %get-tuple-element.8) | copy-start | bytes 1572868

commit v9 on v2

--- a/solution.py
+++ b/solution.py
@@ -38,6 +38,9 @@
     values = rows.astype(jnp.float32)
     factor = lax.rsqrt(jnp.mean(values * values, axis=-1, keepdims=True) + EPSILON)
     return values, factor, values * factor
+
+
+GROUP = 2
 
 
 def attention_kernel(
@@ -47,32 +50,41 @@
     rows = q_ref.shape[0]
     margin = kh_ref.shape[0] // 2
     scaling = HEAD_DIM ** (-0.5)
-    queries = q_ref[...]
-    keys = jnp.concatenate([kh_ref[:margin], ko_ref[...], kh_ref[margin:]], axis=0)
-    values = jnp.concatenate([vh_ref[:margin], vo_ref[...], vh_ref[margin:]], axis=0)
-    grad_out = do_ref[...]
-    scores = lax.dot_general(queries, keys, NT, preferred_element_type=jnp.float32) * scaling
-    scores = scores + live_ref[...]
-    row_max = jnp.max(scores, axis=1, keepdims=True)
-    raw = jnp.exp(scores - row_max)
-    weights = raw * (1.0 / jnp.sum(raw, axis=1, keepdims=True))
-    weights_bf = weights.astype(jnp.bfloat16)
-    out_ref[...] = jnp.dot(weights_bf, values, preferred_element_type=jnp.float32).astype(
-        out_ref.dtype
-    )
-    weight_grad = lax.dot_general(grad_out, values, NT, preferred_element_type=jnp.float32)
-    weight_mean = jnp.sum(weights * weight_grad, axis=1, keepdims=True)
-    score_grad = (weights * (weight_grad - weight_mean) * scaling).astype(jnp.bfloat16)
-    dq_ref[...] = jnp.dot(score_grad, keys, preferred_element_type=jnp.float32).astype(dq_ref.dtype)
-    key_grad = lax.dot_general(score_grad, queries, TN, preferred_element_type=jnp.float32)
-    value_grad = lax.dot_general(weights_bf, grad_out, TN, preferred_element_type=jnp.float32)
-    dtype = dk_ref.dtype
-    dk_ref[...] = key_grad[margin : margin + rows].astype(dtype)
-    dv_ref[...] = value_grad[margin : margin + rows].astype(dtype)
-    dkh_ref[:margin] = key_grad[:margin].astype(dtype)
-    dkh_ref[margin:] = key_grad[margin + rows :].astype(dtype)
-    dvh_ref[:margin] = value_grad[:margin].astype(dtype)
-    dvh_ref[margin:] = value_grad[margin + rows :].astype(dtype)
+    live = live_ref[...]
+    for part in range(q_ref.shape[1] // HEAD_DIM):
+        lanes = slice(part * HEAD_DIM, (part + 1) * HEAD_DIM)
+        queries = q_ref[:, lanes]
+        keys = jnp.concatenate(
+            [kh_ref[:margin, lanes], ko_ref[:, lanes], kh_ref[margin:, lanes]], axis=0
+        )
+        values = jnp.concatenate(
+            [vh_ref[:margin, lanes], vo_ref[:, lanes], vh_ref[margin:, lanes]], axis=0
+        )
+        grad_out = do_ref[:, lanes]
+        scores = lax.dot_general(queries, keys, NT, preferred_element_type=jnp.float32) * scaling
+        scores = scores + live
+        row_max = jnp.max(scores, axis=1, keepdims=True)
+        raw = jnp.exp(scores - row_max)
+        weights = raw * (1.0 / jnp.sum(raw, axis=1, keepdims=True))
+        weights_bf = weights.astype(jnp.bfloat16)
+        out_ref[:, lanes] = jnp.dot(
+            weights_bf, values, preferred_element_type=jnp.float32
+        ).astype(out_ref.dtype)
+        weight_grad = lax.dot_general(grad_out, values, NT, preferred_element_type=jnp.float32)
+        weight_mean = jnp.sum(weights * weight_grad, axis=1, keepdims=True)
+        score_grad = (weights * (weight_grad - weight_mean) * scaling).astype(jnp.bfloat16)
+        dq_ref[:, lanes] = jnp.dot(
+            score_grad, keys, preferred_element_type=jnp.float32
+        ).astype(dq_ref.dtype)
+        key_grad = lax.dot_general(score_grad, queries, TN, preferred_element_type=jnp.float32)
+        value_grad = lax.dot_general(weights_bf, grad_out, TN, preferred_element_type=jnp.float32)
+        dtype = dk_ref.dtype
+        dk_ref[:, lanes] = key_grad[margin : margin + rows].astype(dtype)
+        dv_ref[:, lanes] = value_grad[margin : margin + rows].astype(dtype)
+        dkh_ref[:margin, lanes] = key_grad[:margin].astype(dtype)
+        dkh_ref[margin:, lanes] = key_grad[margin + rows :].astype(dtype)
+        dvh_ref[:margin, lanes] = value_grad[:margin].astype(dtype)
+        dvh_ref[margin:, lanes] = value_grad[margin + rows :].astype(dtype)
 
 
 def attention(projected, halo_kv, attended_grad, live):
@@ -80,15 +92,17 @@
     heads = width // HEAD_DIM
     halo_rows = halo_kv.shape[0]
     window = live.shape[1]
-    own = lambda offset: pl.BlockSpec((rows, HEAD_DIM), lambda h: (0, offset + h))
-    side = lambda offset: pl.BlockSpec((halo_rows, HEAD_DIM), lambda h: (0, offset + h))
+    group = GROUP if heads % GROUP == 0 else 1
+    lanes = group * HEAD_DIM
+    own = lambda offset: pl.BlockSpec((rows, lanes), lambda h: (0, offset // group + h))
+    side = lambda offset: pl.BlockSpec((halo_rows, lanes), lambda h: (0, offset // group + h))
     flops = heads * 5 * 2 * rows * window * HEAD_DIM
     moved = 2 * (2 * projected.size + 2 * halo_kv.size + 2 * attended_grad.size) + 4 * live.size
     own_shape = jax.ShapeDtypeStruct((rows, width), jnp.bfloat16)
     side_shape = jax.ShapeDtypeStruct((halo_rows, width), jnp.bfloat16)
     return pl.pallas_call(
         attention_kernel,
-        grid=(heads,),
+        grid=(heads // group,),
         in_specs=[
             own(0),
             own(heads),

time: 84.6 us -> 83.9 us (level)
  transfers between devices with their start and end apart: 6 -> 6, of which waited for: 4 -> 4; matrix products, arithmetic and copies ran while one was open for 21% -> 22% of each run, Pallas kernels for 0% -> 0%
where the time goes in v9:
time: 83.9 us; the launch traced here: 83.4 us
  starting transfers between devices  24.2 us (29%)
  matrix products  23.8 us (28%)
  waiting for transfers between devices  15.7 us (19%)
  Pallas kernels  12.7 us (15%)
  other arithmetic  4.65 us (6%)
  local copies, waits for them, and re-layouts  1.51 us (2%)
  between operations  0.84 us (1%)
    ppermute x2, starting transfers between devices, from_right(): return lax.ppermute(value, axis, [(i + 1, i) for i in range(count - 1)])  16.9 us
    pallas_call x1, Pallas kernels, attention(): pl.pallas_call(attention_kernel, grid=(heads // group,), in_specs=[own(0)...  12.7 us
    ppermute x2, waiting for transfers between devices, from_left(): return lax.ppermute(value, axis, [(i, i + 1) for i in range(count - 1)])  8.07 us
    ppermute x2, waiting for transfers between devices, shifted(): return lax.ppermute(value, axis, pairs)  6.45 us
    dot_general x1, matrix products, per_device(): jnp.dot(normed.astype(jnp.bfloat16), weights_in, preferred_element_type=j...  5.97 us
    dot_general x1, matrix products, per_device(): jnp.einsum('rc,dc->rd', halo_grads, weights_kv, preferred_element_type=jn...  5.2 us
    dot_general x1, matrix products, per_device(): jnp.einsum('rc,dc->rd', own_grads, weights_in, preferred_element_type=jnp...  4.66 us
    ppermute x2, starting transfers between devices, from_left(): return lax.ppermute(value, axis, [(i, i + 1) for i in range(count - 1)])  3.97 us
  transfers between devices with their start and end apart: 6, of which 4 were waited for; matrix products, arithmetic and copies ran while one was open for 22% of the time, Pallas kernels for 0%

profile of v9, /device:TPU:24, one launch (start us, length us, event | category | flops | bytes accessed | tf_op | source)
XLA Modules:
  0.0 83.4 jit_solution(6449627091319083961)
XLA Ops:
  0.6 0.0 copy-start
  0.6 0.1 collective-permute-start
  0.7 3.2 %collective-permute-start.3 = (bf16[256,1024]{1,0:T(8,128)(2,1)}, bf16[256,1024]{1,0:T(8,128)(2,1)}, u32[]{:S(2)}, u32[]{:S(2)}) collective-permute-start(bf16[256,1024]{1,0:T(8,128)(2,1)} %bitcast.41), channel_id=1, source_target_pairs={{0,192},{64,0},{128,64},{192,128},{1,193},{65,1},{129,65},{193,129... | collective-permute-start | bytes 1572872 | tf_op jit(solution)/shard_map/ppermute | solution.py:24
  4.0 0.7 iota_compare_fusion.1
  4.7 0.7 subtract_add_fusion
  5.4 0.1 fusion.53
  5.5 0.1 copy.9
  5.6 0.1 broadcast_bitcast_fusion
  5.7 0.1 broadcast_in_dim.31
  5.7 1.2 %copy.10.live_ref = f32[256,768]{1,0:T(8,128)} copy(f32[256,768]{0,1:T(8,128)S(1)} %bitcast.34) | data formatting | bytes 1572864 | tf_op jit(solution)/shard_map/jit(_where)/select_n | solution.py:160
  6.9 6.5 %collective-permute-done = bf16[256,1024]{1,0:T(8,128)(2,1)S(1)} collective-permute-done((bf16[256,1024]{1,0:T(8,128)(2,1)}, bf16[256,1024]{1,0:T(8,128)(2,1)S(1)}, u32[]{:S(2)}, u32[]{:S(2)}) %collective-permute-start) | collective-permute-done | bytes 524320 | tf_op jit(solution)/shard_map/ppermute | solution.py:24
  13.3 9.8 %collective-permute-start.2 = (bf16[256,1024]{1,0:T(8,128)(2,1)S(1)}, bf16[256,1024]{1,0:T(8,128)(2,1)S(1)}, u32[]{:S(2)}, u32[]{:S(2)}) collective-permute-start(bf16[256,1024]{1,0:T(8,128)(2,1)S(1)} %collective-permute-done), channel_id=1, source_target_pairs={{1,0},{2,1},{3,2},{4,3},{5,4},{6,5},{7,6},{8,7},{9,8},{10,9},{11,1... | collective-permute-start | bytes 1572872 | tf_op jit(solution)/shard_map/ppermute | solution.py:34
  23.1 1.9 %collective-permute-start.1 = (bf16[256,1024]{1,0:T(8,128)(2,1)S(1)}, bf16[256,1024]{1,0:T(8,128)(2,1)S(1)}, u32[]{:S(2)}, u32[]{:S(2)}) collective-permute-start(bf16[256,1024]{1,0:T(8,128)(2,1)S(1)} %collective-permute-done), channel_id=1, source_target_pairs={{0,1},{1,2},{2,3},{3,4},{4,5},{5,6},{6,7},{7,8},{8,9},{9,10},{10,1... | collective-permute-start | bytes 1572872 | tf_op jit(solution)/shard_map/ppermute | solution.py:29
  25.0 0.2 fusion.46
  25.2 0.0 slice-start
  25.3 2.7 %fusion.35.do_ref = bf16[256,1024]{1,0:T(8,128)(2,1)} fusion(bf16[256,1024]{1,0:T(8,128)(2,1)} %collective-permute-done.3, bf16[1,1024,1024]{2,1,0:T(8,128)(2,1)S(1)} %copy-done), kind=kOutput, calls=%fused_computation.31 | convolution fusion | flops 537133056 | bytes 3145728 | tf_op jit(solution)/shard_map/rd,wd->rw/dot_general | solution.py:145
  28.0 6.0 %convolution_convert_fusion.q_ref.ko_ref.vo_ref = bf16[256,3072]{1,0:T(8,128)(2,1)} fusion(bf16[256,1024]{1,0:T(8,128)(2,1)S(1)} %collective-permute-done, f32[256]{0:T(256)S(1)} %add_rsqrt_fusion.1, bf16[1,1024,3072]{2,1,0:T(8,128)(2,1)} %param.8), kind=kOutput, calls=%fused_computation | convolution fusion | flops 1612185600 | bytes 8389632 | tf_op jit(solution)/shard_map/dot_general | solution.py:142
  34.0 6.7 %collective-permute-done.1 = bf16[256,1024]{1,0:T(8,128)(2,1)S(1)} collective-permute-done((bf16[256,1024]{1,0:T(8,128)(2,1)S(1)}, bf16[256,1024]{1,0:T(8,128)(2,1)S(1)}, u32[]{:S(2)}, u32[]{:S(2)}) %collective-permute-start.1) | collective-permute-done | bytes 524320 | tf_op jit(solution)/shard_map/ppermute | solution.py:29
  40.6 0.3 fusion.7
  41.0 3.8 %fusion.4.kh_ref.vh_ref = bf16[512,2048]{1,0:T(8,128)(2,1)} fusion(bf16[1024,3072]{1,0:T(8,128)(2,1)S(1)} %bitcast.39, f32[512]{0:T(512)S(1)} %add_rsqrt_fusion, bf16[256,1024]{1,0:T(8,128)(2,1)S(1)} %collective-permute-done.2, bf16[256,1024]{1,0:T(8,128)(2,1)S(1)} %collective-permute-done.1), kind=kOutput, calls=%fused_computation.5 | convolution fusion | flops 2151677952 | bytes 7342080 | tf_op jit(solution)/shard_map/dot_general | solution.py:150
  44.7 12.7 %shard_map.77 = (bf16[256,1024]{1,0:T(8,128)(2,1)}, bf16[256,1024]{1,0:T(8,128)(2,1)}, bf16[256,1024]{1,0:T(8,128)(2,1)}, bf16[256,1024]{1,0:T(8,128)(2,1)}, bf1...) custom-call(bf16[256,3072]{1,0:T(8,128)(2,1)} %convolution_convert_fusion.q_ref.ko_ref.vo_ref, ...), custom_call_target="tpu_custom_call" | custom-call | flops 2013265920 | bytes 9175040 | tf_op jit(solution)/shard_map/pallas_call | solution.py:103
  57.4 5.2 %fusion.22 = bf16[512,1024]{1,0:T(8,128)(2,1)S(1)} fusion(bf16[1024,3072]{1,0:T(8,128)(2,1)} %bitcast.36, bf16[512,1024]{1,0:T(8,128)(2,1)} %get-tuple-element.13, bf16[512,1024]{1,0:T(8,128)(2,1)} %get-tuple-element.12), kind=kOutput, calls=%fused_computation.26 | convolution fusion | flops 2152202240 | bytes 7340032 | tf_op jit(solution)/shard_map/rc,dc->rd/dot_general | solution.py:170
  62.6 0.1 fusion.59
  62.7 2.1 %collective-permute-start.4 = (bf16[256,1024]{1,0:T(8,128)(2,1)S(1)}, bf16[256,1024]{1,0:T(8,128)(2,1)S(1)}, u32[]{:S(2)}, u32[]{:S(2)}) collective-permute-start(bf16[256,1024]{1,0:T(8,128)(2,1)S(1)} %get-tuple-element.14), channel_id=1, source_target_pairs={{0,1},{1,2},{2,3},{3,4},{4,5},{5,6},{6,7},{7,8},{8,9},{9,10},{10,1... | collective-permute-start | bytes 1572872 | tf_op jit(solution)/shard_map/ppermute | solution.py:29
  64.8 7.1 %collective-permute-start.5 = (bf16[256,1024]{1,0:T(8,128)(2,1)S(1)}, bf16[256,1024]{1,0:T(8,128)(2,1)S(1)}, u32[]{:S(2)}, u32[]{:S(2)}) collective-permute-start(bf16[256,1024]{1,0:T(8,128)(2,1)S(1)} %get-tuple-element.15), channel_id=1, source_target_pairs={{1,0},{2,1},{3,2},{4,3},{5,4},{6,5},{7,6},{8,7},{9,8},{10,9},{11,1... | collective-permute-start | bytes 1572872 | tf_op jit(solution)/shard_map/ppermute | solution.py:34
  71.9 0.0 copy-start.1
  71.9 4.7 %fusion.16 = f32[256,1024]{1,0:T(8,128)S(1)} fusion(bf16[256,1024]{1,0:T(8,128)(2,1)S(1)} %copy-done.4, bf16[256,1024]{1,0:T(8,128)(2,1)S(1)} %copy-done.3, bf16[256,1024]{1,0:T(8,128)(2,1)S(1)} %copy-done.2, bf16[1,1024,3072]{2,1,0:T(8,128)(2,1)} %param.8), kind=kOutput, calls=%fused_computation.17 | convolution fusion | flops 1615331328 | bytes 8912896 | tf_op jit(solution)/shard_map/rc,dc->rd/dot_general | solution.py:177
  76.6 1.5 %fusion.38 = bf16[1,256,1024]{2,1,0:T(8,128)(2,1)} fusion(bf16[256,1024]{1,0:T(8,128)(2,1)S(1)} %copy-done.1, bf16[1,1024,1024]{2,1,0:T(8,128)(2,1)S(1)} %copy-done, bf16[256,1024]{1,0:T(8,128)(2,1)S(1)} %collective-permute-done), kind=kOutput, calls=%fused_computation.32 | convolution fusion | flops 537657344 | bytes 3670016 | tf_op jit(solution)/shard_map/dot_general | solution.py:165
  78.1 1.4 %collective-permute-done.4 = bf16[256,1024]{1,0:T(8,128)(2,1)S(1)} collective-permute-done((bf16[256,1024]{1,0:T(8,128)(2,1)S(1)}, bf16[256,1024]{1,0:T(8,128)(2,1)S(1)}, u32[]{:S(2)}, u32[]{:S(2)}) %collective-permute-start.4) | collective-permute-done | bytes 524320 | tf_op jit(solution)/shard_map/ppermute | solution.py:29
  79.5 1.2 %collective-permute-done.5 = bf16[256,1024]{1,0:T(8,128)(2,1)S(1)} collective-permute-done((bf16[256,1024]{1,0:T(8,128)(2,1)S(1)}, bf16[256,1024]{1,0:T(8,128)(2,1)S(1)}, u32[]{:S(2)}, u32[]{:S(2)}) %collective-permute-start.5) | collective-permute-done | bytes 524320 | tf_op jit(solution)/shard_map/ppermute | solution.py:34
  80.7 0.4 fusion.41
  81.1 2.3 %fusion.49 = bf16[1,256,1024]{2,1,0:T(8,128)(2,1)} fusion(bf16[256,1024]{1,0:T(8,128)(2,1)S(1)} %collective-permute-done, bf16[256,1024]{1,0:T(8,128)(2,1)} %collective-permute-done.3, f32[256]{0:T(256)S(1)} %broadcast_multiply_fusion, f32[256]{0:T(256)S(1)} %add_rsqrt_fusion.1, bf16[256,1024]{1,0:T(8,128)(2,1)S(1)} %collective-permute-done.5, ...), kind=kLoop, calls=%fused_computation.42 | loop fusion | flops 3145728 | bytes 3672064 | tf_op jit(solution)/shard_map/broadcast_in_dim | solution.py:185
  (19 shorter events, 0.1 us)
Async XLA Ops:
  0.6 24.6 %copy-start = (bf16[1,1024,1024]{2,1,0:T(8,128)(2,1)S(1)}, bf16[1,1024,1024]{2,1,0:T(8,128)(2,1)}, u32[]{:S(2)}) copy-start(bf16[1,1024,1024]{2,1,0:T(8,128)(2,1)} %param.9) | copy-start | bytes 6291460
  0.6 12.7 %collective-permute-start = (bf16[256,1024]{1,0:T(8,128)(2,1)}, bf16[256,1024]{1,0:T(8,128)(2,1)S(1)}, u32[]{:S(2)}, u32[]{:S(2)}) collective-permute-start(bf16[256,1024]{1,0:T(8,128)(2,1)} %bitcast.40), channel_id=1, source_target_pairs={{0,64},{64,128},{128,192},{192,0},{1,65},{65,129},{129,193},{193,1... | collective-permute-start | bytes 1572872 | tf_op jit(solution)/shard_map/ppermute | solution.py:24
  0.7 24.5 %collective-permute-start.3 = (bf16[256,1024]{1,0:T(8,128)(2,1)}, bf16[256,1024]{1,0:T(8,128)(2,1)}, u32[]{:S(2)}, u32[]{:S(2)}) collective-permute-start(bf16[256,1024]{1,0:T(8,128)(2,1)} %bitcast.41), channel_id=1, source_target_pairs={{0,192},{64,0},{128,64},{192,128},{1,193},{65,1},{129,65},{193,129... | collective-permute-start | bytes 1572872 | tf_op jit(solution)/shard_map/ppermute | solution.py:24
  13.3 20.6 %collective-permute-start.2 = (bf16[256,1024]{1,0:T(8,128)(2,1)S(1)}, bf16[256,1024]{1,0:T(8,128)(2,1)S(1)}, u32[]{:S(2)}, u32[]{:S(2)}) collective-permute-start(bf16[256,1024]{1,0:T(8,128)(2,1)S(1)} %collective-permute-done), channel_id=1, source_target_pairs={{1,0},{2,1},{3,2},{4,3},{5,4},{6,5},{7,6},{8,7},{9,8},{10,9},{11,1... | collective-permute-start | bytes 1572872 | tf_op jit(solution)/shard_map/ppermute | solution.py:34
  23.1 17.5 %collective-permute-start.1 = (bf16[256,1024]{1,0:T(8,128)(2,1)S(1)}, bf16[256,1024]{1,0:T(8,128)(2,1)S(1)}, u32[]{:S(2)}, u32[]{:S(2)}) collective-permute-start(bf16[256,1024]{1,0:T(8,128)(2,1)S(1)} %collective-permute-done), channel_id=1, source_target_pairs={{0,1},{1,2},{2,3},{3,4},{4,5},{5,6},{6,7},{7,8},{8,9},{9,10},{10,1... | collective-permute-start | bytes 1572872 | tf_op jit(solution)/shard_map/ppermute | solution.py:29
  25.2 15.7 %slice-start = ((s8[6291456]{0:T(1024)(128)(4,1)}), s8[4194304]{0:T(1024)(128)(4,1)S(1)}, s32[]{:S(2)}) async-start(s8[6291456]{0:T(1024)(128)(4,1)} %bitcast.37), calls=%async_computation | async-start | bytes 8388608
  28.0 13.0 %slice-start.1 = ((s8[6291456]{0:T(1024)(128)(4,1)}), s8[2097152]{0:T(1024)(128)(4,1)S(1)}, s32[]{:S(2)}) async-start(s8[6291456]{0:T(1024)(128)(4,1)} %bitcast.37), calls=%async_computation.1 | async-start | bytes 4194304
  62.6 9.3 %copy-start.2 = (bf16[256,1024]{1,0:T(8,128)(2,1)S(1)}, bf16[256,1024]{1,0:T(8,128)(2,1)}, u32[]{:S(2)}) copy-start(bf16[256,1024]{1,0:T(8,128)(2,1)} %get-tuple-element.9) | copy-start | bytes 1572868
  62.6 9.3 %copy-start.3 = (bf16[256,1024]{1,0:T(8,128)(2,1)S(1)}, bf16[256,1024]{1,0:T(8,128)(2,1)}, u32[]{:S(2)}) copy-start(bf16[256,1024]{1,0:T(8,128)(2,1)} %get-tuple-element.10) | copy-start | bytes 1572868
  62.6 9.3 %copy-start.4 = (bf16[256,1024]{1,0:T(8,128)(2,1)S(1)}, bf16[256,1024]{1,0:T(8,128)(2,1)}, u32[]{:S(2)}) copy-start(bf16[256,1024]{1,0:T(8,128)(2,1)} %get-tuple-element.11) | copy-start | bytes 1572868
  62.7 16.8 %collective-permute-start.4 = (bf16[256,1024]{1,0:T(8,128)(2,1)S(1)}, bf16[256,1024]{1,0:T(8,128)(2,1)S(1)}, u32[]{:S(2)}, u32[]{:S(2)}) collective-permute-start(bf16[256,1024]{1,0:T(8,128)(2,1)S(1)} %get-tuple-element.14), channel_id=1, source_target_pairs={{0,1},{1,2},{2,3},{3,4},{4,5},{5,6},{6,7},{7,8},{8,9},{9,10},{10,1... | collective-permute-start | bytes 1572872 | tf_op jit(solution)/shard_map/ppermute | solution.py:29
  64.8 15.9 %collective-permute-start.5 = (bf16[256,1024]{1,0:T(8,128)(2,1)S(1)}, bf16[256,1024]{1,0:T(8,128)(2,1)S(1)}, u32[]{:S(2)}, u32[]{:S(2)}) collective-permute-start(bf16[256,1024]{1,0:T(8,128)(2,1)S(1)} %get-tuple-element.15), channel_id=1, source_target_pairs={{1,0},{2,1},{3,2},{4,3},{5,4},{6,5},{7,6},{8,7},{9,8},{10,9},{11,1... | collective-permute-start | bytes 1572872 | tf_op jit(solution)/shard_map/ppermute | solution.py:34
  71.9 4.7 %copy-start.1 = (bf16[256,1024]{1,0:T(8,128)(2,1)S(1)}, bf16[256,1024]{1,0:T(8,128)(2,1)}, u32[]{:S(2)}) copy-start(bf16[256,1024]{1,0:T(8,128)(2,1)} %get-tuple-element.8) | copy-start | bytes 1572868

commit v10 on v9

--- a/solution.py
+++ b/solution.py
@@ -40,7 +40,7 @@
     return values, factor, values * factor
 
 
-GROUP = 2
+GROUP = 4
 
 
 def attention_kernel(

time: 83.9 us -> 84.1 us (level)
  transfers between devices with their start and end apart: 6 -> 6, of which waited for: 4 -> 4; matrix products, arithmetic and copies ran while one was open for 22% -> 21% of each run, Pallas kernels for 0% -> 0%
where the time goes in v10:
time: 84.1 us; the launch traced here: 83.6 us
  starting transfers between devices  24.2 us (29%)
  matrix products  23.8 us (28%)
  waiting for transfers between devices  15.7 us (19%)
  Pallas kernels  12.9 us (15%)
  other arithmetic  4.65 us (6%)
  local copies, waits for them, and re-layouts  1.51 us (2%)
    ppermute x2, starting transfers between devices, from_right(): return lax.ppermute(value, axis, [(i + 1, i) for i in range(count - 1)])  16.9 us
    pallas_call x1, Pallas kernels, attention(): pl.pallas_call(attention_kernel, grid=(heads // group,), in_specs=[own(0)...  12.9 us
    ppermute x2, waiting for transfers between devices, from_left(): return lax.ppermute(value, axis, [(i, i + 1) for i in range(count - 1)])  8.07 us
    ppermute x2, waiting for transfers between devices, shifted(): return lax.ppermute(value, axis, pairs)  6.45 us
    dot_general x1, matrix products, per_device(): jnp.dot(normed.astype(jnp.bfloat16), weights_in, preferred_element_type=j...  5.97 us
    dot_general x1, matrix products, per_device(): jnp.einsum('rc,dc->rd', halo_grads, weights_kv, preferred_element_type=jn...  5.2 us
    dot_general x1, matrix products, per_device(): jnp.einsum('rc,dc->rd', own_grads, weights_in, preferred_element_type=jnp...  4.66 us
    ppermute x2, starting transfers between devices, from_left(): return lax.ppermute(value, axis, [(i, i + 1) for i in range(count - 1)])  3.97 us
  transfers between devices with their start and end apart: 6, of which 4 were waited for; matrix products, arithmetic and copies ran while one was open for 21% of the time, Pallas kernels for 0%

profile of v10, /device:TPU:24, one launch (start us, length us, event | category | flops | bytes accessed | tf_op | source)
XLA Modules:
  0.0 83.6 jit_solution(8668195886334916737)
XLA Ops:
  0.6 0.0 copy-start
  0.6 0.1 collective-permute-start
  0.7 3.2 %collective-permute-start.3 = (bf16[256,1024]{1,0:T(8,128)(2,1)}, bf16[256,1024]{1,0:T(8,128)(2,1)}, u32[]{:S(2)}, u32[]{:S(2)}) collective-permute-start(bf16[256,1024]{1,0:T(8,128)(2,1)} %bitcast.41), channel_id=1, source_target_pairs={{0,192},{64,0},{128,64},{192,128},{1,193},{65,1},{129,65},{193,129... | collective-permute-start | bytes 1572872 | tf_op jit(solution)/shard_map/ppermute | solution.py:24
  4.0 0.7 iota_compare_fusion.1
  4.7 0.7 subtract_add_fusion
  5.4 0.1 fusion.53
  5.5 0.1 copy.9
  5.6 0.1 broadcast_bitcast_fusion
  5.7 0.1 broadcast_in_dim.31
  5.7 1.2 %copy.10.live_ref = f32[256,768]{1,0:T(8,128)} copy(f32[256,768]{0,1:T(8,128)S(1)} %bitcast.34) | data formatting | bytes 1572864 | tf_op jit(solution)/shard_map/jit(_where)/select_n | solution.py:160
  6.9 6.5 %collective-permute-done = bf16[256,1024]{1,0:T(8,128)(2,1)S(1)} collective-permute-done((bf16[256,1024]{1,0:T(8,128)(2,1)}, bf16[256,1024]{1,0:T(8,128)(2,1)S(1)}, u32[]{:S(2)}, u32[]{:S(2)}) %collective-permute-start) | collective-permute-done | bytes 524320 | tf_op jit(solution)/shard_map/ppermute | solution.py:24
  13.3 9.8 %collective-permute-start.2 = (bf16[256,1024]{1,0:T(8,128)(2,1)S(1)}, bf16[256,1024]{1,0:T(8,128)(2,1)S(1)}, u32[]{:S(2)}, u32[]{:S(2)}) collective-permute-start(bf16[256,1024]{1,0:T(8,128)(2,1)S(1)} %collective-permute-done), channel_id=1, source_target_pairs={{1,0},{2,1},{3,2},{4,3},{5,4},{6,5},{7,6},{8,7},{9,8},{10,9},{11,1... | collective-permute-start | bytes 1572872 | tf_op jit(solution)/shard_map/ppermute | solution.py:34
  23.1 1.9 %collective-permute-start.1 = (bf16[256,1024]{1,0:T(8,128)(2,1)S(1)}, bf16[256,1024]{1,0:T(8,128)(2,1)S(1)}, u32[]{:S(2)}, u32[]{:S(2)}) collective-permute-start(bf16[256,1024]{1,0:T(8,128)(2,1)S(1)} %collective-permute-done), channel_id=1, source_target_pairs={{0,1},{1,2},{2,3},{3,4},{4,5},{5,6},{6,7},{7,8},{8,9},{9,10},{10,1... | collective-permute-start | bytes 1572872 | tf_op jit(solution)/shard_map/ppermute | solution.py:29
  25.0 0.2 fusion.46
  25.2 0.0 slice-start
  25.3 2.7 %fusion.35.do_ref = bf16[256,1024]{1,0:T(8,128)(2,1)} fusion(bf16[256,1024]{1,0:T(8,128)(2,1)} %collective-permute-done.3, bf16[1,1024,1024]{2,1,0:T(8,128)(2,1)S(1)} %copy-done), kind=kOutput, calls=%fused_computation.31 | convolution fusion | flops 537133056 | bytes 3145728 | tf_op jit(solution)/shard_map/rd,wd->rw/dot_general | solution.py:145
  28.0 6.0 %convolution_convert_fusion.q_ref.ko_ref.vo_ref = bf16[256,3072]{1,0:T(8,128)(2,1)} fusion(bf16[256,1024]{1,0:T(8,128)(2,1)S(1)} %collective-permute-done, f32[256]{0:T(256)S(1)} %add_rsqrt_fusion.1, bf16[1,1024,3072]{2,1,0:T(8,128)(2,1)} %param.8), kind=kOutput, calls=%fused_computation | convolution fusion | flops 1612185600 | bytes 8389632 | tf_op jit(solution)/shard_map/dot_general | solution.py:142
  34.0 6.7 %collective-permute-done.1 = bf16[256,1024]{1,0:T(8,128)(2,1)S(1)} collective-permute-done((bf16[256,1024]{1,0:T(8,128)(2,1)S(1)}, bf16[256,1024]{1,0:T(8,128)(2,1)S(1)}, u32[]{:S(2)}, u32[]{:S(2)}) %collective-permute-start.1) | collective-permute-done | bytes 524320 | tf_op jit(solution)/shard_map/ppermute | solution.py:29
  40.6 0.3 fusion.7
  41.0 3.8 %fusion.4.kh_ref.vh_ref = bf16[512,2048]{1,0:T(8,128)(2,1)} fusion(bf16[1024,3072]{1,0:T(8,128)(2,1)S(1)} %bitcast.39, f32[512]{0:T(512)S(1)} %add_rsqrt_fusion, bf16[256,1024]{1,0:T(8,128)(2,1)S(1)} %collective-permute-done.2, bf16[256,1024]{1,0:T(8,128)(2,1)S(1)} %collective-permute-done.1), kind=kOutput, calls=%fused_computation.5 | convolution fusion | flops 2151677952 | bytes 7342080 | tf_op jit(solution)/shard_map/dot_general | solution.py:150
  44.7 12.9 %shard_map.77 = (bf16[256,1024]{1,0:T(8,128)(2,1)}, bf16[256,1024]{1,0:T(8,128)(2,1)}, bf16[256,1024]{1,0:T(8,128)(2,1)}, bf16[256,1024]{1,0:T(8,128)(2,1)}, bf1...) custom-call(bf16[256,3072]{1,0:T(8,128)(2,1)} %convolution_convert_fusion.q_ref.ko_ref.vo_ref, ...), custom_call_target="tpu_custom_call" | custom-call | flops 2013265920 | bytes 9175040 | tf_op jit(solution)/shard_map/pallas_call | solution.py:103
  57.6 5.2 %fusion.22 = bf16[512,1024]{1,0:T(8,128)(2,1)S(1)} fusion(bf16[1024,3072]{1,0:T(8,128)(2,1)} %bitcast.36, bf16[512,1024]{1,0:T(8,128)(2,1)} %get-tuple-element.13, bf16[512,1024]{1,0:T(8,128)(2,1)} %get-tuple-element.12), kind=kOutput, calls=%fused_computation.26 | convolution fusion | flops 2152202240 | bytes 7340032 | tf_op jit(solution)/shard_map/rc,dc->rd/dot_general | solution.py:170
  62.9 0.1 fusion.59
  62.9 2.1 %collective-permute-start.4 = (bf16[256,1024]{1,0:T(8,128)(2,1)S(1)}, bf16[256,1024]{1,0:T(8,128)(2,1)S(1)}, u32[]{:S(2)}, u32[]{:S(2)}) collective-permute-start(bf16[256,1024]{1,0:T(8,128)(2,1)S(1)} %get-tuple-element.14), channel_id=1, source_target_pairs={{0,1},{1,2},{2,3},{3,4},{4,5},{5,6},{6,7},{7,8},{8,9},{9,10},{10,1... | collective-permute-start | bytes 1572872 | tf_op jit(solution)/shard_map/ppermute | solution.py:29
  65.0 7.1 %collective-permute-start.5 = (bf16[256,1024]{1,0:T(8,128)(2,1)S(1)}, bf16[256,1024]{1,0:T(8,128)(2,1)S(1)}, u32[]{:S(2)}, u32[]{:S(2)}) collective-permute-start(bf16[256,1024]{1,0:T(8,128)(2,1)S(1)} %get-tuple-element.15), channel_id=1, source_target_pairs={{1,0},{2,1},{3,2},{4,3},{5,4},{6,5},{7,6},{8,7},{9,8},{10,9},{11,1... | collective-permute-start | bytes 1572872 | tf_op jit(solution)/shard_map/ppermute | solution.py:34
  72.1 0.0 copy-start.1
  72.2 4.7 %fusion.16 = f32[256,1024]{1,0:T(8,128)S(1)} fusion(bf16[256,1024]{1,0:T(8,128)(2,1)S(1)} %copy-done.4, bf16[256,1024]{1,0:T(8,128)(2,1)S(1)} %copy-done.3, bf16[256,1024]{1,0:T(8,128)(2,1)S(1)} %copy-done.2, bf16[1,1024,3072]{2,1,0:T(8,128)(2,1)} %param.8), kind=kOutput, calls=%fused_computation.17 | convolution fusion | flops 1615331328 | bytes 8912896 | tf_op jit(solution)/shard_map/rc,dc->rd/dot_general | solution.py:177
  76.8 1.5 %fusion.38 = bf16[1,256,1024]{2,1,0:T(8,128)(2,1)} fusion(bf16[256,1024]{1,0:T(8,128)(2,1)S(1)} %copy-done.1, bf16[1,1024,1024]{2,1,0:T(8,128)(2,1)S(1)} %copy-done, bf16[256,1024]{1,0:T(8,128)(2,1)S(1)} %collective-permute-done), kind=kOutput, calls=%fused_computation.32 | convolution fusion | flops 537657344 | bytes 3670016 | tf_op jit(solution)/shard_map/dot_general | solution.py:165
  78.3 1.4 %collective-permute-done.4 = bf16[256,1024]{1,0:T(8,128)(2,1)S(1)} collective-permute-done((bf16[256,1024]{1,0:T(8,128)(2,1)S(1)}, bf16[256,1024]{1,0:T(8,128)(2,1)S(1)}, u32[]{:S(2)}, u32[]{:S(2)}) %collective-permute-start.4) | collective-permute-done | bytes 524320 | tf_op jit(solution)/shard_map/ppermute | solution.py:29
  79.7 1.2 %collective-permute-done.5 = bf16[256,1024]{1,0:T(8,128)(2,1)S(1)} collective-permute-done((bf16[256,1024]{1,0:T(8,128)(2,1)S(1)}, bf16[256,1024]{1,0:T(8,128)(2,1)S(1)}, u32[]{:S(2)}, u32[]{:S(2)}) %collective-permute-start.5) | collective-permute-done | bytes 524320 | tf_op jit(solution)/shard_map/ppermute | solution.py:34
  80.9 0.4 fusion.41
  81.3 2.3 %fusion.49 = bf16[1,256,1024]{2,1,0:T(8,128)(2,1)} fusion(bf16[256,1024]{1,0:T(8,128)(2,1)S(1)} %collective-permute-done, bf16[256,1024]{1,0:T(8,128)(2,1)} %collective-permute-done.3, f32[256]{0:T(256)S(1)} %broadcast_multiply_fusion, f32[256]{0:T(256)S(1)} %add_rsqrt_fusion.1, bf16[256,1024]{1,0:T(8,128)(2,1)S(1)} %collective-permute-done.5, ...), kind=kLoop, calls=%fused_computation.42 | loop fusion | flops 3145728 | bytes 3672064 | tf_op jit(solution)/shard_map/broadcast_in_dim | solution.py:185
  (19 shorter events, 0.1 us)
Async XLA Ops:
  0.6 24.6 %copy-start = (bf16[1,1024,1024]{2,1,0:T(8,128)(2,1)S(1)}, bf16[1,1024,1024]{2,1,0:T(8,128)(2,1)}, u32[]{:S(2)}) copy-start(bf16[1,1024,1024]{2,1,0:T(8,128)(2,1)} %param.9) | copy-start | bytes 6291460
  0.6 12.7 %collective-permute-start = (bf16[256,1024]{1,0:T(8,128)(2,1)}, bf16[256,1024]{1,0:T(8,128)(2,1)S(1)}, u32[]{:S(2)}, u32[]{:S(2)}) collective-permute-start(bf16[256,1024]{1,0:T(8,128)(2,1)} %bitcast.40), channel_id=1, source_target_pairs={{0,64},{64,128},{128,192},{192,0},{1,65},{65,129},{129,193},{193,1... | collective-permute-start | bytes 1572872 | tf_op jit(solution)/shard_map/ppermute | solution.py:24
  0.7 24.5 %collective-permute-start.3 = (bf16[256,1024]{1,0:T(8,128)(2,1)}, bf16[256,1024]{1,0:T(8,128)(2,1)}, u32[]{:S(2)}, u32[]{:S(2)}) collective-permute-start(bf16[256,1024]{1,0:T(8,128)(2,1)} %bitcast.41), channel_id=1, source_target_pairs={{0,192},{64,0},{128,64},{192,128},{1,193},{65,1},{129,65},{193,129... | collective-permute-start | bytes 1572872 | tf_op jit(solution)/shard_map/ppermute | solution.py:24
  13.3 20.6 %collective-permute-start.2 = (bf16[256,1024]{1,0:T(8,128)(2,1)S(1)}, bf16[256,1024]{1,0:T(8,128)(2,1)S(1)}, u32[]{:S(2)}, u32[]{:S(2)}) collective-permute-start(bf16[256,1024]{1,0:T(8,128)(2,1)S(1)} %collective-permute-done), channel_id=1, source_target_pairs={{1,0},{2,1},{3,2},{4,3},{5,4},{6,5},{7,6},{8,7},{9,8},{10,9},{11,1... | collective-permute-start | bytes 1572872 | tf_op jit(solution)/shard_map/ppermute | solution.py:34
  23.1 17.5 %collective-permute-start.1 = (bf16[256,1024]{1,0:T(8,128)(2,1)S(1)}, bf16[256,1024]{1,0:T(8,128)(2,1)S(1)}, u32[]{:S(2)}, u32[]{:S(2)}) collective-permute-start(bf16[256,1024]{1,0:T(8,128)(2,1)S(1)} %collective-permute-done), channel_id=1, source_target_pairs={{0,1},{1,2},{2,3},{3,4},{4,5},{5,6},{6,7},{7,8},{8,9},{9,10},{10,1... | collective-permute-start | bytes 1572872 | tf_op jit(solution)/shard_map/ppermute | solution.py:29
  25.2 15.7 %slice-start = ((s8[6291456]{0:T(1024)(128)(4,1)}), s8[4194304]{0:T(1024)(128)(4,1)S(1)}, s32[]{:S(2)}) async-start(s8[6291456]{0:T(1024)(128)(4,1)} %bitcast.37), calls=%async_computation | async-start | bytes 8388608
  28.0 13.0 %slice-start.1 = ((s8[6291456]{0:T(1024)(128)(4,1)}), s8[2097152]{0:T(1024)(128)(4,1)S(1)}, s32[]{:S(2)}) async-start(s8[6291456]{0:T(1024)(128)(4,1)} %bitcast.37), calls=%async_computation.1 | async-start | bytes 4194304
  62.8 9.3 %copy-start.2 = (bf16[256,1024]{1,0:T(8,128)(2,1)S(1)}, bf16[256,1024]{1,0:T(8,128)(2,1)}, u32[]{:S(2)}) copy-start(bf16[256,1024]{1,0:T(8,128)(2,1)} %get-tuple-element.9) | copy-start | bytes 1572868
  62.8 9.3 %copy-start.3 = (bf16[256,1024]{1,0:T(8,128)(2,1)S(1)}, bf16[256,1024]{1,0:T(8,128)(2,1)}, u32[]{:S(2)}) copy-start(bf16[256,1024]{1,0:T(8,128)(2,1)} %get-tuple-element.10) | copy-start | bytes 1572868
  62.8 9.3 %copy-start.4 = (bf16[256,1024]{1,0:T(8,128)(2,1)S(1)}, bf16[256,1024]{1,0:T(8,128)(2,1)}, u32[]{:S(2)}) copy-start(bf16[256,1024]{1,0:T(8,128)(2,1)} %get-tuple-element.11) | copy-start | bytes 1572868
  62.9 16.8 %collective-permute-start.4 = (bf16[256,1024]{1,0:T(8,128)(2,1)S(1)}, bf16[256,1024]{1,0:T(8,128)(2,1)S(1)}, u32[]{:S(2)}, u32[]{:S(2)}) collective-permute-start(bf16[256,1024]{1,0:T(8,128)(2,1)S(1)} %get-tuple-element.14), channel_id=1, source_target_pairs={{0,1},{1,2},{2,3},{3,4},{4,5},{5,6},{6,7},{7,8},{8,9},{9,10},{10,1... | collective-permute-start | bytes 1572872 | tf_op jit(solution)/shard_map/ppermute | solution.py:29
  65.0 15.9 %collective-permute-start.5 = (bf16[256,1024]{1,0:T(8,128)(2,1)S(1)}, bf16[256,1024]{1,0:T(8,128)(2,1)S(1)}, u32[]{:S(2)}, u32[]{:S(2)}) collective-permute-start(bf16[256,1024]{1,0:T(8,128)(2,1)S(1)} %get-tuple-element.15), channel_id=1, source_target_pairs={{1,0},{2,1},{3,2},{4,3},{5,4},{6,5},{7,6},{8,7},{9,8},{10,9},{11,1... | collective-permute-start | bytes 1572872 | tf_op jit(solution)/shard_map/ppermute | solution.py:34
  72.1 4.7 %copy-start.1 = (bf16[256,1024]{1,0:T(8,128)(2,1)S(1)}, bf16[256,1024]{1,0:T(8,128)(2,1)}, u32[]{:S(2)}) copy-start(bf16[256,1024]{1,0:T(8,128)(2,1)} %get-tuple-element.8) | copy-start | bytes 1572868

commit v11 on v9

--- a/solution.py
+++ b/solution.py
@@ -44,21 +44,21 @@
 
 
 def attention_kernel(
-    q_ref, ko_ref, vo_ref, kh_ref, vh_ref, do_ref, live_ref,
+    q_ref, ko_ref, vo_ref, kl_ref, vl_ref, kr_ref, vr_ref, do_ref, live_ref,
     out_ref, dq_ref, dk_ref, dv_ref, dkh_ref, dvh_ref,
 ):
     rows = q_ref.shape[0]
-    margin = kh_ref.shape[0] // 2
+    margin = kl_ref.shape[0]
     scaling = HEAD_DIM ** (-0.5)
     live = live_ref[...]
     for part in range(q_ref.shape[1] // HEAD_DIM):
         lanes = slice(part * HEAD_DIM, (part + 1) * HEAD_DIM)
         queries = q_ref[:, lanes]
         keys = jnp.concatenate(
-            [kh_ref[:margin, lanes], ko_ref[:, lanes], kh_ref[margin:, lanes]], axis=0
+            [kl_ref[:, lanes], ko_ref[:, lanes], kr_ref[:, lanes]], axis=0
         )
         values = jnp.concatenate(
-            [vh_ref[:margin, lanes], vo_ref[:, lanes], vh_ref[margin:, lanes]], axis=0
+            [vl_ref[:, lanes], vo_ref[:, lanes], vr_ref[:, lanes]], axis=0
         )
         grad_out = do_ref[:, lanes]
         scores = lax.dot_general(queries, keys, NT, preferred_element_type=jnp.float32) * scaling
@@ -87,17 +87,19 @@
         dvh_ref[margin:, lanes] = value_grad[margin + rows :].astype(dtype)
 
 
-def attention(projected, halo_kv, attended_grad, live):
+def attention(projected, left_kv, right_kv, attended_grad, live):
     rows, width = attended_grad.shape
     heads = width // HEAD_DIM
-    halo_rows = halo_kv.shape[0]
+    margin = left_kv.shape[0]
+    halo_rows = 2 * margin
     window = live.shape[1]
     group = GROUP if heads % GROUP == 0 else 1
     lanes = group * HEAD_DIM
     own = lambda offset: pl.BlockSpec((rows, lanes), lambda h: (0, offset // group + h))
     side = lambda offset: pl.BlockSpec((halo_rows, lanes), lambda h: (0, offset // group + h))
+    edge = lambda offset: pl.BlockSpec((margin, lanes), lambda h: (0, offset // group + h))
     flops = heads * 5 * 2 * rows * window * HEAD_DIM
-    moved = 2 * (2 * projected.size + 2 * halo_kv.size + 2 * attended_grad.size) + 4 * live.size
+    moved = 2 * (2 * projected.size + 4 * left_kv.size + 2 * attended_grad.size) + 4 * live.size
     own_shape = jax.ShapeDtypeStruct((rows, width), jnp.bfloat16)
     side_shape = jax.ShapeDtypeStruct((halo_rows, width), jnp.bfloat16)
     return pl.pallas_call(
@@ -107,8 +109,10 @@
             own(0),
             own(heads),
             own(2 * heads),
-            side(0),
-            side(heads),
+            edge(0),
+            edge(heads),
+            edge(0),
+            edge(heads),
             own(0),
             pl.BlockSpec((rows, window), lambda h: (0, 0)),
         ],
@@ -118,7 +122,9 @@
         cost_estimate=pl.CostEstimate(
             flops=flops, transcendentals=heads * rows * window, bytes_accessed=moved
         ),
-    )(projected, projected, projected, halo_kv, halo_kv, attended_grad, live)
+    )(
+        projected, projected, projected, left_kv, left_kv, right_kv, right_kv, attended_grad, live
+    )
 
 
 def per_device(activations, cotangent, input_weights, output_weights, key_blocks, block_counts):
@@ -135,9 +141,8 @@
     span_blocks = nblock + 2 * REACH
     first_block = lax.axis_index("seq") * nblock
 
-    halo_rows = jnp.concatenate(
-        [from_left(arrived[rows - margin :], "seq"), from_right(arrived[:margin], "seq")], axis=0
-    )
+    left_rows = from_left(arrived[rows - margin :], "seq")
+    right_rows = from_right(arrived[:margin], "seq")
     values, factor, normed = normalize(arrived)
     projected = jnp.dot(
         normed.astype(jnp.bfloat16), weights_in, preferred_element_type=jnp.float32
@@ -145,11 +150,17 @@
     attended_grad = jnp.einsum(
         "rd,wd->rw", upstream, weights_out, preferred_element_type=jnp.float32
     ).astype(jnp.bfloat16)
-    _, _, halo_normed = normalize(halo_rows)
     weights_kv = weights_in[:, width:]
-    halo_kv = jnp.dot(
-        halo_normed.astype(jnp.bfloat16), weights_kv, preferred_element_type=jnp.float32
-    ).astype(jnp.bfloat16)
+
+    def side_kv(side_rows):
+        _, _, side_normed = normalize(side_rows)
+        return jnp.dot(
+            side_normed.astype(jnp.bfloat16), weights_kv, preferred_element_type=jnp.float32
+        ).astype(jnp.bfloat16)
+
+    right_kv = side_kv(right_rows)
+    right_kv, left_rows = lax.optimization_barrier((right_kv, left_rows))
+    left_kv = side_kv(left_rows)
 
     window_index = key_blocks - first_block + REACH
     live_slots = jnp.arange(slot_count)[None, :] < block_counts[:, None]
@@ -160,7 +171,7 @@
     live = jnp.where(jnp.repeat(jnp.repeat(live_blocks, BLOCK, axis=0), BLOCK, axis=1), 0.0, -1e30)
 
     attended, query_grad, key_grad, value_grad, halo_key_grad, halo_value_grad = attention(
-        projected, halo_kv, attended_grad, live
+        projected, left_kv, right_kv, attended_grad, live
     )
     result = (values + jnp.dot(attended, weights_out, preferred_element_type=jnp.float32)).astype(
         jnp.bfloat16

time: 83.9 us -> 81.8 us (0.975); the launches traced: 83.4 us -> 80.3 us
  waiting for transfers between devices: 15.7 us -> 11 us
  matrix products: 23.8 us -> 25 us
    ppermute x2, waiting for transfers between devices: 8.07 us -> 1.94 us  [from_left(): return lax.ppermute(value, axis, [(i, i + 1) for i in range(count - 1)])]
    ppermute x2, starting transfers between devices: 3.97 us -> 5.73 us  [from_left(): return lax.ppermute(value, axis, [(i, i + 1) for i in range(count - 1)])]
    ppermute x2, waiting for transfers between devices: 1.18 us -> 2.63 us  [from_right(): return lax.ppermute(value, axis, [(i + 1, i) for i in range(count - 1)])]
    ppermute x2, starting transfers between devices: 16.9 us -> 15.4 us  [from_right(): return lax.ppermute(value, axis, [(i + 1, i) for i in range(count - 1)])]
    dot_general x1 -> x2, matrix products: 3.76 us -> 4.73 us  [side_kv(): jnp.dot(side_normed.astype(jnp.bfloat16), weights_kv, preferred_element_t...]
  transfers between devices with their start and end apart: 6 -> 6, of which waited for: 4 -> 4; matrix products, arithmetic and copies ran while one was open for 22% -> 26% of each run, Pallas kernels for 0% -> 0%
where the time goes in v11:
time: 81.8 us; the launch traced here: 80.3 us
  matrix products  25 us (31%)
  starting transfers between devices  24.5 us (30%)
  Pallas kernels  12.7 us (16%)
  waiting for transfers between devices  11 us (13%)
  other arithmetic  4.75 us (6%)
  local copies, waits for them, and re-layouts  1.52 us (2%)
  between operations  0.84 us (1%)
    ppermute x2, starting transfers between devices, from_right(): return lax.ppermute(value, axis, [(i + 1, i) for i in range(count - 1)])  15.4 us
    pallas_call x1, Pallas kernels, attention(): pl.pallas_call(attention_kernel, grid=(heads // group,), in_specs=[own(0)...  12.7 us
    ppermute x2, waiting for transfers between devices, shifted(): return lax.ppermute(value, axis, pairs)  6.44 us
    dot_general x1, matrix products, per_device(): jnp.dot(normed.astype(jnp.bfloat16), weights_in, preferred_element_type=j...  5.99 us
    ppermute x2, starting transfers between devices, from_left(): return lax.ppermute(value, axis, [(i, i + 1) for i in range(count - 1)])  5.73 us
    dot_general x1, matrix products, per_device(): jnp.einsum('rc,dc->rd', halo_grads, weights_kv, preferred_element_type=jn...  5.29 us
    dot_general x2, matrix products, side_kv(): jnp.dot(side_normed.astype(jnp.bfloat16), weights_kv, preferred_element_t...  4.73 us
    dot_general x1, matrix products, per_device(): jnp.einsum('rc,dc->rd', own_grads, weights_in, preferred_element_type=jnp...  4.66 us
  transfers between devices with their start and end apart: 6, of which 4 were waited for; matrix products, arithmetic and copies ran while one was open for 26% of the time, Pallas kernels for 0%

profile of v11, /device:TPU:24, one launch (start us, length us, event | category | flops | bytes accessed | tf_op | source)
XLA Modules:
  0.0 80.3 jit_solution(5542157047221863940)
XLA Ops:
  0.6 0.0 copy-start
  0.6 0.1 collective-permute-start
  0.7 3.2 %collective-permute-start.3 = (bf16[256,1024]{1,0:T(8,128)(2,1)}, bf16[256,1024]{1,0:T(8,128)(2,1)}, u32[]{:S(2)}, u32[]{:S(2)}) collective-permute-start(bf16[256,1024]{1,0:T(8,128)(2,1)} %bitcast.42), channel_id=1, source_target_pairs={{0,192},{64,0},{128,64},{192,128},{1,193},{65,1},{129,65},{193,129... | collective-permute-start | bytes 1572872 | tf_op jit(solution)/shard_map/ppermute | solution.py:24
  4.0 0.7 iota_compare_fusion.1
  4.7 0.7 subtract_add_fusion
  5.4 0.1 fusion.62
  5.5 0.1 copy.9
  5.6 0.1 broadcast_bitcast_fusion
  5.7 0.1 broadcast_in_dim.32
  5.7 1.2 %copy.10.live_ref = f32[256,768]{1,0:T(8,128)} copy(f32[256,768]{0,1:T(8,128)S(1)} %bitcast.34) | data formatting | bytes 1572864 | tf_op jit(solution)/shard_map/jit(_where)/select_n | solution.py:171
  6.9 6.4 %collective-permute-done = bf16[256,1024]{1,0:T(8,128)(2,1)S(1)} collective-permute-done((bf16[256,1024]{1,0:T(8,128)(2,1)}, bf16[256,1024]{1,0:T(8,128)(2,1)S(1)}, u32[]{:S(2)}, u32[]{:S(2)}) %collective-permute-start) | collective-permute-done | bytes 524320 | tf_op jit(solution)/shard_map/ppermute | solution.py:24
  13.3 3.8 %collective-permute-start.2 = (bf16[256,1024]{1,0:T(8,128)(2,1)S(1)}, bf16[256,1024]{1,0:T(8,128)(2,1)S(1)}, u32[]{:S(2)}, u32[]{:S(2)}) collective-permute-start(bf16[256,1024]{1,0:T(8,128)(2,1)S(1)} %collective-permute-done), channel_id=1, source_target_pairs={{0,1},{1,2},{2,3},{3,4},{4,5},{5,6},{6,7},{7,8},{8,9},{9,10},{10,1... | collective-permute-start | bytes 1572872 | tf_op jit(solution)/shard_map/ppermute | solution.py:29
  17.2 7.9 %collective-permute-start.1 = (bf16[256,1024]{1,0:T(8,128)(2,1)S(1)}, bf16[256,1024]{1,0:T(8,128)(2,1)S(1)}, u32[]{:S(2)}, u32[]{:S(2)}) collective-permute-start(bf16[256,1024]{1,0:T(8,128)(2,1)S(1)} %collective-permute-done), channel_id=1, source_target_pairs={{1,0},{2,1},{3,2},{4,3},{5,4},{6,5},{7,6},{8,7},{9,8},{10,9},{11,1... | collective-permute-start | bytes 1572872 | tf_op jit(solution)/shard_map/ppermute | solution.py:34
  25.0 0.2 fusion.53
  25.3 2.7 %fusion.38.do_ref = bf16[256,1024]{1,0:T(8,128)(2,1)} fusion(bf16[256,1024]{1,0:T(8,128)(2,1)} %collective-permute-done.3, bf16[1,1024,1024]{2,1,0:T(8,128)(2,1)S(1)} %copy-done), kind=kOutput, calls=%fused_computation.34 | convolution fusion | flops 537133056 | bytes 3145728 | tf_op jit(solution)/shard_map/rd,wd->rw/dot_general | solution.py:150
  28.0 6.0 %convolution_convert_fusion.q_ref.ko_ref.vo_ref = bf16[256,3072]{1,0:T(8,128)(2,1)} fusion(bf16[256,1024]{1,0:T(8,128)(2,1)S(1)} %collective-permute-done, f32[256]{0:T(256)S(1)} %add_rsqrt_fusion.2, bf16[1,1024,3072]{2,1,0:T(8,128)(2,1)} %param.8), kind=kOutput, calls=%fused_computation | convolution fusion | flops 1612185600 | bytes 8389632 | tf_op jit(solution)/shard_map/dot_general | solution.py:147
  34.0 1.4 %collective-permute-done.1 = bf16[256,1024]{1,0:T(8,128)(2,1)S(1)} collective-permute-done((bf16[256,1024]{1,0:T(8,128)(2,1)S(1)}, bf16[256,1024]{1,0:T(8,128)(2,1)S(1)}, u32[]{:S(2)}, u32[]{:S(2)}) %collective-permute-start.1) | collective-permute-done | bytes 524320 | tf_op jit(solution)/shard_map/ppermute | solution.py:34
  35.4 0.2 fusion.44
  35.7 2.4 %fusion.6.kr_ref.vr_ref = bf16[256,2048]{1,0:T(8,128)(2,1)} fusion(bf16[1024,3072]{1,0:T(8,128)(2,1)S(1)} %bitcast.39, bf16[256,1024]{1,0:T(8,128)(2,1)S(1)} %collective-permute-done.1, f32[256]{0:T(256)S(1)} %add_rsqrt_fusion.1), kind=kOutput, calls=%fused_computation.7 | convolution fusion | flops 1075052544 | bytes 5768192 | tf_op jit(solution)/shard_map/dot_general | solution.py:157
  38.0 0.2 fusion.46
  38.2 2.4 %fusion.9.kl_ref.vl_ref = bf16[256,2048]{1,0:T(8,128)(2,1)} fusion(bf16[1024,3072]{1,0:T(8,128)(2,1)S(1)} %bitcast.40, bf16[256,1024]{1,0:T(8,128)(2,1)S(1)} %collective-permute-done.2, f32[256]{0:T(256)S(1)} %add_rsqrt_fusion), kind=kOutput, calls=%fused_computation.8 | convolution fusion | flops 1075052544 | bytes 5768192 | tf_op jit(solution)/shard_map/dot_general | solution.py:157
  40.6 12.7 %shard_map.77 = (bf16[256,1024]{1,0:T(8,128)(2,1)}, bf16[256,1024]{1,0:T(8,128)(2,1)}, bf16[256,1024]{1,0:T(8,128)(2,1)}, bf16[256,1024]{1,0:T(8,128)(2,1)}, bf1...) custom-call(bf16[256,3072]{1,0:T(8,128)(2,1)} %convolution_convert_fusion.q_ref.ko_ref.vo_ref, ...), custom_call_target="tpu_custom_call" | custom-call | flops 2013265920 | bytes 9175040 | tf_op jit(solution)/shard_map/pallas_call | solution.py:105
  53.4 5.3 %fusion.25 = bf16[512,1024]{1,0:T(8,128)(2,1)S(1)} fusion(bf16[1024,3072]{1,0:T(8,128)(2,1)} %bitcast.36, bf16[512,1024]{1,0:T(8,128)(2,1)} %get-tuple-element.17, bf16[512,1024]{1,0:T(8,128)(2,1)} %get-tuple-element.16), kind=kOutput, calls=%fused_computation.25 | convolution fusion | flops 2152202240 | bytes 7340032 | tf_op jit(solution)/shard_map/rc,dc->rd/dot_general | solution.py:181
  58.7 0.1 fusion.67
  58.7 1.9 %collective-permute-start.4 = (bf16[256,1024]{1,0:T(8,128)(2,1)S(1)}, bf16[256,1024]{1,0:T(8,128)(2,1)S(1)}, u32[]{:S(2)}, u32[]{:S(2)}) collective-permute-start(bf16[256,1024]{1,0:T(8,128)(2,1)S(1)} %get-tuple-element.18), channel_id=1, source_target_pairs={{0,1},{1,2},{2,3},{3,4},{4,5},{5,6},{6,7},{7,8},{8,9},{9,10},{10,1... | collective-permute-start | bytes 1572872 | tf_op jit(solution)/shard_map/ppermute | solution.py:29
  60.7 7.6 %collective-permute-start.5 = (bf16[256,1024]{1,0:T(8,128)(2,1)S(1)}, bf16[256,1024]{1,0:T(8,128)(2,1)S(1)}, u32[]{:S(2)}, u32[]{:S(2)}) collective-permute-start(bf16[256,1024]{1,0:T(8,128)(2,1)S(1)} %get-tuple-element.19), channel_id=1, source_target_pairs={{1,0},{2,1},{3,2},{4,3},{5,4},{6,5},{7,6},{8,7},{9,8},{10,9},{11,1... | collective-permute-start | bytes 1572872 | tf_op jit(solution)/shard_map/ppermute | solution.py:34
  68.3 4.7 %fusion.19 = f32[256,1024]{1,0:T(8,128)S(1)} fusion(bf16[256,1024]{1,0:T(8,128)(2,1)S(1)} %copy-done.4, bf16[256,1024]{1,0:T(8,128)(2,1)S(1)} %copy-done.3, bf16[256,1024]{1,0:T(8,128)(2,1)S(1)} %copy-done.2, bf16[1,1024,3072]{2,1,0:T(8,128)(2,1)} %param.8), kind=kOutput, calls=%fused_computation.16 | convolution fusion | flops 1615331328 | bytes 8912896 | tf_op jit(solution)/shard_map/rc,dc->rd/dot_general | solution.py:188
  73.0 1.5 %fusion.41 = bf16[1,256,1024]{2,1,0:T(8,128)(2,1)} fusion(bf16[256,1024]{1,0:T(8,128)(2,1)S(1)} %copy-done.1, bf16[1,1024,1024]{2,1,0:T(8,128)(2,1)S(1)} %copy-done, bf16[256,1024]{1,0:T(8,128)(2,1)S(1)} %collective-permute-done), kind=kOutput, calls=%fused_computation.35 | convolution fusion | flops 537657344 | bytes 3670016 | tf_op jit(solution)/shard_map/dot_general | solution.py:176
  74.5 1.9 %collective-permute-done.4 = bf16[256,1024]{1,0:T(8,128)(2,1)S(1)} collective-permute-done((bf16[256,1024]{1,0:T(8,128)(2,1)S(1)}, bf16[256,1024]{1,0:T(8,128)(2,1)S(1)}, u32[]{:S(2)}, u32[]{:S(2)}) %collective-permute-start.4) | collective-permute-done | bytes 524320 | tf_op jit(solution)/shard_map/ppermute | solution.py:29
  76.4 1.2 %collective-permute-done.5 = bf16[256,1024]{1,0:T(8,128)(2,1)S(1)} collective-permute-done((bf16[256,1024]{1,0:T(8,128)(2,1)S(1)}, bf16[256,1024]{1,0:T(8,128)(2,1)S(1)}, u32[]{:S(2)}, u32[]{:S(2)}) %collective-permute-start.5) | collective-permute-done | bytes 524320 | tf_op jit(solution)/shard_map/ppermute | solution.py:34
  77.6 0.4 fusion.48
  78.0 2.3 %fusion.54 = bf16[1,256,1024]{2,1,0:T(8,128)(2,1)} fusion(bf16[256,1024]{1,0:T(8,128)(2,1)S(1)} %collective-permute-done, bf16[256,1024]{1,0:T(8,128)(2,1)} %collective-permute-done.3, f32[256]{0:T(256)S(1)} %broadcast_multiply_fusion, f32[256]{0:T(256)S(1)} %add_rsqrt_fusion.2, bf16[256,1024]{1,0:T(8,128)(2,1)S(1)} %collective-permute-done.5, ...), kind=kLoop, calls=%fused_computation.47 | loop fusion | flops 3145728 | bytes 3672064 | tf_op jit(solution)/shard_map/broadcast_in_dim | solution.py:196
  (22 shorter events, 0.1 us)
Async XLA Ops:
  0.6 24.6 %copy-start = (bf16[1,1024,1024]{2,1,0:T(8,128)(2,1)S(1)}, bf16[1,1024,1024]{2,1,0:T(8,128)(2,1)}, u32[]{:S(2)}) copy-start(bf16[1,1024,1024]{2,1,0:T(8,128)(2,1)} %param.9) | copy-start | bytes 6291460
  0.6 12.7 %collective-permute-start = (bf16[256,1024]{1,0:T(8,128)(2,1)}, bf16[256,1024]{1,0:T(8,128)(2,1)S(1)}, u32[]{:S(2)}, u32[]{:S(2)}) collective-permute-start(bf16[256,1024]{1,0:T(8,128)(2,1)} %bitcast.41), channel_id=1, source_target_pairs={{0,64},{64,128},{128,192},{192,0},{1,65},{65,129},{129,193},{193,1... | collective-permute-start | bytes 1572872 | tf_op jit(solution)/shard_map/ppermute | solution.py:24
  0.7 24.5 %collective-permute-start.3 = (bf16[256,1024]{1,0:T(8,128)(2,1)}, bf16[256,1024]{1,0:T(8,128)(2,1)}, u32[]{:S(2)}, u32[]{:S(2)}) collective-permute-start(bf16[256,1024]{1,0:T(8,128)(2,1)} %bitcast.42), channel_id=1, source_target_pairs={{0,192},{64,0},{128,64},{192,128},{1,193},{65,1},{129,65},{193,129... | collective-permute-start | bytes 1572872 | tf_op jit(solution)/shard_map/ppermute | solution.py:24
  13.3 24.7 %collective-permute-start.2 = (bf16[256,1024]{1,0:T(8,128)(2,1)S(1)}, bf16[256,1024]{1,0:T(8,128)(2,1)S(1)}, u32[]{:S(2)}, u32[]{:S(2)}) collective-permute-start(bf16[256,1024]{1,0:T(8,128)(2,1)S(1)} %collective-permute-done), channel_id=1, source_target_pairs={{0,1},{1,2},{2,3},{3,4},{4,5},{5,6},{6,7},{7,8},{8,9},{9,10},{10,1... | collective-permute-start | bytes 1572872 | tf_op jit(solution)/shard_map/ppermute | solution.py:29
  17.2 18.3 %collective-permute-start.1 = (bf16[256,1024]{1,0:T(8,128)(2,1)S(1)}, bf16[256,1024]{1,0:T(8,128)(2,1)S(1)}, u32[]{:S(2)}, u32[]{:S(2)}) collective-permute-start(bf16[256,1024]{1,0:T(8,128)(2,1)S(1)} %collective-permute-done), channel_id=1, source_target_pairs={{1,0},{2,1},{3,2},{4,3},{5,4},{6,5},{7,6},{8,7},{9,8},{10,9},{11,1... | collective-permute-start | bytes 1572872 | tf_op jit(solution)/shard_map/ppermute | solution.py:34
  25.2 10.4 %slice-start = ((s8[6291456]{0:T(1024)(128)(4,1)}), s8[4194304]{0:T(1024)(128)(4,1)S(1)}, s32[]{:S(2)}) async-start(s8[6291456]{0:T(1024)(128)(4,1)} %bitcast.37), calls=%async_computation | async-start | bytes 8388608
  28.0 7.6 %slice-start.1 = ((s8[6291456]{0:T(1024)(128)(4,1)}), s8[2097152]{0:T(1024)(128)(4,1)S(1)}, s32[]{:S(2)}) async-start(s8[6291456]{0:T(1024)(128)(4,1)} %bitcast.37), calls=%async_computation.1 | async-start | bytes 4194304
  53.3 14.9 %copy-start.2 = (bf16[256,1024]{1,0:T(8,128)(2,1)S(1)}, bf16[256,1024]{1,0:T(8,128)(2,1)}, u32[]{:S(2)}) copy-start(bf16[256,1024]{1,0:T(8,128)(2,1)} %get-tuple-element.13) | copy-start | bytes 1572868
  53.3 14.9 %copy-start.3 = (bf16[256,1024]{1,0:T(8,128)(2,1)S(1)}, bf16[256,1024]{1,0:T(8,128)(2,1)}, u32[]{:S(2)}) copy-start(bf16[256,1024]{1,0:T(8,128)(2,1)} %get-tuple-element.14) | copy-start | bytes 1572868
  53.4 14.9 %copy-start.4 = (bf16[256,1024]{1,0:T(8,128)(2,1)S(1)}, bf16[256,1024]{1,0:T(8,128)(2,1)}, u32[]{:S(2)}) copy-start(bf16[256,1024]{1,0:T(8,128)(2,1)} %get-tuple-element.15) | copy-start | bytes 1572868
  58.7 17.7 %collective-permute-start.4 = (bf16[256,1024]{1,0:T(8,128)(2,1)S(1)}, bf16[256,1024]{1,0:T(8,128)(2,1)S(1)}, u32[]{:S(2)}, u32[]{:S(2)}) collective-permute-start(bf16[256,1024]{1,0:T(8,128)(2,1)S(1)} %get-tuple-element.18), channel_id=1, source_target_pairs={{0,1},{1,2},{2,3},{3,4},{4,5},{5,6},{6,7},{7,8},{8,9},{9,10},{10,1... | collective-permute-start | bytes 1572872 | tf_op jit(solution)/shard_map/ppermute | solution.py:29
  60.7 17.0 %collective-permute-start.5 = (bf16[256,1024]{1,0:T(8,128)(2,1)S(1)}, bf16[256,1024]{1,0:T(8,128)(2,1)S(1)}, u32[]{:S(2)}, u32[]{:S(2)}) collective-permute-start(bf16[256,1024]{1,0:T(8,128)(2,1)S(1)} %get-tuple-element.19), channel_id=1, source_target_pairs={{1,0},{2,1},{3,2},{4,3},{5,4},{6,5},{7,6},{8,7},{9,8},{10,9},{11,1... | collective-permute-start | bytes 1572872 | tf_op jit(solution)/shard_map/ppermute | solution.py:34
  68.3 4.7 %copy-start.1 = (bf16[256,1024]{1,0:T(8,128)(2,1)S(1)}, bf16[256,1024]{1,0:T(8,128)(2,1)}, u32[]{:S(2)}) copy-start(bf16[256,1024]{1,0:T(8,128)(2,1)} %get-tuple-element.12) | copy-start | bytes 1572868

commit v12 on v11

--- a/solution.py
+++ b/solution.py
@@ -158,9 +158,9 @@
             side_normed.astype(jnp.bfloat16), weights_kv, preferred_element_type=jnp.float32
         ).astype(jnp.bfloat16)
 
+    left_kv = side_kv(left_rows)
+    left_kv, right_rows = lax.optimization_barrier((left_kv, right_rows))
     right_kv = side_kv(right_rows)
-    right_kv, left_rows = lax.optimization_barrier((right_kv, left_rows))
-    left_kv = side_kv(left_rows)
 
     window_index = key_blocks - first_block + REACH
     live_slots = jnp.arange(slot_count)[None, :] < block_counts[:, None]

time: 81.8 us -> 85 us (1.039); the launches traced: 80.3 us -> 84.5 us
  waiting for transfers between devices: 11 us -> 15.6 us
    ppermute x2, waiting for transfers between devices: 1.94 us -> 8.03 us  [from_left(): return lax.ppermute(value, axis, [(i, i + 1) for i in range(count - 1)])]
    ppermute x2, starting transfers between devices: 5.73 us -> 3.84 us  [from_left(): return lax.ppermute(value, axis, [(i, i + 1) for i in range(count - 1)])]
    ppermute x2, waiting for transfers between devices: 2.63 us -> 1.18 us  [from_right(): return lax.ppermute(value, axis, [(i + 1, i) for i in range(count - 1)])]
    ppermute x2, starting transfers between devices: 15.4 us -> 16.9 us  [from_right(): return lax.ppermute(value, axis, [(i + 1, i) for i in range(count - 1)])]
  transfers between devices with their start and end apart: 6 -> 6, of which waited for: 4 -> 4; matrix products, arithmetic and copies ran while one was open for 26% -> 24% of each run, Pallas kernels for 0% -> 0%
where the time goes in v12:
time: 85 us; the launch traced here: 84.5 us
  matrix products  25 us (29%)
  starting transfers between devices  24 us (28%)
  waiting for transfers between devices  15.6 us (18%)
  Pallas kernels  12.7 us (15%)
  other arithmetic  4.75 us (6%)
  local copies, waits for them, and re-layouts  1.52 us (2%)
    ppermute x2, starting transfers between devices, from_right(): return lax.ppermute(value, axis, [(i + 1, i) for i in range(count - 1)])  16.9 us
    pallas_call x1, Pallas kernels, attention(): pl.pallas_call(attention_kernel, grid=(heads // group,), in_specs=[own(0)...  12.7 us
    ppermute x2, waiting for transfers between devices, from_left(): return lax.ppermute(value, axis, [(i, i + 1) for i in range(count - 1)])  8.03 us
    ppermute x2, waiting for transfers between devices, shifted(): return lax.ppermute(value, axis, pairs)  6.44 us
    dot_general x1, matrix products, per_device(): jnp.dot(normed.astype(jnp.bfloat16), weights_in, preferred_element_type=j...  5.99 us
    dot_general x1, matrix products, per_device(): jnp.einsum('rc,dc->rd', halo_grads, weights_kv, preferred_element_type=jn...  5.3 us
    dot_general x2, matrix products, side_kv(): jnp.dot(side_normed.astype(jnp.bfloat16), weights_kv, preferred_element_t...  4.73 us
    dot_general x1, matrix products, per_device(): jnp.einsum('rc,dc->rd', own_grads, weights_in, preferred_element_type=jnp...  4.66 us
  transfers between devices with their start and end apart: 6, of which 4 were waited for; matrix products, arithmetic and copies ran while one was open for 24% of the time, Pallas kernels for 0%

profile of v12, /device:TPU:24, one launch (start us, length us, event | category | flops | bytes accessed | tf_op | source)
XLA Modules:
  0.0 84.5 jit_solution(16811099835791033540)
XLA Ops:
  0.6 0.0 copy-start
  0.6 0.1 collective-permute-start
  0.7 3.2 %collective-permute-start.3 = (bf16[256,1024]{1,0:T(8,128)(2,1)}, bf16[256,1024]{1,0:T(8,128)(2,1)}, u32[]{:S(2)}, u32[]{:S(2)}) collective-permute-start(bf16[256,1024]{1,0:T(8,128)(2,1)} %bitcast.42), channel_id=1, source_target_pairs={{0,192},{64,0},{128,64},{192,128},{1,193},{65,1},{129,65},{193,129... | collective-permute-start | bytes 1572872 | tf_op jit(solution)/shard_map/ppermute | solution.py:24
  4.0 0.7 iota_compare_fusion.1
  4.7 0.7 subtract_add_fusion
  5.4 0.1 fusion.62
  5.5 0.1 copy.9
  5.6 0.1 broadcast_bitcast_fusion
  5.7 0.1 broadcast_in_dim.32
  5.7 1.2 %copy.10.live_ref = f32[256,768]{1,0:T(8,128)} copy(f32[256,768]{0,1:T(8,128)S(1)} %bitcast.34) | data formatting | bytes 1572864 | tf_op jit(solution)/shard_map/jit(_where)/select_n | solution.py:171
  6.9 6.4 %collective-permute-done = bf16[256,1024]{1,0:T(8,128)(2,1)S(1)} collective-permute-done((bf16[256,1024]{1,0:T(8,128)(2,1)}, bf16[256,1024]{1,0:T(8,128)(2,1)S(1)}, u32[]{:S(2)}, u32[]{:S(2)}) %collective-permute-start) | collective-permute-done | bytes 524320 | tf_op jit(solution)/shard_map/ppermute | solution.py:24
  13.3 9.8 %collective-permute-start.2 = (bf16[256,1024]{1,0:T(8,128)(2,1)S(1)}, bf16[256,1024]{1,0:T(8,128)(2,1)S(1)}, u32[]{:S(2)}, u32[]{:S(2)}) collective-permute-start(bf16[256,1024]{1,0:T(8,128)(2,1)S(1)} %collective-permute-done), channel_id=1, source_target_pairs={{1,0},{2,1},{3,2},{4,3},{5,4},{6,5},{7,6},{8,7},{9,8},{10,9},{11,1... | collective-permute-start | bytes 1572872 | tf_op jit(solution)/shard_map/ppermute | solution.py:34
  23.1 1.9 %collective-permute-start.1 = (bf16[256,1024]{1,0:T(8,128)(2,1)S(1)}, bf16[256,1024]{1,0:T(8,128)(2,1)S(1)}, u32[]{:S(2)}, u32[]{:S(2)}) collective-permute-start(bf16[256,1024]{1,0:T(8,128)(2,1)S(1)} %collective-permute-done), channel_id=1, source_target_pairs={{0,1},{1,2},{2,3},{3,4},{4,5},{5,6},{6,7},{7,8},{8,9},{9,10},{10,1... | collective-permute-start | bytes 1572872 | tf_op jit(solution)/shard_map/ppermute | solution.py:29
  25.0 0.2 fusion.53
  25.3 2.7 %fusion.38.do_ref = bf16[256,1024]{1,0:T(8,128)(2,1)} fusion(bf16[256,1024]{1,0:T(8,128)(2,1)} %collective-permute-done.3, bf16[1,1024,1024]{2,1,0:T(8,128)(2,1)S(1)} %copy-done), kind=kOutput, calls=%fused_computation.34 | convolution fusion | flops 537133056 | bytes 3145728 | tf_op jit(solution)/shard_map/rd,wd->rw/dot_general | solution.py:150
  28.0 6.0 %convolution_convert_fusion.q_ref.ko_ref.vo_ref = bf16[256,3072]{1,0:T(8,128)(2,1)} fusion(bf16[256,1024]{1,0:T(8,128)(2,1)S(1)} %collective-permute-done, f32[256]{0:T(256)S(1)} %add_rsqrt_fusion.2, bf16[1,1024,3072]{2,1,0:T(8,128)(2,1)} %param.8), kind=kOutput, calls=%fused_computation | convolution fusion | flops 1612185600 | bytes 8389632 | tf_op jit(solution)/shard_map/dot_general | solution.py:147
  34.0 6.6 %collective-permute-done.1 = bf16[256,1024]{1,0:T(8,128)(2,1)S(1)} collective-permute-done((bf16[256,1024]{1,0:T(8,128)(2,1)S(1)}, bf16[256,1024]{1,0:T(8,128)(2,1)S(1)}, u32[]{:S(2)}, u32[]{:S(2)}) %collective-permute-start.1) | collective-permute-done | bytes 524320 | tf_op jit(solution)/shard_map/ppermute | solution.py:29
  40.6 0.2 fusion.44
  40.9 2.3 %fusion.6.kl_ref.vl_ref = bf16[256,2048]{1,0:T(8,128)(2,1)} fusion(bf16[1024,3072]{1,0:T(8,128)(2,1)S(1)} %bitcast.39, bf16[256,1024]{1,0:T(8,128)(2,1)S(1)} %collective-permute-done.1, f32[256]{0:T(256)S(1)} %add_rsqrt_fusion.1), kind=kOutput, calls=%fused_computation.7 | convolution fusion | flops 1075052544 | bytes 5768192 | tf_op jit(solution)/shard_map/dot_general | solution.py:157
  43.2 0.2 fusion.46
  43.4 2.4 %fusion.9.kr_ref.vr_ref = bf16[256,2048]{1,0:T(8,128)(2,1)} fusion(bf16[1024,3072]{1,0:T(8,128)(2,1)S(1)} %bitcast.40, bf16[256,1024]{1,0:T(8,128)(2,1)S(1)} %collective-permute-done.2, f32[256]{0:T(256)S(1)} %add_rsqrt_fusion), kind=kOutput, calls=%fused_computation.8 | convolution fusion | flops 1075052544 | bytes 5768192 | tf_op jit(solution)/shard_map/dot_general | solution.py:157
  45.8 12.7 %shard_map.77 = (bf16[256,1024]{1,0:T(8,128)(2,1)}, bf16[256,1024]{1,0:T(8,128)(2,1)}, bf16[256,1024]{1,0:T(8,128)(2,1)}, bf16[256,1024]{1,0:T(8,128)(2,1)}, bf1...) custom-call(bf16[256,3072]{1,0:T(8,128)(2,1)} %convolution_convert_fusion.q_ref.ko_ref.vo_ref, ...), custom_call_target="tpu_custom_call" | custom-call | flops 2013265920 | bytes 9175040 | tf_op jit(solution)/shard_map/pallas_call | solution.py:105
  58.6 5.3 %fusion.25 = bf16[512,1024]{1,0:T(8,128)(2,1)S(1)} fusion(bf16[1024,3072]{1,0:T(8,128)(2,1)} %bitcast.36, bf16[512,1024]{1,0:T(8,128)(2,1)} %get-tuple-element.17, bf16[512,1024]{1,0:T(8,128)(2,1)} %get-tuple-element.16), kind=kOutput, calls=%fused_computation.25 | convolution fusion | flops 2152202240 | bytes 7340032 | tf_op jit(solution)/shard_map/rc,dc->rd/dot_general | solution.py:181
  63.9 0.1 fusion.67
  63.9 1.9 %collective-permute-start.4 = (bf16[256,1024]{1,0:T(8,128)(2,1)S(1)}, bf16[256,1024]{1,0:T(8,128)(2,1)S(1)}, u32[]{:S(2)}, u32[]{:S(2)}) collective-permute-start(bf16[256,1024]{1,0:T(8,128)(2,1)S(1)} %get-tuple-element.18), channel_id=1, source_target_pairs={{0,1},{1,2},{2,3},{3,4},{4,5},{5,6},{6,7},{7,8},{8,9},{9,10},{10,1... | collective-permute-start | bytes 1572872 | tf_op jit(solution)/shard_map/ppermute | solution.py:29
  65.9 7.1 %collective-permute-start.5 = (bf16[256,1024]{1,0:T(8,128)(2,1)S(1)}, bf16[256,1024]{1,0:T(8,128)(2,1)S(1)}, u32[]{:S(2)}, u32[]{:S(2)}) collective-permute-start(bf16[256,1024]{1,0:T(8,128)(2,1)S(1)} %get-tuple-element.19), channel_id=1, source_target_pairs={{1,0},{2,1},{3,2},{4,3},{5,4},{6,5},{7,6},{8,7},{9,8},{10,9},{11,1... | collective-permute-start | bytes 1572872 | tf_op jit(solution)/shard_map/ppermute | solution.py:34
  73.0 4.7 %fusion.19 = f32[256,1024]{1,0:T(8,128)S(1)} fusion(bf16[256,1024]{1,0:T(8,128)(2,1)S(1)} %copy-done.4, bf16[256,1024]{1,0:T(8,128)(2,1)S(1)} %copy-done.3, bf16[256,1024]{1,0:T(8,128)(2,1)S(1)} %copy-done.2, bf16[1,1024,3072]{2,1,0:T(8,128)(2,1)} %param.8), kind=kOutput, calls=%fused_computation.16 | convolution fusion | flops 1615331328 | bytes 8912896 | tf_op jit(solution)/shard_map/rc,dc->rd/dot_general | solution.py:188
  77.7 1.5 %fusion.41 = bf16[1,256,1024]{2,1,0:T(8,128)(2,1)} fusion(bf16[256,1024]{1,0:T(8,128)(2,1)S(1)} %copy-done.1, bf16[1,1024,1024]{2,1,0:T(8,128)(2,1)S(1)} %copy-done, bf16[256,1024]{1,0:T(8,128)(2,1)S(1)} %collective-permute-done), kind=kOutput, calls=%fused_computation.35 | convolution fusion | flops 537657344 | bytes 3670016 | tf_op jit(solution)/shard_map/dot_general | solution.py:176
  79.2 1.4 %collective-permute-done.4 = bf16[256,1024]{1,0:T(8,128)(2,1)S(1)} collective-permute-done((bf16[256,1024]{1,0:T(8,128)(2,1)S(1)}, bf16[256,1024]{1,0:T(8,128)(2,1)S(1)}, u32[]{:S(2)}, u32[]{:S(2)}) %collective-permute-start.4) | collective-permute-done | bytes 524320 | tf_op jit(solution)/shard_map/ppermute | solution.py:29
  80.6 1.2 %collective-permute-done.5 = bf16[256,1024]{1,0:T(8,128)(2,1)S(1)} collective-permute-done((bf16[256,1024]{1,0:T(8,128)(2,1)S(1)}, bf16[256,1024]{1,0:T(8,128)(2,1)S(1)}, u32[]{:S(2)}, u32[]{:S(2)}) %collective-permute-start.5) | collective-permute-done | bytes 524320 | tf_op jit(solution)/shard_map/ppermute | solution.py:34
  81.8 0.4 fusion.48
  82.2 2.3 %fusion.54 = bf16[1,256,1024]{2,1,0:T(8,128)(2,1)} fusion(bf16[256,1024]{1,0:T(8,128)(2,1)S(1)} %collective-permute-done, bf16[256,1024]{1,0:T(8,128)(2,1)} %collective-permute-done.3, f32[256]{0:T(256)S(1)} %broadcast_multiply_fusion, f32[256]{0:T(256)S(1)} %add_rsqrt_fusion.2, bf16[256,1024]{1,0:T(8,128)(2,1)S(1)} %collective-permute-done.5, ...), kind=kLoop, calls=%fused_computation.47 | loop fusion | flops 3145728 | bytes 3672064 | tf_op jit(solution)/shard_map/broadcast_in_dim | solution.py:196
  (22 shorter events, 0.1 us)
Async XLA Ops:
  0.6 24.6 %copy-start = (bf16[1,1024,1024]{2,1,0:T(8,128)(2,1)S(1)}, bf16[1,1024,1024]{2,1,0:T(8,128)(2,1)}, u32[]{:S(2)}) copy-start(bf16[1,1024,1024]{2,1,0:T(8,128)(2,1)} %param.9) | copy-start | bytes 6291460
  0.6 12.7 %collective-permute-start = (bf16[256,1024]{1,0:T(8,128)(2,1)}, bf16[256,1024]{1,0:T(8,128)(2,1)S(1)}, u32[]{:S(2)}, u32[]{:S(2)}) collective-permute-start(bf16[256,1024]{1,0:T(8,128)(2,1)} %bitcast.41), channel_id=1, source_target_pairs={{0,64},{64,128},{128,192},{192,0},{1,65},{65,129},{129,193},{193,1... | collective-permute-start | bytes 1572872 | tf_op jit(solution)/shard_map/ppermute | solution.py:24
  0.7 24.5 %collective-permute-start.3 = (bf16[256,1024]{1,0:T(8,128)(2,1)}, bf16[256,1024]{1,0:T(8,128)(2,1)}, u32[]{:S(2)}, u32[]{:S(2)}) collective-permute-start(bf16[256,1024]{1,0:T(8,128)(2,1)} %bitcast.42), channel_id=1, source_target_pairs={{0,192},{64,0},{128,64},{192,128},{1,193},{65,1},{129,65},{193,129... | collective-permute-start | bytes 1572872 | tf_op jit(solution)/shard_map/ppermute | solution.py:24
  13.3 29.9 %collective-permute-start.2 = (bf16[256,1024]{1,0:T(8,128)(2,1)S(1)}, bf16[256,1024]{1,0:T(8,128)(2,1)S(1)}, u32[]{:S(2)}, u32[]{:S(2)}) collective-permute-start(bf16[256,1024]{1,0:T(8,128)(2,1)S(1)} %collective-permute-done), channel_id=1, source_target_pairs={{1,0},{2,1},{3,2},{4,3},{5,4},{6,5},{7,6},{8,7},{9,8},{10,9},{11,1... | collective-permute-start | bytes 1572872 | tf_op jit(solution)/shard_map/ppermute | solution.py:34
  23.1 17.5 %collective-permute-start.1 = (bf16[256,1024]{1,0:T(8,128)(2,1)S(1)}, bf16[256,1024]{1,0:T(8,128)(2,1)S(1)}, u32[]{:S(2)}, u32[]{:S(2)}) collective-permute-start(bf16[256,1024]{1,0:T(8,128)(2,1)S(1)} %collective-permute-done), channel_id=1, source_target_pairs={{0,1},{1,2},{2,3},{3,4},{4,5},{5,6},{6,7},{7,8},{8,9},{9,10},{10,1... | collective-permute-start | bytes 1572872 | tf_op jit(solution)/shard_map/ppermute | solution.py:29
  25.2 15.6 %slice-start = ((s8[6291456]{0:T(1024)(128)(4,1)}), s8[4194304]{0:T(1024)(128)(4,1)S(1)}, s32[]{:S(2)}) async-start(s8[6291456]{0:T(1024)(128)(4,1)} %bitcast.37), calls=%async_computation | async-start | bytes 8388608
  28.0 12.8 %slice-start.1 = ((s8[6291456]{0:T(1024)(128)(4,1)}), s8[2097152]{0:T(1024)(128)(4,1)S(1)}, s32[]{:S(2)}) async-start(s8[6291456]{0:T(1024)(128)(4,1)} %bitcast.37), calls=%async_computation.1 | async-start | bytes 4194304
  58.5 14.5 %copy-start.2 = (bf16[256,1024]{1,0:T(8,128)(2,1)S(1)}, bf16[256,1024]{1,0:T(8,128)(2,1)}, u32[]{:S(2)}) copy-start(bf16[256,1024]{1,0:T(8,128)(2,1)} %get-tuple-element.13) | copy-start | bytes 1572868
  58.5 14.5 %copy-start.3 = (bf16[256,1024]{1,0:T(8,128)(2,1)S(1)}, bf16[256,1024]{1,0:T(8,128)(2,1)}, u32[]{:S(2)}) copy-start(bf16[256,1024]{1,0:T(8,128)(2,1)} %get-tuple-element.14) | copy-start | bytes 1572868
  58.5 14.5 %copy-start.4 = (bf16[256,1024]{1,0:T(8,128)(2,1)S(1)}, bf16[256,1024]{1,0:T(8,128)(2,1)}, u32[]{:S(2)}) copy-start(bf16[256,1024]{1,0:T(8,128)(2,1)} %get-tuple-element.15) | copy-start | bytes 1572868
  63.9 16.7 %collective-permute-start.4 = (bf16[256,1024]{1,0:T(8,128)(2,1)S(1)}, bf16[256,1024]{1,0:T(8,128)(2,1)S(1)}, u32[]{:S(2)}, u32[]{:S(2)}) collective-permute-start(bf16[256,1024]{1,0:T(8,128)(2,1)S(1)} %get-tuple-element.18), channel_id=1, source_target_pairs={{0,1},{1,2},{2,3},{3,4},{4,5},{5,6},{6,7},{7,8},{8,9},{9,10},{10,1... | collective-permute-start | bytes 1572872 | tf_op jit(solution)/shard_map/ppermute | solution.py:29
  65.9 15.9 %collective-permute-start.5 = (bf16[256,1024]{1,0:T(8,128)(2,1)S(1)}, bf16[256,1024]{1,0:T(8,128)(2,1)S(1)}, u32[]{:S(2)}, u32[]{:S(2)}) collective-permute-start(bf16[256,1024]{1,0:T(8,128)(2,1)S(1)} %get-tuple-element.19), channel_id=1, source_target_pairs={{1,0},{2,1},{3,2},{4,3},{5,4},{6,5},{7,6},{8,7},{9,8},{10,9},{11,1... | collective-permute-start | bytes 1572872 | tf_op jit(solution)/shard_map/ppermute | solution.py:34
  73.0 4.7 %copy-start.1 = (bf16[256,1024]{1,0:T(8,128)(2,1)S(1)}, bf16[256,1024]{1,0:T(8,128)(2,1)}, u32[]{:S(2)}) copy-start(bf16[256,1024]{1,0:T(8,128)(2,1)} %get-tuple-element.12) | copy-start | bytes 1572868
